TPU v7x, 1024 devices: a whole 8x8x8 slice. The times are simulated.
1024 devices in a mesh: seq: 64 (over z, x), fsdp: 16 (over y, core).
Axes of the slice: x: 8, y: 8, z: 8, core: 2. Of those that a mesh axis runs over, the one named last changes fastest.
Arguments:
- query_act: bfloat16 [16384, 8192], P('seq', 'fsdp'), may hold values from -6 to 6
- key_act: bfloat16 [16384, 8192], P('seq', 'fsdp'), may hold values from -6 to 6
- value_act: bfloat16 [16384, 8192], P('seq', 'fsdp'), may hold values from -6 to 6
- gate_act: bfloat16 [16384, 8192], P('seq', 'fsdp'), may hold values from -6 to 6
- rate_index: int32 [64], P('fsdp'), may hold values from 0 to 63, each once
- norm_gain: float32 [8192], P('fsdp'), may hold values from 0.1 to 1.9
- out_weight: bfloat16 [8192, 6144], P('fsdp'), may hold values from -0.0625 to 0.0625
Outputs:
- layer_out: bfloat16 [16384, 6144], P(('seq', 'fsdp'))
Inputs may be any that keep to these rules, and one draw needn't show every extreme that they name: `rate_index`: each head index of 0 to 63 appears once.
All inputs are finite; a program needn't handle non-finite values.
Results may differ from a plain program's by a relative error of at most 0.018.
Values may be sent and summed in bfloat16 or wider, within the bound.
No kernel may reach another device: no remote copies, remote signals or barrier semaphores. Data moves between devices by JAX's collectives and lax.ppermute only.
A program may use at most 64 MiB of HBM per device.

v0:
```python
import math

import jax
import jax.numpy as jnp
from jax import lax
from jax.sharding import PartitionSpec as P

HEADS = 64
HEAD_DIM = 128


layer_factor = 1.0 - 78.0 / 79.0 + 1e-05


def prefix(value, axis, combine, identity):
    peers, mine = (lax.axis_size(axis), lax.axis_index(axis))
    everything = jax.tree.map(lambda part: lax.all_gather(part, axis), value)
    start = jax.tree.map(
        lambda part, zero: jnp.broadcast_to(jnp.asarray(zero, part.dtype), part.shape),
        value,
        identity,
    )

    def hop(k, before):
        reached = k < mine
        new = combine(before, jax.tree.map(lambda part: part[k], everything))
        return jax.tree.map(lambda a, b: jnp.where(reached, a, b), new, before)

    return lax.fori_loop(0, peers, hop, start)


def decay_slopes(rate_index):
    exponent = -8.0 * (rate_index.astype(jnp.float32) + 1.0) / HEADS
    return jnp.exp(exponent * math.log(2.0)) * layer_factor


def span_terms(query_rows, key_rows, value_rows, slopes):
    tok_count = query_rows.shape[0]
    position = jnp.arange(tok_count).astype(jnp.float32)
    offset = position[:, None] - position[None, :]
    causal = jnp.where(
        offset[None] >= 0.0, jnp.exp(-slopes[:, None, None] * jnp.maximum(offset, 0.0)[None]), 0.0
    )
    scores = jnp.einsum("thd,shd->hts", query_rows, key_rows, preferred_element_type=jnp.float32)
    weighted = (scores * causal).astype(jnp.bfloat16)
    intra_part = jnp.einsum(
        "hts,she->the", weighted, value_rows, preferred_element_type=jnp.float32
    )
    to_end = jnp.exp(-slopes[None, :] * (tok_count - 1.0 - position)[:, None])
    key_scaled = (key_rows.astype(jnp.float32) * to_end[:, :, None]).astype(jnp.bfloat16)
    local_state = jnp.einsum(
        "thd,the->hde", key_scaled, value_rows, preferred_element_type=jnp.float32
    )
    from_start = jnp.exp(-slopes[None, :] * (position + 1.0)[:, None])
    return (intra_part, local_state, from_start)


def normalize_gate(intra_part, from_start, query_rows, incoming, gate_rows, gain_table):
    inter_part = jnp.einsum(
        "thd,hde->the", query_rows.astype(jnp.float32), incoming, precision=lax.Precision.HIGHEST
    )
    attended = intra_part + from_start[:, :, None] * inter_part
    local_squares = jnp.sum(attended * attended, axis=(1, 2))
    square_sum = lax.psum(local_squares, "fsdp")
    inv_rms = lax.rsqrt(square_sum / (HEADS * HEAD_DIM) + 1e-06)
    normed = (
        attended
        * inv_rms[:, None, None]
        * gain_table[None]
        * jax.nn.sigmoid(gate_rows.astype(jnp.float32))
    )
    return normed.reshape(query_rows.shape[0], -1).astype(jnp.bfloat16)


def combine_pairs(earlier_pair, later_pair):
    return (
        earlier_pair[0] * later_pair[0],
        later_pair[0][:, None, None] * earlier_pair[1] + later_pair[1],
    )


def per_device(query_act, key_act, value_act, gate_act, rate_index, norm_gain, out_weight):
    tok_count = query_act.shape[0]
    heads_here = rate_index.shape[0]
    slopes = decay_slopes(rate_index)
    carry_decay = jnp.exp(-slopes * tok_count)
    span_shape = (tok_count, heads_here, HEAD_DIM)
    query_rows = query_act.reshape(span_shape)
    key_rows = key_act.reshape(span_shape)
    value_rows = value_act.reshape(span_shape)
    gate_rows = gate_act.reshape(span_shape)
    gain_table = norm_gain.reshape(heads_here, HEAD_DIM)
    intra_part, local_state, from_start = span_terms(query_rows, key_rows, value_rows, slopes)
    scanned = prefix(
        (carry_decay, local_state),
        "seq",
        combine_pairs,
        (jnp.ones_like(carry_decay), jnp.zeros_like(local_state)),
    )
    incoming = scanned[1]
    hidden = normalize_gate(intra_part, from_start, query_rows, incoming, gate_rows, gain_table)
    return lax.psum_scatter(
        jnp.dot(hidden, out_weight, preferred_element_type=jnp.float32).astype(jnp.bfloat16),
        "fsdp",
        scatter_dimension=0,
        tiled=True,
    )


def solution(mesh):
    placed = (
        P("seq", "fsdp"),
        P("seq", "fsdp"),
        P("seq", "fsdp"),
        P("seq", "fsdp"),
        P("fsdp"),
        P("fsdp"),
        P("fsdp", None),
    )
    return jax.shard_map(
        per_device, mesh=mesh, in_specs=placed, out_specs=P(("seq", "fsdp"), None), check_vma=False
    )
```

profile of v0, /device:TPU:1, one launch (start us, length us, event | category | flops | bytes accessed | tf_op | source)
XLA Modules:
  0.0 343.4 jit_solution(13943119722820602781)
XLA Ops:
  6.5 1.1 copy.29
  7.7 1.3 dynamic-slice
  10.5 1.9 fusion.11
  12.4 131.2 %all-reduce = f32[256]{0:T(256)S(1)} all-reduce(f32[256]{0:T(256)S(1)} %get-tuple-element.130), channel_id=2, replica_groups=mesh['seq'=64,'fsdp'=16] {'seq'}, use_global_device_ids=true, to_apply=%add | all-reduce | flops 256 | bytes 2048
  143.8 1.1 add_divide_fusion
  145.3 1.5 convolution_bitcast_fusion.1
  146.8 26.6 %all-gather.4.cloned.1.call-done = f32[256,128,128]{2,1,0:T(8,128)} async-done(((f32[4,128,128]{2,1,0:T(8,128)}), f32[256,128,128]{2,1,0:T(8,128)}) %all-gather.4.cloned.1.call-update) | async-done | bytes 16777232 | tf_op jit(solution)/shard_map/all_gather | solution.py:17
  173.5 70.0 %while.14 = (s32[]{:T(128)}, f32[4,128,128]{2,1,0:T(8,128)S(1)}, s32[]{:T(128)}, f32[64,4]{1,0:T(8,128)S(1)}, f32[64,4,128,128]{3,2,1,0:T(8,128)}, /*index=5*/s32[]{:T(128)}, s32[]{:T(128)}) while((s32[]{:T(128)}, f32[4,128,128]{2,1,0:T(8,128)S(1)}, s32[]{:T(128)}, f32[64,4]{1,0:T(8,128)S(1)}, f32[64,4,128,128]{3,2,1,0:T(8,128)}, ...), condition=%wide.region_1.2_spmd.clone, body=%wide.region_0.1_spmd.clone.sunk | while | flops 262148 | bytes 786585 | solution.py:29
  175.7 1.1 fusion.35
  176.8 1.1 fusion.35
  180.1 1.1 fusion.35
  181.1 1.1 fusion.35
  182.2 1.1 fusion.35
  185.5 1.1 fusion.35
  186.6 1.1 fusion.35
  187.7 1.1 fusion.35
  191.0 1.1 fusion.35
  192.1 1.1 fusion.35
  193.2 1.1 fusion.35
  196.5 1.1 fusion.35
  197.6 1.1 fusion.35
  200.8 1.1 fusion.35
  201.9 1.1 fusion.35
  203.0 1.1 fusion.35
  206.3 1.1 fusion.35
  207.4 1.1 fusion.35
  208.5 1.1 fusion.35
  211.8 1.1 fusion.35
  212.9 1.1 fusion.35
  243.9 25.5 %psum.7 = f32[256]{0:T(256)S(1)} all-reduce(f32[256]{0:T(256)S(1)} %get-tuple-element.132), channel_id=1, replica_groups=mesh['seq'=64,'fsdp'=16] {'fsdp'}, use_global_device_ids=true, to_apply=%region_3.4 | all-reduce | flops 256 | bytes 2048 | tf_op jit(solution)/shard_map/psum | solution.py:64
  269.6 6.3 %convolution_convert_fusion = bf16[256,6144]{1,0:T(8,128)(2,1)} fusion(bf16[256,512]{0,1:T(8,128)(2,1)S(1)} %bitcast.59, bf16[512,6144]{1,0:T(8,128)(2,1)} %param.15), kind=kOutput, calls=%fused_computation.3 | convolution fusion | flops 1612185600 | bytes 9699328 | tf_op jit(solution)/shard_map/dot_general | solution.py:103
  275.9 60.7 %reduce-scatter.2.cloned.1.call-done = bf16[16,6144]{1,0:T(8,128)(2,1)} async-done(((bf16[256,6144]{1,0:T(8,128)(2,1)}), bf16[16,6144]{1,0:T(8,128)(2,1)}) %reduce-scatter.2.cloned.1.call-update) | async-done | bytes 196624 | tf_op jit(solution)/shard_map/reduce_scatter | solution.py:102
  (128 shorter events, 47.9 us)
Async XLA Ops:
  6.5 138.8 %copy-start = (bf16[256,512]{1,0:T(8,128)(2,1)S(1)}, bf16[256,512]{1,0:T(8,128)(2,1)}, u32[]{:S(2)}) copy-start(bf16[256,512]{1,0:T(8,128)(2,1)} %param.9) | copy-start | bytes 786436
  6.5 262.9 %copy-start.1 = (f32[512]{0:T(512)S(1)}, f32[512]{0:T(512)}, u32[]{:S(2)}) copy-start(f32[512]{0:T(512)} %param.14) | copy-start | bytes 6148
  6.5 166.9 %all-gather.4.cloned.1.call-start = ((), (), s32[]{:S(2)}) async-start(), calls=%async_computation.2 | async-start | bytes 17039360 | tf_op jit(solution)/shard_map/all_gather | solution.py:17
  12.4 324.2 %reduce-scatter.2.cloned.1.call-start = ((), (), s32[]{:S(2)}) async-start(), calls=%async_computation.1 | async-start | bytes 3342336 | tf_op jit(solution)/shard_map/reduce_scatter | solution.py:102
Sparse Core Ops, SparseCore 0:
  12.5 160.9 all-gather.3
  276.0 60.4 reduce-scatter.1
where the time goes:
time: 346 us; the launch traced here: 343 us
  blocking collectives  157 us (45%)
  waiting for transfers between devices  87.3 us (25%)
  other arithmetic  69.7 us (20%)
  between operations  14.2 us (4%)
  matrix products  10.1 us (3%)
    unnamed x1, blocking collectives  131 us
    select_n x64, other arithmetic, hop(): return jax.tree.map(lambda a, b: jnp.where(reached, a, b), new, before)  67.4 us
    reduce_scatter x1, waiting for transfers between devices, per_device(): lax.psum_scatter(jnp.dot(hidden, out_weight, preferred_element_type=jnp.f...  60.7 us
    all_gather x1, waiting for transfers between devices, prefix(): everything = jax.tree.map(lambda part: lax.all_gather(part, axis), value)  26.6 us
    psum x1, blocking collectives, normalize_gate(): square_sum = lax.psum(local_squares, 'fsdp')  25.5 us
  transfers between devices with their start and end apart: 2, of which 2 were waited for; matrix products, arithmetic and copies ran while one was open for 1% of the time, Pallas kernels for 0%

commit v1 on v0

v1 whole, which is shorter than its diff:
```python
import math

import jax
import jax.numpy as jnp
from jax import lax
from jax.sharding import PartitionSpec as P

HEADS = 64
HEAD_DIM = 128


layer_factor = 1.0 - 78.0 / 79.0 + 1e-05


def decay_slopes(rate_index):
    exponent = -8.0 * (rate_index.astype(jnp.float32) + 1.0) / HEADS
    return jnp.exp(exponent * math.log(2.0)) * layer_factor


def span_terms(query_rows, key_rows, value_rows, slopes):
    tok_count = query_rows.shape[0]
    position = jnp.arange(tok_count).astype(jnp.float32)
    offset = position[:, None] - position[None, :]
    causal = jnp.where(
        offset[None] >= 0.0, jnp.exp(-slopes[:, None, None] * jnp.maximum(offset, 0.0)[None]), 0.0
    )
    scores = jnp.einsum("thd,shd->hts", query_rows, key_rows, preferred_element_type=jnp.float32)
    weighted = (scores * causal).astype(jnp.bfloat16)
    intra_part = jnp.einsum(
        "hts,she->the", weighted, value_rows, preferred_element_type=jnp.float32
    )
    to_end = jnp.exp(-slopes[None, :] * (tok_count - 1.0 - position)[:, None])
    key_scaled = (key_rows.astype(jnp.float32) * to_end[:, :, None]).astype(jnp.bfloat16)
    local_state = jnp.einsum(
        "thd,the->hde", key_scaled, value_rows, preferred_element_type=jnp.float32
    )
    from_start = jnp.exp(-slopes[None, :] * (position + 1.0)[:, None])
    return (intra_part, local_state, from_start)


def decayed_scan(local_state, slopes, tok_count, axis):
    peers = lax.axis_size(axis)
    total = local_state
    shift = 1
    while shift < peers:
        decay = jnp.exp(-slopes * (tok_count * shift))
        moved = lax.ppermute(total, axis, perm=[(i, i + shift) for i in range(peers - shift)])
        total = total + decay[:, None, None] * moved
        shift *= 2
    undo = jnp.exp(slopes * tok_count)
    return (total - local_state) * undo[:, None, None]


def per_device(query_act, key_act, value_act, gate_act, rate_index, norm_gain, out_weight):
    tok_count = query_act.shape[0]
    heads_here = rate_index.shape[0]
    slopes = decay_slopes(rate_index)
    span_shape = (tok_count, heads_here, HEAD_DIM)
    query_rows = query_act.reshape(span_shape)
    key_rows = key_act.reshape(span_shape)
    value_rows = value_act.reshape(span_shape)
    gate_rows = gate_act.reshape(span_shape)
    gain_table = norm_gain.reshape(heads_here, HEAD_DIM)
    intra_part, local_state, from_start = span_terms(query_rows, key_rows, value_rows, slopes)
    incoming = decayed_scan(local_state, slopes, tok_count, "seq")
    inter_part = jnp.einsum(
        "thd,hde->the", query_rows.astype(jnp.float32), incoming, precision=lax.Precision.HIGHEST
    )
    attended = intra_part + from_start[:, :, None] * inter_part
    local_squares = jnp.sum(attended * attended, axis=(1, 2))
    gated = attended * gain_table[None] * jax.nn.sigmoid(gate_rows.astype(jnp.float32))
    gated = gated.reshape(tok_count, -1).astype(jnp.bfloat16)
    projected = jnp.dot(gated, out_weight, preferred_element_type=jnp.float32).astype(jnp.bfloat16)
    summed = lax.psum_scatter(projected, "fsdp", scatter_dimension=0, tiled=True)
    square_sum = lax.psum_scatter(local_squares, "fsdp", scatter_dimension=0, tiled=True)
    inv_rms = lax.rsqrt(square_sum / (HEADS * HEAD_DIM) + 1e-06)
    return (summed.astype(jnp.float32) * inv_rms[:, None]).astype(jnp.bfloat16)


def solution(mesh):
    placed = (
        P("seq", "fsdp"),
        P("seq", "fsdp"),
        P("seq", "fsdp"),
        P("seq", "fsdp"),
        P("fsdp"),
        P("fsdp"),
        P("fsdp", None),
    )
    return jax.shard_map(
        per_device, mesh=mesh, in_specs=placed, out_specs=P(("seq", "fsdp"), None), check_vma=False
    )
```

time: 346 us -> 189 us (0.55)
  blocking collectives: 157 us -> 26.4 us
  starting transfers between devices: 0.04 us -> 69 us
  other arithmetic: 69.7 us -> 4.37 us
  waiting for transfers between devices: 87.3 us -> 63.6 us
    unnamed x1, blocking collectives: 131 us -> 26.4 us
    ppermute x0 -> x6, starting transfers between devices: none -> 69 us  [decayed_scan(): lax.ppermute(total, axis, perm=[(i, i + shift) for i in range(peers - shi...]
    select_n x64 -> x0, other arithmetic: 67.4 us -> none  [hop(): return jax.tree.map(lambda a, b: jnp.where(reached, a, b), new, before)]
    all_gather x1 -> x0, waiting for transfers between devices: 26.6 us -> none  [prefix(): everything = jax.tree.map(lambda part: lax.all_gather(part, axis), value)]
    psum x1 -> x0, blocking collectives: 25.5 us -> none  [normalize_gate(): square_sum = lax.psum(local_squares, 'fsdp')]
    ppermute x0 -> x6, waiting for transfers between devices: none -> 21.9 us  [decayed_scan(): lax.ppermute(total, axis, perm=[(i, i + shift) for i in range(peers - shi...]
    reduce_scatter x1, waiting for transfers between devices: 60.7 us -> 41.7 us  [per_device(): lax.psum_scatter(projected, 'fsdp', scatter_dimension=0, tiled=True)]
  transfers between devices with their start and end apart: 2 -> 7, of which waited for: 2 -> 7; matrix products, arithmetic and copies ran while one was open for 1% -> 2% of each run, Pallas kernels for 0% -> 0%
where the time goes in v1:
time: 189 us
  starting transfers between devices  69 us (37%)
  waiting for transfers between devices  63.6 us (34%)
  blocking collectives  26.4 us (14%)
  between operations  14.2 us (8%)
  matrix products  8.53 us (5%)
  other arithmetic  4.37 us (2%)
  local copies, waits for them, and re-layouts  2.57 us (1%)
    ppermute x6, starting transfers between devices, decayed_scan(): lax.ppermute(total, axis, perm=[(i, i + shift) for i in range(peers - shi...  69 us
    reduce_scatter x1, waiting for transfers between devices, per_device(): lax.psum_scatter(projected, 'fsdp', scatter_dimension=0, tiled=True)  41.7 us
    unnamed x1, blocking collectives  26.4 us
    ppermute x6, waiting for transfers between devices, decayed_scan(): lax.ppermute(total, axis, perm=[(i, i + shift) for i in range(peers - shi...  21.9 us
    dot_general x1, matrix products, per_device(): jnp.dot(gated, out_weight, preferred_element_type=jnp.float32)  6.25 us
  transfers between devices with their start and end apart: 7, of which 7 were waited for; matrix products, arithmetic and copies ran while one was open for 2% of the time, Pallas kernels for 0%

profile of v1, /device:TPU:1, one launch (start us, length us, event | category | flops | bytes accessed | tf_op | source)
XLA Modules:
  0.0 188.7 jit_solution(17634988946317229664)
XLA Ops:
  6.6 0.7 multiply_exponential_fusion.3
  7.3 1.1 copy.21
  8.5 1.2 fusion.10
  9.6 4.0 %collective-permute-start = (f32[4,128,128]{2,1,0:T(8,128)S(1)}, f32[4,128,128]{2,1,0:T(8,128)S(1)}, u32[]{:S(2)}, u32[]{:S(2)}) collective-permute-start(f32[4,128,128]{2,1,0:T(8,128)S(1)} %fusion.10), channel_id=1, source_target_pairs={{0,16},{16,32},{32,48},{48,64},{64,80},{80,96},{96,112},{112,128},... | collective-permute-start | bytes 786440 | tf_op jit(solution)/shard_map/ppermute | solution.py:47
  13.6 3.3 %collective-permute-done = f32[4,128,128]{2,1,0:T(8,128)S(1)} collective-permute-done((f32[4,128,128]{2,1,0:T(8,128)S(1)}, f32[4,128,128]{2,1,0:T(8,128)S(1)}, u32[]{:S(2)}, u32[]{:S(2)}) %collective-permute-start) | collective-permute-done | bytes 262176 | tf_op jit(solution)/shard_map/ppermute | solution.py:47
  16.9 0.1 multiply_add_fusion.4
  17.0 6.7 %collective-permute-start.1 = (f32[4,128,128]{2,1,0:T(8,128)S(1)}, f32[4,128,128]{2,1,0:T(8,128)S(1)}, u32[]{:S(2)}, u32[]{:S(2)}) collective-permute-start(f32[4,128,128]{2,1,0:T(8,128)S(1)} %multiply_add_fusion.4), channel_id=1, source_target_pairs={{0,32},{16,48},{32,64},{48,80},{64,96},{80,112},{96,128},{112,144}... | collective-permute-start | bytes 786440 | tf_op jit(solution)/shard_map/ppermute | solution.py:47
  23.7 4.4 %collective-permute-done.1 = f32[4,128,128]{2,1,0:T(8,128)S(1)} collective-permute-done((f32[4,128,128]{2,1,0:T(8,128)S(1)}, f32[4,128,128]{2,1,0:T(8,128)S(1)}, u32[]{:S(2)}, u32[]{:S(2)}) %collective-permute-start.1) | collective-permute-done | bytes 262176 | tf_op jit(solution)/shard_map/ppermute | solution.py:47
  28.1 0.1 multiply_add_fusion.3
  28.2 13.7 %collective-permute-start.2 = (f32[4,128,128]{2,1,0:T(8,128)S(1)}, f32[4,128,128]{2,1,0:T(8,128)S(1)}, u32[]{:S(2)}, u32[]{:S(2)}) collective-permute-start(f32[4,128,128]{2,1,0:T(8,128)S(1)} %multiply_add_fusion.3), channel_id=1, source_target_pairs={{0,64},{16,80},{32,96},{48,112},{64,128},{80,144},{96,160},{112,17... | collective-permute-start | bytes 786440 | tf_op jit(solution)/shard_map/ppermute | solution.py:47
  41.9 4.4 %collective-permute-done.2 = f32[4,128,128]{2,1,0:T(8,128)S(1)} collective-permute-done((f32[4,128,128]{2,1,0:T(8,128)S(1)}, f32[4,128,128]{2,1,0:T(8,128)S(1)}, u32[]{:S(2)}, u32[]{:S(2)}) %collective-permute-start.2) | collective-permute-done | bytes 262176 | tf_op jit(solution)/shard_map/ppermute | solution.py:47
  46.3 0.1 multiply_add_fusion.2
  46.4 13.7 %collective-permute-start.3 = (f32[4,128,128]{2,1,0:T(8,128)S(1)}, f32[4,128,128]{2,1,0:T(8,128)S(1)}, u32[]{:S(2)}, u32[]{:S(2)}) collective-permute-start(f32[4,128,128]{2,1,0:T(8,128)S(1)} %multiply_add_fusion.2), channel_id=1, source_target_pairs={{0,128},{16,144},{32,160},{48,176},{64,192},{80,208},{96,224},{112... | collective-permute-start | bytes 786440 | tf_op jit(solution)/shard_map/ppermute | solution.py:47
  60.1 1.1 add_divide_fusion
  61.2 2.2 %collective-permute-done.3 = f32[4,128,128]{2,1,0:T(8,128)S(1)} collective-permute-done((f32[4,128,128]{2,1,0:T(8,128)S(1)}, f32[4,128,128]{2,1,0:T(8,128)S(1)}, u32[]{:S(2)}, u32[]{:S(2)}) %collective-permute-start.3) | collective-permute-done | bytes 262176 | tf_op jit(solution)/shard_map/ppermute | solution.py:47
  63.4 0.1 multiply_add_fusion.1
  63.5 11.6 %collective-permute-start.4 = (f32[4,128,128]{2,1,0:T(8,128)S(1)}, f32[4,128,128]{2,1,0:T(8,128)S(1)}, u32[]{:S(2)}, u32[]{:S(2)}) collective-permute-start(f32[4,128,128]{2,1,0:T(8,128)S(1)} %multiply_add_fusion.1), channel_id=1, source_target_pairs={{0,256},{16,272},{32,288},{48,304},{64,320},{80,336},{96,352},{112... | collective-permute-start | bytes 786440 | tf_op jit(solution)/shard_map/ppermute | solution.py:47
  75.0 0.1 subtract_compare_fusion
  75.1 0.2 copy.19
  75.3 0.1 subtract_maximum_fusion
  75.5 3.8 %collective-permute-done.4 = f32[4,128,128]{2,1,0:T(8,128)S(1)} collective-permute-done((f32[4,128,128]{2,1,0:T(8,128)S(1)}, f32[4,128,128]{2,1,0:T(8,128)S(1)}, u32[]{:S(2)}, u32[]{:S(2)}) %collective-permute-start.4) | collective-permute-done | bytes 262176 | tf_op jit(solution)/shard_map/ppermute | solution.py:47
  79.3 0.1 multiply_add_fusion
  79.4 19.4 %collective-permute-start.5 = (f32[4,128,128]{2,1,0:T(8,128)S(1)}, f32[4,128,128]{2,1,0:T(8,128)S(1)}, u32[]{:S(2)}, u32[]{:S(2)}) collective-permute-start(f32[4,128,128]{2,1,0:T(8,128)S(1)} %multiply_add_fusion), channel_id=1, source_target_pairs={{0,512},{16,528},{32,544},{48,560},{64,576},{80,592},{96,608},{112... | collective-permute-start | bytes 786440 | tf_op jit(solution)/shard_map/ppermute | solution.py:47
  98.8 0.5 convolution_bitcast_fusion.1
  99.4 3.8 %collective-permute-done.5 = f32[4,128,128]{2,1,0:T(8,128)S(1)} collective-permute-done((f32[4,128,128]{2,1,0:T(8,128)S(1)}, f32[4,128,128]{2,1,0:T(8,128)S(1)}, u32[]{:S(2)}, u32[]{:S(2)}) %collective-permute-start.5) | collective-permute-done | bytes 262176 | tf_op jit(solution)/shard_map/ppermute | solution.py:47
  103.2 0.6 multiply_reduce_fusion
  103.8 6.3 %convolution_convert_fusion = bf16[256,6144]{1,0:T(8,128)(2,1)} fusion(bf16[256,512]{0,1:T(8,128)(2,1)S(1)} %bitcast.45, bf16[512,6144]{1,0:T(8,128)(2,1)} %param.13), kind=kOutput, calls=%fused_computation | convolution fusion | flops 1612185600 | bytes 9699328 | tf_op jit(solution)/shard_map/dot_general | solution.py:73
  110.0 1.3 dynamic-slice
  112.0 26.4 %all-reduce = f32[256]{0:T(256)S(1)} all-reduce(f32[256]{0:T(256)S(1)} %get-tuple-element.7), channel_id=3, replica_groups=mesh['seq'=64,'fsdp'=16] {'fsdp'}, use_global_device_ids=true, to_apply=%region_2.3.clone | all-reduce | flops 256 | bytes 2048
  138.4 0.1 fusion.31
  138.5 41.7 %reduce-scatter.2.cloned.1.call-done = bf16[16,6144]{1,0:T(8,128)(2,1)} async-done(((bf16[256,6144]{1,0:T(8,128)(2,1)}), bf16[16,6144]{1,0:T(8,128)(2,1)}) %reduce-scatter.2.cloned.1.call-update) | async-done | bytes 196624 | tf_op jit(solution)/shard_map/reduce_scatter | solution.py:74
  180.2 1.7 multiply_convert_fusion.2
  (12 shorter events, 0.1 us)
Async XLA Ops:
  6.5 92.3 %copy-start = (bf16[256,512]{1,0:T(8,128)(2,1)S(1)}, bf16[256,512]{1,0:T(8,128)(2,1)}, u32[]{:S(2)}) copy-start(bf16[256,512]{1,0:T(8,128)(2,1)} %param.7) | copy-start | bytes 786436
  6.5 92.3 %copy-start.1 = (bf16[256,512]{1,0:T(8,128)(2,1)S(1)}, bf16[256,512]{1,0:T(8,128)(2,1)}, u32[]{:S(2)}) copy-start(bf16[256,512]{1,0:T(8,128)(2,1)} %param.9) | copy-start | bytes 786436
  6.5 96.6 %copy-start.2 = (f32[512]{0:T(512)S(1)}, f32[512]{0:T(512)}, u32[]{:S(2)}) copy-start(f32[512]{0:T(512)} %param.12) | copy-start | bytes 6148
  6.5 173.6 %reduce-scatter.2.cloned.1.call-start = ((), (), s32[]{:S(2)}) async-start(), calls=%async_computation.1 | async-start | bytes 3342336 | tf_op jit(solution)/shard_map/reduce_scatter | solution.py:74
  9.6 7.3 %collective-permute-start = (f32[4,128,128]{2,1,0:T(8,128)S(1)}, f32[4,128,128]{2,1,0:T(8,128)S(1)}, u32[]{:S(2)}, u32[]{:S(2)}) collective-permute-start(f32[4,128,128]{2,1,0:T(8,128)S(1)} %fusion.10), channel_id=1, source_target_pairs={{0,16},{16,32},{32,48},{48,64},{64,80},{80,96},{96,112},{112,128},... | collective-permute-start | bytes 786440 | tf_op jit(solution)/shard_map/ppermute | solution.py:47
  17.0 11.1 %collective-permute-start.1 = (f32[4,128,128]{2,1,0:T(8,128)S(1)}, f32[4,128,128]{2,1,0:T(8,128)S(1)}, u32[]{:S(2)}, u32[]{:S(2)}) collective-permute-start(f32[4,128,128]{2,1,0:T(8,128)S(1)} %multiply_add_fusion.4), channel_id=1, source_target_pairs={{0,32},{16,48},{32,64},{48,80},{64,96},{80,112},{96,128},{112,144}... | collective-permute-start | bytes 786440 | tf_op jit(solution)/shard_map/ppermute | solution.py:47
  28.2 18.1 %collective-permute-start.2 = (f32[4,128,128]{2,1,0:T(8,128)S(1)}, f32[4,128,128]{2,1,0:T(8,128)S(1)}, u32[]{:S(2)}, u32[]{:S(2)}) collective-permute-start(f32[4,128,128]{2,1,0:T(8,128)S(1)} %multiply_add_fusion.3), channel_id=1, source_target_pairs={{0,64},{16,80},{32,96},{48,112},{64,128},{80,144},{96,160},{112,17... | collective-permute-start | bytes 786440 | tf_op jit(solution)/shard_map/ppermute | solution.py:47
  46.4 16.9 %collective-permute-start.3 = (f32[4,128,128]{2,1,0:T(8,128)S(1)}, f32[4,128,128]{2,1,0:T(8,128)S(1)}, u32[]{:S(2)}, u32[]{:S(2)}) collective-permute-start(f32[4,128,128]{2,1,0:T(8,128)S(1)} %multiply_add_fusion.2), channel_id=1, source_target_pairs={{0,128},{16,144},{32,160},{48,176},{64,192},{80,208},{96,224},{112... | collective-permute-start | bytes 786440 | tf_op jit(solution)/shard_map/ppermute | solution.py:47
  63.5 15.8 %collective-permute-start.4 = (f32[4,128,128]{2,1,0:T(8,128)S(1)}, f32[4,128,128]{2,1,0:T(8,128)S(1)}, u32[]{:S(2)}, u32[]{:S(2)}) collective-permute-start(f32[4,128,128]{2,1,0:T(8,128)S(1)} %multiply_add_fusion.1), channel_id=1, source_target_pairs={{0,256},{16,272},{32,288},{48,304},{64,320},{80,336},{96,352},{112... | collective-permute-start | bytes 786440 | tf_op jit(solution)/shard_map/ppermute | solution.py:47
  79.4 23.8 %collective-permute-start.5 = (f32[4,128,128]{2,1,0:T(8,128)S(1)}, f32[4,128,128]{2,1,0:T(8,128)S(1)}, u32[]{:S(2)}, u32[]{:S(2)}) collective-permute-start(f32[4,128,128]{2,1,0:T(8,128)S(1)} %multiply_add_fusion), channel_id=1, source_target_pairs={{0,512},{16,528},{32,544},{48,560},{64,576},{80,592},{96,608},{112... | collective-permute-start | bytes 786440 | tf_op jit(solution)/shard_map/ppermute | solution.py:47
Sparse Core Ops, SparseCore 0:
  110.2 69.9 reduce-scatter.1

commit v2 on v1

--- a/solution.py
+++ b/solution.py
@@ -62,7 +62,7 @@
     gate_rows = gate_act.reshape(span_shape)
     gain_table = norm_gain.reshape(heads_here, HEAD_DIM)
     intra_part, local_state, from_start = span_terms(query_rows, key_rows, value_rows, slopes)
-    incoming = decayed_scan(local_state, slopes, tok_count, "seq")
+    incoming = decayed_scan(local_state, slopes, tok_count, ("sz", "sx"))
     inter_part = jnp.einsum(
         "thd,hde->the", query_rows.astype(jnp.float32), incoming, precision=lax.Precision.HIGHEST
     )
@@ -71,22 +71,40 @@
     gated = attended * gain_table[None] * jax.nn.sigmoid(gate_rows.astype(jnp.float32))
     gated = gated.reshape(tok_count, -1).astype(jnp.bfloat16)
     projected = jnp.dot(gated, out_weight, preferred_element_type=jnp.float32).astype(jnp.bfloat16)
-    summed = lax.psum_scatter(projected, "fsdp", scatter_dimension=0, tiled=True)
-    square_sum = lax.psum_scatter(local_squares, "fsdp", scatter_dimension=0, tiled=True)
+    lanes = projected.shape[1]
+    cores = lax.axis_size("fc")
+    chips = lax.axis_size("fy")
+    projected = projected.reshape(chips, cores, tok_count // (chips * cores), lanes)
+    projected = projected.transpose(1, 0, 2, 3).reshape(tok_count, lanes)
+    summed = lax.psum_scatter(projected, "fc", scatter_dimension=0, tiled=True)
+    summed = lax.psum_scatter(summed, "fy", scatter_dimension=0, tiled=True)
+    square_sum = lax.psum_scatter(local_squares, ("fy", "fc"), scatter_dimension=0, tiled=True)
     inv_rms = lax.rsqrt(square_sum / (HEADS * HEAD_DIM) + 1e-06)
     return (summed.astype(jnp.float32) * inv_rms[:, None]).astype(jnp.bfloat16)
 
 
+def split_mesh(mesh):
+    devices = mesh.devices
+    seq, fsdp = devices.shape
+    chips_x = 8 if seq % 8 == 0 else 1
+    cores = 2 if fsdp % 2 == 0 else 1
+    grid = devices.reshape(seq // chips_x, chips_x, fsdp // cores, cores)
+    return jax.sharding.Mesh(grid, ("sz", "sx", "fy", "fc"))
+
+
 def solution(mesh):
+    fine = split_mesh(mesh)
+    seq = ("sz", "sx")
+    fsdp = ("fy", "fc")
     placed = (
-        P("seq", "fsdp"),
-        P("seq", "fsdp"),
-        P("seq", "fsdp"),
-        P("seq", "fsdp"),
-        P("fsdp"),
-        P("fsdp"),
-        P("fsdp", None),
+        P(seq, fsdp),
+        P(seq, fsdp),
+        P(seq, fsdp),
+        P(seq, fsdp),
+        P(fsdp),
+        P(fsdp),
+        P(fsdp, None),
     )
     return jax.shard_map(
-        per_device, mesh=mesh, in_specs=placed, out_specs=P(("seq", "fsdp"), None), check_vma=False
+        per_device, mesh=fine, in_specs=placed, out_specs=P(seq + fsdp, None), check_vma=False
     )

time: 189 us -> 196 us (1.037); the launches traced: 189 us -> 193 us
  waiting for transfers between devices: 63.6 us -> 71.5 us
  blocking collectives: 26.4 us -> 22.3 us
  local copies, waits for them, and re-layouts: 2.57 us -> 4.54 us
    reduce_scatter x1 -> x2, waiting for transfers between devices: 41.7 us -> 49.6 us  [the longest x1 28.7 us: per_device(): summed = lax.psum_scatter(projected, 'fc', scatter_dimension=0, tiled=True)]
    unnamed x1, blocking collectives: 26.4 us -> 22.3 us
    transpose x0 -> x1, local copies, waits for them, and re-layouts: none -> 1.97 us  [per_device(): projected = projected.transpose(1, 0, 2, 3).reshape(tok_count, lanes)]
  transfers between devices with their start and end apart: 7 -> 8, of which waited for: 7 -> 8; matrix products, arithmetic and copies ran while one was open for 2% -> 2% of each run, Pallas kernels for 0% -> 0%
where the time goes in v2:
time: 196 us; the launch traced here: 193 us
  waiting for transfers between devices  71.5 us (36%)
  starting transfers between devices  69.1 us (35%)
  blocking collectives  22.3 us (11%)
  between operations  14.2 us (7%)
  matrix products  6.88 us (4%)
  local copies, waits for them, and re-layouts  4.54 us (2%)
  other arithmetic  4.37 us (2%)
    ppermute x6, starting transfers between devices, decayed_scan(): lax.ppermute(total, axis, perm=[(i, i + shift) for i in range(peers - shi...  69 us
    reduce_scatter x1, waiting for transfers between devices, per_device(): summed = lax.psum_scatter(projected, 'fc', scatter_dimension=0, tiled=True)  28.7 us
    unnamed x1, blocking collectives  22.3 us
    ppermute x6, waiting for transfers between devices, decayed_scan(): lax.ppermute(total, axis, perm=[(i, i + shift) for i in range(peers - shi...  21.9 us
    reduce_scatter x1, waiting for transfers between devices, per_device(): summed = lax.psum_scatter(summed, 'fy', scatter_dimension=0, tiled=True)  20.9 us
    dot_general x1, matrix products, per_device(): jnp.dot(gated, out_weight, preferred_element_type=jnp.float32)  4.61 us
  transfers between devices with their start and end apart: 8, of which 8 were waited for; matrix products, arithmetic and copies ran while one was open for 2% of the time, Pallas kernels for 0%

profile of v2, /device:TPU:1, one launch (start us, length us, event | category | flops | bytes accessed | tf_op | source)
XLA Modules:
  0.0 192.9 jit_solution(7318107697621020515)
XLA Ops:
  6.6 0.7 multiply_exponential_fusion.3
  7.3 1.1 copy.23
  8.5 1.2 fusion.10
  9.6 4.0 %collective-permute-start = (f32[4,128,128]{2,1,0:T(8,128)S(1)}, f32[4,128,128]{2,1,0:T(8,128)S(1)}, u32[]{:S(2)}, u32[]{:S(2)}) collective-permute-start(f32[4,128,128]{2,1,0:T(8,128)S(1)} %fusion.10), channel_id=1, source_target_pairs={{0,16},{16,32},{32,48},{48,64},{64,80},{80,96},{96,112},{112,128},... | collective-permute-start | bytes 786440 | tf_op jit(solution)/shard_map/ppermute | solution.py:47
  13.6 3.3 %collective-permute-done = f32[4,128,128]{2,1,0:T(8,128)S(1)} collective-permute-done((f32[4,128,128]{2,1,0:T(8,128)S(1)}, f32[4,128,128]{2,1,0:T(8,128)S(1)}, u32[]{:S(2)}, u32[]{:S(2)}) %collective-permute-start) | collective-permute-done | bytes 262176 | tf_op jit(solution)/shard_map/ppermute | solution.py:47
  16.9 0.1 multiply_add_fusion.4
  17.0 6.7 %collective-permute-start.1 = (f32[4,128,128]{2,1,0:T(8,128)S(1)}, f32[4,128,128]{2,1,0:T(8,128)S(1)}, u32[]{:S(2)}, u32[]{:S(2)}) collective-permute-start(f32[4,128,128]{2,1,0:T(8,128)S(1)} %multiply_add_fusion.4), channel_id=1, source_target_pairs={{0,32},{16,48},{32,64},{48,80},{64,96},{80,112},{96,128},{112,144}... | collective-permute-start | bytes 786440 | tf_op jit(solution)/shard_map/ppermute | solution.py:47
  23.7 4.4 %collective-permute-done.1 = f32[4,128,128]{2,1,0:T(8,128)S(1)} collective-permute-done((f32[4,128,128]{2,1,0:T(8,128)S(1)}, f32[4,128,128]{2,1,0:T(8,128)S(1)}, u32[]{:S(2)}, u32[]{:S(2)}) %collective-permute-start.1) | collective-permute-done | bytes 262176 | tf_op jit(solution)/shard_map/ppermute | solution.py:47
  28.2 13.7 %collective-permute-start.2 = (f32[4,128,128]{2,1,0:T(8,128)S(1)}, f32[4,128,128]{2,1,0:T(8,128)S(1)}, u32[]{:S(2)}, u32[]{:S(2)}) collective-permute-start(f32[4,128,128]{2,1,0:T(8,128)S(1)} %multiply_add_fusion.3), channel_id=1, source_target_pairs={{0,64},{16,80},{32,96},{48,112},{64,128},{80,144},{96,160},{112,17... | collective-permute-start | bytes 786440 | tf_op jit(solution)/shard_map/ppermute | solution.py:47
  41.9 4.4 %collective-permute-done.2 = f32[4,128,128]{2,1,0:T(8,128)S(1)} collective-permute-done((f32[4,128,128]{2,1,0:T(8,128)S(1)}, f32[4,128,128]{2,1,0:T(8,128)S(1)}, u32[]{:S(2)}, u32[]{:S(2)}) %collective-permute-start.2) | collective-permute-done | bytes 262176 | tf_op jit(solution)/shard_map/ppermute | solution.py:47
  46.3 0.1 multiply_add_fusion.2
  46.4 13.7 %collective-permute-start.3 = (f32[4,128,128]{2,1,0:T(8,128)S(1)}, f32[4,128,128]{2,1,0:T(8,128)S(1)}, u32[]{:S(2)}, u32[]{:S(2)}) collective-permute-start(f32[4,128,128]{2,1,0:T(8,128)S(1)} %multiply_add_fusion.2), channel_id=1, source_target_pairs={{0,128},{16,144},{32,160},{48,176},{64,192},{80,208},{96,224},{112... | collective-permute-start | bytes 786440 | tf_op jit(solution)/shard_map/ppermute | solution.py:47
  60.1 1.1 add_divide_fusion
  61.2 2.2 %collective-permute-done.3 = f32[4,128,128]{2,1,0:T(8,128)S(1)} collective-permute-done((f32[4,128,128]{2,1,0:T(8,128)S(1)}, f32[4,128,128]{2,1,0:T(8,128)S(1)}, u32[]{:S(2)}, u32[]{:S(2)}) %collective-permute-start.3) | collective-permute-done | bytes 262176 | tf_op jit(solution)/shard_map/ppermute | solution.py:47
  63.4 0.1 multiply_add_fusion.1
  63.5 11.6 %collective-permute-start.4 = (f32[4,128,128]{2,1,0:T(8,128)S(1)}, f32[4,128,128]{2,1,0:T(8,128)S(1)}, u32[]{:S(2)}, u32[]{:S(2)}) collective-permute-start(f32[4,128,128]{2,1,0:T(8,128)S(1)} %multiply_add_fusion.1), channel_id=1, source_target_pairs={{0,256},{16,272},{32,288},{48,304},{64,320},{80,336},{96,352},{112... | collective-permute-start | bytes 786440 | tf_op jit(solution)/shard_map/ppermute | solution.py:47
  75.0 0.1 subtract_compare_fusion
  75.1 0.2 copy.20
  75.3 0.1 subtract_maximum_fusion
  75.5 3.8 %collective-permute-done.4 = f32[4,128,128]{2,1,0:T(8,128)S(1)} collective-permute-done((f32[4,128,128]{2,1,0:T(8,128)S(1)}, f32[4,128,128]{2,1,0:T(8,128)S(1)}, u32[]{:S(2)}, u32[]{:S(2)}) %collective-permute-start.4) | collective-permute-done | bytes 262176 | tf_op jit(solution)/shard_map/ppermute | solution.py:47
  79.3 0.1 multiply_add_fusion
  79.4 19.4 %collective-permute-start.5 = (f32[4,128,128]{2,1,0:T(8,128)S(1)}, f32[4,128,128]{2,1,0:T(8,128)S(1)}, u32[]{:S(2)}, u32[]{:S(2)}) collective-permute-start(f32[4,128,128]{2,1,0:T(8,128)S(1)} %multiply_add_fusion), channel_id=1, source_target_pairs={{0,512},{16,528},{32,544},{48,560},{64,576},{80,592},{96,608},{112... | collective-permute-start | bytes 786440 | tf_op jit(solution)/shard_map/ppermute | solution.py:47
  98.8 0.5 convolution_bitcast_fusion.1
  99.4 3.8 %collective-permute-done.5 = f32[4,128,128]{2,1,0:T(8,128)S(1)} collective-permute-done((f32[4,128,128]{2,1,0:T(8,128)S(1)}, f32[4,128,128]{2,1,0:T(8,128)S(1)}, u32[]{:S(2)}, u32[]{:S(2)}) %collective-permute-start.5) | collective-permute-done | bytes 262176 | tf_op jit(solution)/shard_map/ppermute | solution.py:47
  103.2 0.6 multiply_reduce_fusion
  103.8 4.6 %convolution_convert_fusion = bf16[256,6144]{1,0:T(8,128)(2,1)S(1)} fusion(bf16[256,512]{0,1:T(8,128)(2,1)S(1)} %bitcast.51, bf16[512,6144]{1,0:T(8,128)(2,1)} %param.13), kind=kOutput, calls=%fused_computation | convolution fusion | flops 1612185600 | bytes 9699328 | tf_op jit(solution)/shard_map/dot_general | solution.py:73
  108.4 2.0 %copy.21 = bf16[2,8,16,6144]{3,2,1,0:T(8,128)(2,1)} copy(bf16[2,8,16,6144]{3,2,0,1:T(8,128)(2,1)S(1)} %bitcast.49) | data formatting | bytes 6291456 | tf_op jit(solution)/shard_map/transpose | solution.py:78
  110.4 28.7 %reduce-scatter.3.cloned.1.call-done = bf16[128,6144]{1,0:T(8,128)(2,1)} async-done(((bf16[256,6144]{1,0:T(8,128)(2,1)}), bf16[128,6144]{1,0:T(8,128)(2,1)}) %reduce-scatter.3.cloned.1.call-update) | async-done | bytes 1572880 | tf_op jit(solution)/shard_map/reduce_scatter | solution.py:79
  139.2 1.3 dynamic-slice
  141.1 22.3 %all-reduce = f32[256]{0:T(256)S(1)} all-reduce(f32[256]{0:T(256)S(1)} %get-tuple-element.7), channel_id=4, replica_groups=mesh['sz'=8,'sx'=8,'fy'=8,'fc'=2] {'fy','fc'}, use_global_device_ids=true, to_apply=%region_3.4.clone | all-reduce | flops 256 | bytes 2048
  163.5 20.9 %reduce-scatter.5.cloned.1.call-done = bf16[16,6144]{1,0:T(8,128)(2,1)} async-done(((bf16[128,6144]{1,0:T(8,128)(2,1)}), bf16[16,6144]{1,0:T(8,128)(2,1)}) %reduce-scatter.5.cloned.1.call-update) | async-done | bytes 196624 | tf_op jit(solution)/shard_map/reduce_scatter | solution.py:80
  184.3 1.7 multiply_convert_fusion.2
  (16 shorter events, 0.4 us)
Async XLA Ops:
  6.5 92.3 %copy-start = (bf16[256,512]{1,0:T(8,128)(2,1)S(1)}, bf16[256,512]{1,0:T(8,128)(2,1)}, u32[]{:S(2)}) copy-start(bf16[256,512]{1,0:T(8,128)(2,1)} %param.7) | copy-start | bytes 786436
  6.5 92.3 %copy-start.1 = (bf16[256,512]{1,0:T(8,128)(2,1)S(1)}, bf16[256,512]{1,0:T(8,128)(2,1)}, u32[]{:S(2)}) copy-start(bf16[256,512]{1,0:T(8,128)(2,1)} %param.9) | copy-start | bytes 786436
  6.5 96.6 %copy-start.2 = (f32[512]{0:T(512)S(1)}, f32[512]{0:T(512)}, u32[]{:S(2)}) copy-start(f32[512]{0:T(512)} %param.12) | copy-start | bytes 6148
  6.5 132.6 %reduce-scatter.3.cloned.1.call-start = ((), (), s32[]{:S(2)}) async-start(), calls=%async_computation.2 | async-start | bytes 4718592 | tf_op jit(solution)/shard_map/reduce_scatter | solution.py:79
  9.6 7.3 %collective-permute-start = (f32[4,128,128]{2,1,0:T(8,128)S(1)}, f32[4,128,128]{2,1,0:T(8,128)S(1)}, u32[]{:S(2)}, u32[]{:S(2)}) collective-permute-start(f32[4,128,128]{2,1,0:T(8,128)S(1)} %fusion.10), channel_id=1, source_target_pairs={{0,16},{16,32},{32,48},{48,64},{64,80},{80,96},{96,112},{112,128},... | collective-permute-start | bytes 786440 | tf_op jit(solution)/shard_map/ppermute | solution.py:47
  17.0 11.1 %collective-permute-start.1 = (f32[4,128,128]{2,1,0:T(8,128)S(1)}, f32[4,128,128]{2,1,0:T(8,128)S(1)}, u32[]{:S(2)}, u32[]{:S(2)}) collective-permute-start(f32[4,128,128]{2,1,0:T(8,128)S(1)} %multiply_add_fusion.4), channel_id=1, source_target_pairs={{0,32},{16,48},{32,64},{48,80},{64,96},{80,112},{96,128},{112,144}... | collective-permute-start | bytes 786440 | tf_op jit(solution)/shard_map/ppermute | solution.py:47
  28.2 18.1 %collective-permute-start.2 = (f32[4,128,128]{2,1,0:T(8,128)S(1)}, f32[4,128,128]{2,1,0:T(8,128)S(1)}, u32[]{:S(2)}, u32[]{:S(2)}) collective-permute-start(f32[4,128,128]{2,1,0:T(8,128)S(1)} %multiply_add_fusion.3), channel_id=1, source_target_pairs={{0,64},{16,80},{32,96},{48,112},{64,128},{80,144},{96,160},{112,17... | collective-permute-start | bytes 786440 | tf_op jit(solution)/shard_map/ppermute | solution.py:47
  46.4 16.9 %collective-permute-start.3 = (f32[4,128,128]{2,1,0:T(8,128)S(1)}, f32[4,128,128]{2,1,0:T(8,128)S(1)}, u32[]{:S(2)}, u32[]{:S(2)}) collective-permute-start(f32[4,128,128]{2,1,0:T(8,128)S(1)} %multiply_add_fusion.2), channel_id=1, source_target_pairs={{0,128},{16,144},{32,160},{48,176},{64,192},{80,208},{96,224},{112... | collective-permute-start | bytes 786440 | tf_op jit(solution)/shard_map/ppermute | solution.py:47
  63.5 15.8 %collective-permute-start.4 = (f32[4,128,128]{2,1,0:T(8,128)S(1)}, f32[4,128,128]{2,1,0:T(8,128)S(1)}, u32[]{:S(2)}, u32[]{:S(2)}) collective-permute-start(f32[4,128,128]{2,1,0:T(8,128)S(1)} %multiply_add_fusion.1), channel_id=1, source_target_pairs={{0,256},{16,272},{32,288},{48,304},{64,320},{80,336},{96,352},{112... | collective-permute-start | bytes 786440 | tf_op jit(solution)/shard_map/ppermute | solution.py:47
  79.4 23.8 %collective-permute-start.5 = (f32[4,128,128]{2,1,0:T(8,128)S(1)}, f32[4,128,128]{2,1,0:T(8,128)S(1)}, u32[]{:S(2)}, u32[]{:S(2)}) collective-permute-start(f32[4,128,128]{2,1,0:T(8,128)S(1)} %multiply_add_fusion), channel_id=1, source_target_pairs={{0,512},{16,528},{32,544},{48,560},{64,576},{80,592},{96,608},{112... | collective-permute-start | bytes 786440 | tf_op jit(solution)/shard_map/ppermute | solution.py:47
  110.4 74.0 %reduce-scatter.5.cloned.1.call-start = ((), (), s32[]{:S(2)}) async-start(), calls=%async_computation.3 | async-start | bytes 1769472 | tf_op jit(solution)/shard_map/reduce_scatter | solution.py:80
Sparse Core Ops, SparseCore 0:
  110.5 28.6 reduce-scatter.2
  143.0 41.3 reduce-scatter.4

commit v3 on v2

--- a/solution.py
+++ b/solution.py
@@ -38,17 +38,25 @@
     return (intra_part, local_state, from_start)
 
 
-def decayed_scan(local_state, slopes, tok_count, axis):
-    peers = lax.axis_size(axis)
-    total = local_state
-    shift = 1
-    while shift < peers:
-        decay = jnp.exp(-slopes * (tok_count * shift))
-        moved = lax.ppermute(total, axis, perm=[(i, i + shift) for i in range(peers - shift)])
-        total = total + decay[:, None, None] * moved
-        shift *= 2
-    undo = jnp.exp(slopes * tok_count)
-    return (total - local_state) * undo[:, None, None]
+def decayed_scan(local_state, slopes, tok_count):
+    chips_x = lax.axis_size("sx")
+    chips_z = lax.axis_size("sz")
+    x = lax.axis_index("sx")
+    z = lax.axis_index("sz")
+    rate = slopes[None, :] * tok_count
+    row = lax.all_gather(local_state.astype(jnp.bfloat16), "sx").astype(jnp.float32)
+    xs = jnp.arange(chips_x)
+    before = jnp.where(
+        (xs < x)[:, None], jnp.exp(-rate * jnp.maximum(x - 1 - xs, 0).astype(jnp.float32)[:, None]), 0.0
+    )
+    to_end = jnp.exp(-rate * (chips_x - 1 - xs).astype(jnp.float32)[:, None])
+    in_row = jnp.sum(before[:, :, None, None] * row, axis=0)
+    row_total = jnp.sum(to_end[:, :, None, None] * row, axis=0)
+    column = lax.all_gather(row_total.astype(jnp.bfloat16), "sz").astype(jnp.float32)
+    zs = jnp.arange(chips_z)
+    steps = chips_x * jnp.maximum(z - 1 - zs, 0) + x
+    earlier = jnp.where((zs < z)[:, None], jnp.exp(-rate * steps.astype(jnp.float32)[:, None]), 0.0)
+    return in_row + jnp.sum(earlier[:, :, None, None] * column, axis=0)
 
 
 def per_device(query_act, key_act, value_act, gate_act, rate_index, norm_gain, out_weight):
@@ -62,7 +70,7 @@
     gate_rows = gate_act.reshape(span_shape)
     gain_table = norm_gain.reshape(heads_here, HEAD_DIM)
     intra_part, local_state, from_start = span_terms(query_rows, key_rows, value_rows, slopes)
-    incoming = decayed_scan(local_state, slopes, tok_count, ("sz", "sx"))
+    incoming = decayed_scan(local_state, slopes, tok_count)
     inter_part = jnp.einsum(
         "thd,hde->the", query_rows.astype(jnp.float32), incoming, precision=lax.Precision.HIGHEST
     )
@@ -71,13 +79,7 @@
     gated = attended * gain_table[None] * jax.nn.sigmoid(gate_rows.astype(jnp.float32))
     gated = gated.reshape(tok_count, -1).astype(jnp.bfloat16)
     projected = jnp.dot(gated, out_weight, preferred_element_type=jnp.float32).astype(jnp.bfloat16)
-    lanes = projected.shape[1]
-    cores = lax.axis_size("fc")
-    chips = lax.axis_size("fy")
-    projected = projected.reshape(chips, cores, tok_count // (chips * cores), lanes)
-    projected = projected.transpose(1, 0, 2, 3).reshape(tok_count, lanes)
-    summed = lax.psum_scatter(projected, "fc", scatter_dimension=0, tiled=True)
-    summed = lax.psum_scatter(summed, "fy", scatter_dimension=0, tiled=True)
+    summed = lax.psum_scatter(projected, ("fy", "fc"), scatter_dimension=0, tiled=True)
     square_sum = lax.psum_scatter(local_squares, ("fy", "fc"), scatter_dimension=0, tiled=True)
     inv_rms = lax.rsqrt(square_sum / (HEADS * HEAD_DIM) + 1e-06)
     return (summed.astype(jnp.float32) * inv_rms[:, None]).astype(jnp.bfloat16)

time: 196 us -> 194 us (0.990); the launches traced: 193 us -> 194 us
  starting transfers between devices: 69.1 us -> 0.09 us
  waiting for transfers between devices: 71.5 us -> 133 us
  blocking collectives: 22.3 us -> 28.5 us
  other arithmetic: 4.37 us -> 7.04 us
  matrix products: 6.88 us -> 9.12 us
  local copies, waits for them, and re-layouts: 4.54 us -> 2.57 us
    all_gather x0 -> x2, waiting for transfers between devices: none -> 95.2 us  [the longest x1 50.8 us: decayed_scan(): lax.all_gather(local_state.astype(jnp.bfloat16), 'sx').astype(jnp.float32)]
    ppermute x6 -> x0, starting transfers between devices: 69 us -> none  [decayed_scan(): lax.ppermute(total, axis, perm=[(i, i + shift) for i in range(peers - shi...]
    ppermute x6 -> x0, waiting for transfers between devices: 21.9 us -> none  [decayed_scan(): lax.ppermute(total, axis, perm=[(i, i + shift) for i in range(peers - shi...]
    reduce_scatter x2 -> x1, waiting for transfers between devices: 49.6 us -> 37.6 us  [per_device(): lax.psum_scatter(projected, ('fy', 'fc'), scatter_dimension=0, tiled=True)]
    unnamed x1, blocking collectives: 22.3 us -> 28.5 us
    reduce_sum x0 -> x2, other arithmetic: none -> 3.99 us  [the longest x1 2.43 us: decayed_scan(): row_total = jnp.sum(to_end[:, :, None, None] * row, axis=0)]
    transpose x1 -> x0, local copies, waits for them, and re-layouts: 1.97 us -> none  [per_device(): projected = projected.transpose(1, 0, 2, 3).reshape(tok_count, lanes)]
  transfers between devices with their start and end apart: 8 -> 3, of which waited for: 8 -> 3; matrix products, arithmetic and copies ran while one was open for 2% -> 1% of each run, Pallas kernels for 0% -> 0%
where the time goes in v3:
time: 194 us
  waiting for transfers between devices  133 us (69%)
  blocking collectives  28.5 us (15%)
  between operations  13.9 us (7%)
  matrix products  9.12 us (5%)
  other arithmetic  7.04 us (4%)
  local copies, waits for them, and re-layouts  2.57 us (1%)
    all_gather x1, waiting for transfers between devices, decayed_scan(): lax.all_gather(local_state.astype(jnp.bfloat16), 'sx').astype(jnp.float32)  50.8 us
    all_gather x1, waiting for transfers between devices, decayed_scan(): lax.all_gather(row_total.astype(jnp.bfloat16), 'sz').astype(jnp.float32)  44.5 us
    reduce_scatter x1, waiting for transfers between devices, per_device(): lax.psum_scatter(projected, ('fy', 'fc'), scatter_dimension=0, tiled=True)  37.6 us
    unnamed x1, blocking collectives  28.5 us
    dot_general x1, matrix products, per_device(): jnp.dot(gated, out_weight, preferred_element_type=jnp.float32)  6.26 us
  transfers between devices with their start and end apart: 3, of which 3 were waited for; matrix products, arithmetic and copies ran while one was open for 1% of the time, Pallas kernels for 0%

profile of v3, /device:TPU:1, one launch (start us, length us, event | category | flops | bytes accessed | tf_op | source)
XLA Modules:
  0.0 194.1 jit_solution(8791376020023067751)
XLA Ops:
  6.5 0.0 copy-start
  6.5 0.0 all-gather.5.cloned.1.call-start
  6.5 0.7 multiply_negate_fusion
  7.3 1.1 copy.20
  8.4 0.1 multiply_exponential_fusion.2
  8.4 1.8 convolution_convert_fusion.1
  10.3 0.0 all-gather.5.cloned.1.call-update
  10.3 0.0 all-gather.7.cloned.1.call-start
  10.4 0.1 exponential_select_fusion
  10.5 50.8 %all-gather.5.cloned.1.call-done = bf16[32,128,128]{2,1,0:T(8,128)(2,1)} async-done(((bf16[4,128,128]{2,1,0:T(8,128)(2,1)}), bf16[32,128,128]{2,1,0:T(8,128)(2,1)}) %all-gather.5.cloned.1.call-update) | async-done | bytes 1048592 | tf_op jit(solution)/shard_map/all_gather | solution.py:47
  61.3 2.4 %fusion.1 = (bf16[4,128,128]{2,1,0:T(8,128)(2,1)}, f32[4,128,128]{2,1,0:T(8,128)S(1)}) fusion(bf16[8,4,128,128]{3,2,1,0:T(8,128)(2,1)} %bitcast.51, f32[8,4]{1,0:T(8,128)S(1)} %get-tuple-element.12, f32[8,4]{1,0:T(8,128)S(1)} %get-tuple-element.13), kind=kLoop, calls=%fused_computation.4 | loop fusion | flops 2490368 | bytes 1442048 | tf_op jit(solution)/shard_map/reduce_sum | solution.py:54
  63.7 0.0 all-gather.7.cloned.1.call-update
  63.7 0.0 reduce-scatter.2.cloned.1.call-start
  63.8 0.0 copy-done.1
  63.8 0.1 add_divide_fusion
  63.9 0.2 copy.18
  64.1 0.0 copy-start.2
  64.1 0.1 subtract_compare_fusion
  64.3 0.1 subtract_maximum_fusion
  64.4 0.0 copy-done
  64.4 0.0 copy-done.3
  64.4 0.5 convolution_bitcast_fusion.1
  64.9 44.5 %all-gather.7.cloned.1.call-done = bf16[32,128,128]{2,1,0:T(8,128)(2,1)} async-done(((bf16[4,128,128]{2,1,0:T(8,128)(2,1)}), bf16[32,128,128]{2,1,0:T(8,128)(2,1)}) %all-gather.7.cloned.1.call-update) | async-done | bytes 1048592 | tf_op jit(solution)/shard_map/all_gather | solution.py:55
  109.4 1.6 fusion.2
  111.0 0.5 multiply_reduce_fusion
  111.5 6.3 %convolution_convert_fusion = bf16[256,6144]{1,0:T(8,128)(2,1)} fusion(bf16[256,512]{0,1:T(8,128)(2,1)S(1)} %bitcast.49, bf16[512,6144]{1,0:T(8,128)(2,1)} %param.13), kind=kOutput, calls=%fused_computation | convolution fusion | flops 1612185600 | bytes 9699328 | tf_op jit(solution)/shard_map/dot_general | solution.py:81
  117.7 0.0 reduce-scatter.2.cloned.1.call-update
  117.8 1.3 dynamic-slice
  119.7 28.5 %all-reduce = f32[256]{0:T(256)S(1)} all-reduce(f32[256]{0:T(256)S(1)} %get-tuple-element.7), channel_id=5, replica_groups=mesh['sz'=8,'sx'=8,'fy'=8,'fc'=2] {'fy','fc'}, use_global_device_ids=true, to_apply=%region_5.6.clone | all-reduce | flops 256 | bytes 2048
  148.2 0.1 fusion.28
  148.3 37.6 %reduce-scatter.2.cloned.1.call-done = bf16[16,6144]{1,0:T(8,128)(2,1)} async-done(((bf16[256,6144]{1,0:T(8,128)(2,1)}), bf16[16,6144]{1,0:T(8,128)(2,1)}) %reduce-scatter.2.cloned.1.call-update) | async-done | bytes 196624 | tf_op jit(solution)/shard_map/reduce_scatter | solution.py:82
  185.9 1.7 multiply_convert_fusion.2
  (8 shorter events, 0.0 us)
Async XLA Ops:
  6.5 57.8 %copy-start = (bf16[256,512]{1,0:T(8,128)(2,1)S(1)}, bf16[256,512]{1,0:T(8,128)(2,1)}, u32[]{:S(2)}) copy-start(bf16[256,512]{1,0:T(8,128)(2,1)} %param.7) | copy-start | bytes 786436
  6.5 57.2 %copy-start.1 = (bf16[256,512]{1,0:T(8,128)(2,1)S(1)}, bf16[256,512]{1,0:T(8,128)(2,1)}, u32[]{:S(2)}) copy-start(bf16[256,512]{1,0:T(8,128)(2,1)} %param.10) | copy-start | bytes 786436
  6.5 54.7 %all-gather.5.cloned.1.call-start = ((), (), s32[]{:S(2)}) async-start(), calls=%async_computation.2 | async-start | bytes 1179648 | tf_op jit(solution)/shard_map/all_gather | solution.py:47
  10.3 54.1 %copy-start.3 = (bf16[256,512]{1,0:T(8,128)(2,1)S(1)}, bf16[256,512]{1,0:T(8,128)(2,1)}, u32[]{:S(2)}) copy-start(bf16[256,512]{1,0:T(8,128)(2,1)} %param.9) | copy-start | bytes 786436
  10.3 99.1 %all-gather.7.cloned.1.call-start = ((), (), s32[]{:S(2)}) async-start(), calls=%async_computation.3 | async-start | bytes 1179648 | tf_op jit(solution)/shard_map/all_gather | solution.py:55
  63.7 122.2 %reduce-scatter.2.cloned.1.call-start = ((), (), s32[]{:S(2)}) async-start(), calls=%async_computation.1 | async-start | bytes 3342336 | tf_op jit(solution)/shard_map/reduce_scatter | solution.py:82
  64.1 46.8 %copy-start.2 = (f32[512]{0:T(512)S(1)}, f32[512]{0:T(512)}, u32[]{:S(2)}) copy-start(f32[512]{0:T(512)} %param.12) | copy-start | bytes 6148
Sparse Core Ops, SparseCore 0:
  10.4 50.7 all-gather.4
  63.9 45.4 all-gather.6
  117.9 67.9 reduce-scatter.1

commit v4 on v2

--- a/solution.py
+++ b/solution.py
@@ -51,6 +51,28 @@
     return (total - local_state) * undo[:, None, None]
 
 
+def fsdp_reduce(parts):
+    chips = lax.axis_size("fy")
+    core = lax.axis_index("fc")
+    chip = lax.axis_index("fy")
+    keep = lax.dynamic_index_in_dim(parts, core, axis=1, keepdims=False)
+    give = lax.dynamic_index_in_dim(parts, 1 - core, axis=1, keepdims=False)
+    got = lax.ppermute(give, "fc", perm=[(0, 1), (1, 0)])
+    mine = keep.astype(jnp.float32) + got.astype(jnp.float32)
+    half = mine.shape[2] // 2
+    halves = []
+    for sign, cols in ((1, slice(0, half)), (-1, slice(half, None))):
+        blocks = mine[:, :, cols]
+        pairs = [(j, (j + sign) % chips) for j in range(chips)]
+        cur = lax.dynamic_index_in_dim(blocks, (chip - sign) % chips, axis=0, keepdims=False)
+        for k in range(chips - 1):
+            recv = lax.ppermute(cur.astype(jnp.bfloat16), "fy", perm=pairs)
+            own = lax.dynamic_index_in_dim(blocks, (chip - sign * (k + 2)) % chips, axis=0, keepdims=False)
+            cur = recv.astype(jnp.float32) + own
+        halves.append(cur)
+    return jnp.concatenate(halves, axis=1)
+
+
 def per_device(query_act, key_act, value_act, gate_act, rate_index, norm_gain, out_weight):
     tok_count = query_act.shape[0]
     heads_here = rate_index.shape[0]
@@ -71,14 +93,11 @@
     gated = attended * gain_table[None] * jax.nn.sigmoid(gate_rows.astype(jnp.float32))
     gated = gated.reshape(tok_count, -1).astype(jnp.bfloat16)
     projected = jnp.dot(gated, out_weight, preferred_element_type=jnp.float32).astype(jnp.bfloat16)
-    lanes = projected.shape[1]
-    cores = lax.axis_size("fc")
-    chips = lax.axis_size("fy")
-    projected = projected.reshape(chips, cores, tok_count // (chips * cores), lanes)
-    projected = projected.transpose(1, 0, 2, 3).reshape(tok_count, lanes)
-    summed = lax.psum_scatter(projected, "fc", scatter_dimension=0, tiled=True)
-    summed = lax.psum_scatter(summed, "fy", scatter_dimension=0, tiled=True)
-    square_sum = lax.psum_scatter(local_squares, ("fy", "fc"), scatter_dimension=0, tiled=True)
+    summed = fsdp_reduce(projected.reshape(-1, 2, tok_count // 16, projected.shape[1]))
+    gathered = lax.all_gather(local_squares, ("fy", "fc"))
+    owner = lax.axis_index("fy") * lax.axis_size("fc") + lax.axis_index("fc")
+    rows = summed.shape[0]
+    square_sum = lax.dynamic_slice_in_dim(jnp.sum(gathered, axis=0), owner * rows, rows)
     inv_rms = lax.rsqrt(square_sum / (HEADS * HEAD_DIM) + 1e-06)
     return (summed.astype(jnp.float32) * inv_rms[:, None]).astype(jnp.bfloat16)
 

time: 196 us -> 187 us (0.954)
  the two profiles are of different devices: /device:TPU:1 before, /device:TPU:256 now
where the time goes in v4:
time: 187 us
  starting transfers between devices  87.9 us (47%)
  waiting for transfers between devices  64.9 us (35%)
  blocking collectives  18.7 us (10%)
  matrix products  6.93 us (4%)
  other arithmetic  4.6 us (2%)
  local copies, waits for them, and re-layouts  2.88 us (2%)
    ppermute x6, waiting for transfers between devices, decayed_scan(): lax.ppermute(total, axis, perm=[(i, i + shift) for i in range(peers - shi...  58 us
    ppermute x14, starting transfers between devices, fsdp_reduce(): recv = lax.ppermute(cur.astype(jnp.bfloat16), 'fy', perm=pairs)  49.6 us
    ppermute x6, starting transfers between devices, decayed_scan(): lax.ppermute(total, axis, perm=[(i, i + shift) for i in range(peers - shi...  36.4 us
    all_gather x1, blocking collectives, per_device(): gathered = lax.all_gather(local_squares, ('fy', 'fc'))  18.7 us
    ppermute x14, waiting for transfers between devices, fsdp_reduce(): recv = lax.ppermute(cur.astype(jnp.bfloat16), 'fy', perm=pairs)  6.83 us
    dot_general x1, matrix products, per_device(): jnp.dot(gated, out_weight, preferred_element_type=jnp.float32)  4.61 us
  transfers between devices with their start and end apart: 21, of which 14 were waited for; matrix products, arithmetic and copies ran while one was open for 1% of the time, Pallas kernels for 0%

profile of v4, /device:TPU:256, one launch (start us, length us, event | category | flops | bytes accessed | tf_op | source)
XLA Modules:
  0.0 186.6 jit_solution(17785140492050479041)
XLA Ops:
  3.1 3.4 %collective-permute-start = (f32[4,128,128]{2,1,0:T(8,128)S(1)}, f32[4,128,128]{2,1,0:T(8,128)S(1)}, u32[]{:S(2)}, u32[]{:S(2)}) collective-permute-start(f32[4,128,128]{2,1,0:T(8,128)S(1)} %fusion.11), channel_id=1, source_target_pairs={{0,16},{16,32},{32,48},{48,64},{64,80},{80,96},{96,112},{112,128},... | collective-permute-start | bytes 786440 | tf_op jit(solution)/shard_map/ppermute | solution.py:47
  6.5 8.6 %collective-permute-done = f32[4,128,128]{2,1,0:T(8,128)S(1)} collective-permute-done((f32[4,128,128]{2,1,0:T(8,128)S(1)}, f32[4,128,128]{2,1,0:T(8,128)S(1)}, u32[]{:S(2)}, u32[]{:S(2)}) %collective-permute-start) | collective-permute-done | bytes 262176 | tf_op jit(solution)/shard_map/ppermute | solution.py:47
  15.3 2.2 %collective-permute-start.1 = (f32[4,128,128]{2,1,0:T(8,128)S(1)}, f32[4,128,128]{2,1,0:T(8,128)S(1)}, u32[]{:S(2)}, u32[]{:S(2)}) collective-permute-start(f32[4,128,128]{2,1,0:T(8,128)S(1)} %multiply_add_fusion.4), channel_id=1, source_target_pairs={{0,32},{16,48},{32,64},{48,80},{64,96},{80,112},{96,128},{112,144}... | collective-permute-start | bytes 786440 | tf_op jit(solution)/shard_map/ppermute | solution.py:47
  17.5 13.6 %collective-permute-done.1 = f32[4,128,128]{2,1,0:T(8,128)S(1)} collective-permute-done((f32[4,128,128]{2,1,0:T(8,128)S(1)}, f32[4,128,128]{2,1,0:T(8,128)S(1)}, u32[]{:S(2)}, u32[]{:S(2)}) %collective-permute-start.1) | collective-permute-done | bytes 262176 | tf_op jit(solution)/shard_map/ppermute | solution.py:47
  31.2 7.4 %collective-permute-start.2 = (f32[4,128,128]{2,1,0:T(8,128)S(1)}, f32[4,128,128]{2,1,0:T(8,128)S(1)}, u32[]{:S(2)}, u32[]{:S(2)}) collective-permute-start(f32[4,128,128]{2,1,0:T(8,128)S(1)} %multiply_add_fusion.3), channel_id=1, source_target_pairs={{0,64},{16,80},{32,96},{48,112},{64,128},{80,144},{96,160},{112,17... | collective-permute-start | bytes 786440 | tf_op jit(solution)/shard_map/ppermute | solution.py:47
  38.6 11.0 %collective-permute-done.2 = f32[4,128,128]{2,1,0:T(8,128)S(1)} collective-permute-done((f32[4,128,128]{2,1,0:T(8,128)S(1)}, f32[4,128,128]{2,1,0:T(8,128)S(1)}, u32[]{:S(2)}, u32[]{:S(2)}) %collective-permute-start.2) | collective-permute-done | bytes 262176 | tf_op jit(solution)/shard_map/ppermute | solution.py:47
  49.7 5.1 %collective-permute-start.3 = (f32[4,128,128]{2,1,0:T(8,128)S(1)}, f32[4,128,128]{2,1,0:T(8,128)S(1)}, u32[]{:S(2)}, u32[]{:S(2)}) collective-permute-start(f32[4,128,128]{2,1,0:T(8,128)S(1)} %multiply_add_fusion.2), channel_id=1, source_target_pairs={{0,128},{16,144},{32,160},{48,176},{64,192},{80,208},{96,224},{112... | collective-permute-start | bytes 786440 | tf_op jit(solution)/shard_map/ppermute | solution.py:47
  55.1 5.5 %collective-permute-done.3 = f32[4,128,128]{2,1,0:T(8,128)S(1)} collective-permute-done((f32[4,128,128]{2,1,0:T(8,128)S(1)}, f32[4,128,128]{2,1,0:T(8,128)S(1)}, u32[]{:S(2)}, u32[]{:S(2)}) %collective-permute-start.3) | collective-permute-done | bytes 262176 | tf_op jit(solution)/shard_map/ppermute | solution.py:47
  60.7 9.1 %collective-permute-start.4 = (f32[4,128,128]{2,1,0:T(8,128)S(1)}, f32[4,128,128]{2,1,0:T(8,128)S(1)}, u32[]{:S(2)}, u32[]{:S(2)}) collective-permute-start(f32[4,128,128]{2,1,0:T(8,128)S(1)} %multiply_add_fusion.1), channel_id=1, source_target_pairs={{0,256},{16,272},{32,288},{48,304},{64,320},{80,336},{96,352},{112... | collective-permute-start | bytes 786440 | tf_op jit(solution)/shard_map/ppermute | solution.py:47
  70.2 9.9 %collective-permute-done.4 = f32[4,128,128]{2,1,0:T(8,128)S(1)} collective-permute-done((f32[4,128,128]{2,1,0:T(8,128)S(1)}, f32[4,128,128]{2,1,0:T(8,128)S(1)}, u32[]{:S(2)}, u32[]{:S(2)}) %collective-permute-start.4) | collective-permute-done | bytes 262176 | tf_op jit(solution)/shard_map/ppermute | solution.py:47
  80.3 9.2 %collective-permute-start.5 = (f32[4,128,128]{2,1,0:T(8,128)S(1)}, f32[4,128,128]{2,1,0:T(8,128)S(1)}, u32[]{:S(2)}, u32[]{:S(2)}) collective-permute-start(f32[4,128,128]{2,1,0:T(8,128)S(1)} %multiply_add_fusion), channel_id=1, source_target_pairs={{0,512},{16,528},{32,544},{48,560},{64,576},{80,592},{96,608},{112... | collective-permute-start | bytes 786440 | tf_op jit(solution)/shard_map/ppermute | solution.py:47
  90.0 9.3 %collective-permute-done.5 = f32[4,128,128]{2,1,0:T(8,128)S(1)} collective-permute-done((f32[4,128,128]{2,1,0:T(8,128)S(1)}, f32[4,128,128]{2,1,0:T(8,128)S(1)}, u32[]{:S(2)}, u32[]{:S(2)}) %collective-permute-start.5) | collective-permute-done | bytes 262176 | tf_op jit(solution)/shard_map/ppermute | solution.py:47
  99.8 4.6 %convolution_convert_fusion = bf16[256,6144]{1,0:T(8,128)(2,1)S(1)} fusion(bf16[256,512]{0,1:T(8,128)(2,1)S(1)} %bitcast.111, bf16[512,6144]{1,0:T(8,128)(2,1)} %param.13), kind=kOutput, calls=%fused_computation | convolution fusion | flops 1612185600 | bytes 9699328 | tf_op jit(solution)/shard_map/dot_general | solution.py:95
  104.5 1.3 dynamic-slice_bitcast_fusion
  105.8 1.9 %collective-permute-start.6 = (bf16[8,16,6144]{2,1,0:T(8,128)(2,1)}, bf16[8,16,6144]{2,1,0:T(8,128)(2,1)}, u32[]{:S(2)}, u32[]{:S(2)}) collective-permute-start(bf16[8,16,6144]{2,1,0:T(8,128)(2,1)} %dynamic-slice_bitcast_fusion), channel_id=1, source_target_pairs={{0,1},{1,0},{2,3},{3,2},{4,5},{5,4},{6,7},{7,6},{8,9},{9,8},{10,11... | collective-permute-start | bytes 4718600 | tf_op jit(solution)/shard_map/ppermute | solution.py:60
  108.0 18.7 %all-gather.1 = f32[16,1,256]{2,1,0:T(1,128)S(1)} all-gather(f32[1,1,256]{2,1,0:T(1,128)S(1)} %bitcast.114), channel_id=2, replica_groups=mesh['sz'=8,'sx'=8,'fy'=8,'fc'=2] {'fy','fc'}, dimensions={0}, use_global_device_ids=true | all-gather | bytes 17408 | tf_op jit(solution)/shard_map/all_gather | solution.py:97
  126.8 1.8 convert_add_fusion
  128.8 1.9 %collective-permute-start.7 = (bf16[16,3072]{1,0:T(8,128)(2,1)S(1)}, bf16[16,3072]{1,0:T(8,128)(2,1)S(1)}, u32[]{:S(2)}, u32[]{:S(2)}) collective-permute-start(bf16[16,3072]{1,0:T(8,128)(2,1)S(1)} %fusion.41), channel_id=1, source_target_pairs={{0,2},{2,4},{4,6},{6,8},{8,10},{10,12},{12,14},{14,0},{1,3},{3,5},... | collective-permute-start | bytes 294920 | tf_op jit(solution)/shard_map/ppermute | solution.py:69
  130.8 5.1 %collective-permute-start.14 = (bf16[16,3072]{1,0:T(8,128)(2,1)S(1)}, bf16[16,3072]{1,0:T(8,128)(2,1)S(1)}, u32[]{:S(2)}, u32[]{:S(2)}) collective-permute-start(bf16[16,3072]{1,0:T(8,128)(2,1)S(1)} %fusion.42), channel_id=1, source_target_pairs={{0,14},{2,0},{4,2},{6,4},{8,6},{10,8},{12,10},{14,12},{1,15},{3,1}... | collective-permute-start | bytes 294920 | tf_op jit(solution)/shard_map/ppermute | solution.py:69
  137.0 1.9 %collective-permute-start.8 = (bf16[16,3072]{1,0:T(8,128)(2,1)S(1)}, bf16[16,3072]{1,0:T(8,128)(2,1)S(1)}, u32[]{:S(2)}, u32[]{:S(2)}) collective-permute-start(bf16[16,3072]{1,0:T(8,128)(2,1)S(1)} %fusion.38), channel_id=1, source_target_pairs={{0,2},{2,4},{4,6},{6,8},{8,10},{10,12},{12,14},{14,0},{1,3},{3,5},... | collective-permute-start | bytes 294920 | tf_op jit(solution)/shard_map/ppermute | solution.py:69
  139.0 5.1 %collective-permute-start.15 = (bf16[16,3072]{1,0:T(8,128)(2,1)S(1)}, bf16[16,3072]{1,0:T(8,128)(2,1)S(1)}, u32[]{:S(2)}, u32[]{:S(2)}) collective-permute-start(bf16[16,3072]{1,0:T(8,128)(2,1)S(1)} %fusion.32), channel_id=1, source_target_pairs={{0,14},{2,0},{4,2},{6,4},{8,6},{10,8},{12,10},{14,12},{1,15},{3,1}... | collective-permute-start | bytes 294920 | tf_op jit(solution)/shard_map/ppermute | solution.py:69
  144.7 1.9 %collective-permute-start.9 = (bf16[16,3072]{1,0:T(8,128)(2,1)S(1)}, bf16[16,3072]{1,0:T(8,128)(2,1)S(1)}, u32[]{:S(2)}, u32[]{:S(2)}) collective-permute-start(bf16[16,3072]{1,0:T(8,128)(2,1)S(1)} %fusion.37), channel_id=1, source_target_pairs={{0,2},{2,4},{4,6},{6,8},{8,10},{10,12},{12,14},{14,0},{1,3},{3,5},... | collective-permute-start | bytes 294920 | tf_op jit(solution)/shard_map/ppermute | solution.py:69
  146.7 5.1 %collective-permute-start.16 = (bf16[16,3072]{1,0:T(8,128)(2,1)S(1)}, bf16[16,3072]{1,0:T(8,128)(2,1)S(1)}, u32[]{:S(2)}, u32[]{:S(2)}) collective-permute-start(bf16[16,3072]{1,0:T(8,128)(2,1)S(1)} %fusion.31), channel_id=1, source_target_pairs={{0,14},{2,0},{4,2},{6,4},{8,6},{10,8},{12,10},{14,12},{1,15},{3,1}... | collective-permute-start | bytes 294920 | tf_op jit(solution)/shard_map/ppermute | solution.py:69
  152.5 1.9 %collective-permute-start.10 = (bf16[16,3072]{1,0:T(8,128)(2,1)S(1)}, bf16[16,3072]{1,0:T(8,128)(2,1)S(1)}, u32[]{:S(2)}, u32[]{:S(2)}) collective-permute-start(bf16[16,3072]{1,0:T(8,128)(2,1)S(1)} %fusion.36), channel_id=1, source_target_pairs={{0,2},{2,4},{4,6},{6,8},{8,10},{10,12},{12,14},{14,0},{1,3},{3,5},... | collective-permute-start | bytes 294920 | tf_op jit(solution)/shard_map/ppermute | solution.py:69
  154.4 5.1 %collective-permute-start.17 = (bf16[16,3072]{1,0:T(8,128)(2,1)S(1)}, bf16[16,3072]{1,0:T(8,128)(2,1)S(1)}, u32[]{:S(2)}, u32[]{:S(2)}) collective-permute-start(bf16[16,3072]{1,0:T(8,128)(2,1)S(1)} %fusion.30), channel_id=1, source_target_pairs={{0,14},{2,0},{4,2},{6,4},{8,6},{10,8},{12,10},{14,12},{1,15},{3,1}... | collective-permute-start | bytes 294920 | tf_op jit(solution)/shard_map/ppermute | solution.py:69
  160.2 1.9 %collective-permute-start.11 = (bf16[16,3072]{1,0:T(8,128)(2,1)S(1)}, bf16[16,3072]{1,0:T(8,128)(2,1)S(1)}, u32[]{:S(2)}, u32[]{:S(2)}) collective-permute-start(bf16[16,3072]{1,0:T(8,128)(2,1)S(1)} %fusion.35), channel_id=1, source_target_pairs={{0,2},{2,4},{4,6},{6,8},{8,10},{10,12},{12,14},{14,0},{1,3},{3,5},... | collective-permute-start | bytes 294920 | tf_op jit(solution)/shard_map/ppermute | solution.py:69
  162.2 5.1 %collective-permute-start.18 = (bf16[16,3072]{1,0:T(8,128)(2,1)S(1)}, bf16[16,3072]{1,0:T(8,128)(2,1)S(1)}, u32[]{:S(2)}, u32[]{:S(2)}) collective-permute-start(bf16[16,3072]{1,0:T(8,128)(2,1)S(1)} %fusion.29), channel_id=1, source_target_pairs={{0,14},{2,0},{4,2},{6,4},{8,6},{10,8},{12,10},{14,12},{1,15},{3,1}... | collective-permute-start | bytes 294920 | tf_op jit(solution)/shard_map/ppermute | solution.py:69
  168.0 1.9 %collective-permute-start.12 = (bf16[16,3072]{1,0:T(8,128)(2,1)S(1)}, bf16[16,3072]{1,0:T(8,128)(2,1)S(1)}, u32[]{:S(2)}, u32[]{:S(2)}) collective-permute-start(bf16[16,3072]{1,0:T(8,128)(2,1)S(1)} %fusion.34), channel_id=1, source_target_pairs={{0,2},{2,4},{4,6},{6,8},{8,10},{10,12},{12,14},{14,0},{1,3},{3,5},... | collective-permute-start | bytes 294920 | tf_op jit(solution)/shard_map/ppermute | solution.py:69
  169.9 5.1 %collective-permute-start.19 = (bf16[16,3072]{1,0:T(8,128)(2,1)S(1)}, bf16[16,3072]{1,0:T(8,128)(2,1)S(1)}, u32[]{:S(2)}, u32[]{:S(2)}) collective-permute-start(bf16[16,3072]{1,0:T(8,128)(2,1)S(1)} %fusion.28), channel_id=1, source_target_pairs={{0,14},{2,0},{4,2},{6,4},{8,6},{10,8},{12,10},{14,12},{1,15},{3,1}... | collective-permute-start | bytes 294920 | tf_op jit(solution)/shard_map/ppermute | solution.py:69
  176.3 1.9 %collective-permute-start.13 = (bf16[16,3072]{1,0:T(8,128)(2,1)S(1)}, bf16[16,3072]{1,0:T(8,128)(2,1)S(1)}, u32[]{:S(2)}, u32[]{:S(2)}) collective-permute-start(bf16[16,3072]{1,0:T(8,128)(2,1)S(1)} %fusion.33), channel_id=1, source_target_pairs={{0,2},{2,4},{4,6},{6,8},{8,10},{10,12},{12,14},{14,0},{1,3},{3,5},... | collective-permute-start | bytes 294920 | tf_op jit(solution)/shard_map/ppermute | solution.py:69
  178.3 5.3 %collective-permute-start.20 = (bf16[16,3072]{1,0:T(8,128)(2,1)S(1)}, bf16[16,3072]{1,0:T(8,128)(2,1)S(1)}, u32[]{:S(2)}, u32[]{:S(2)}) collective-permute-start(bf16[16,3072]{1,0:T(8,128)(2,1)S(1)} %fusion.27), channel_id=1, source_target_pairs={{0,14},{2,0},{4,2},{6,4},{8,6},{10,8},{12,10},{14,12},{1,15},{3,1}... | collective-permute-start | bytes 294920 | tf_op jit(solution)/shard_map/ppermute | solution.py:69
  184.0 1.8 collective-permute-done.20
  (60 shorter events, 11.8 us)
Async XLA Ops:
  0.0 89.4 %copy-start = (bf16[256,512]{1,0:T(8,128)(2,1)S(1)}, bf16[256,512]{1,0:T(8,128)(2,1)}, u32[]{:S(2)}) copy-start(bf16[256,512]{1,0:T(8,128)(2,1)} %param.7) | copy-start | bytes 786436
  1.9 53.0 %copy-start.1 = (bf16[256,512]{1,0:T(8,128)(2,1)S(1)}, bf16[256,512]{1,0:T(8,128)(2,1)}, u32[]{:S(2)}) copy-start(bf16[256,512]{1,0:T(8,128)(2,1)} %param.10) | copy-start | bytes 786436
  3.1 12.1 %collective-permute-start = (f32[4,128,128]{2,1,0:T(8,128)S(1)}, f32[4,128,128]{2,1,0:T(8,128)S(1)}, u32[]{:S(2)}, u32[]{:S(2)}) collective-permute-start(f32[4,128,128]{2,1,0:T(8,128)S(1)} %fusion.11), channel_id=1, source_target_pairs={{0,16},{16,32},{32,48},{48,64},{64,80},{80,96},{96,112},{112,128},... | collective-permute-start | bytes 786440 | tf_op jit(solution)/shard_map/ppermute | solution.py:47
  15.3 15.8 %collective-permute-start.1 = (f32[4,128,128]{2,1,0:T(8,128)S(1)}, f32[4,128,128]{2,1,0:T(8,128)S(1)}, u32[]{:S(2)}, u32[]{:S(2)}) collective-permute-start(f32[4,128,128]{2,1,0:T(8,128)S(1)} %multiply_add_fusion.4), channel_id=1, source_target_pairs={{0,32},{16,48},{32,64},{48,80},{64,96},{80,112},{96,128},{112,144}... | collective-permute-start | bytes 786440 | tf_op jit(solution)/shard_map/ppermute | solution.py:47
  31.2 18.5 %collective-permute-start.2 = (f32[4,128,128]{2,1,0:T(8,128)S(1)}, f32[4,128,128]{2,1,0:T(8,128)S(1)}, u32[]{:S(2)}, u32[]{:S(2)}) collective-permute-start(f32[4,128,128]{2,1,0:T(8,128)S(1)} %multiply_add_fusion.3), channel_id=1, source_target_pairs={{0,64},{16,80},{32,96},{48,112},{64,128},{80,144},{96,160},{112,17... | collective-permute-start | bytes 786440 | tf_op jit(solution)/shard_map/ppermute | solution.py:47
  49.7 10.9 %collective-permute-start.3 = (f32[4,128,128]{2,1,0:T(8,128)S(1)}, f32[4,128,128]{2,1,0:T(8,128)S(1)}, u32[]{:S(2)}, u32[]{:S(2)}) collective-permute-start(f32[4,128,128]{2,1,0:T(8,128)S(1)} %multiply_add_fusion.2), channel_id=1, source_target_pairs={{0,128},{16,144},{32,160},{48,176},{64,192},{80,208},{96,224},{112... | collective-permute-start | bytes 786440 | tf_op jit(solution)/shard_map/ppermute | solution.py:47
  55.0 34.4 %copy-start.2 = (bf16[256,512]{1,0:T(8,128)(2,1)S(1)}, bf16[256,512]{1,0:T(8,128)(2,1)}, u32[]{:S(2)}) copy-start(bf16[256,512]{1,0:T(8,128)(2,1)} %param.9) | copy-start | bytes 786436
  60.7 19.5 %collective-permute-start.4 = (f32[4,128,128]{2,1,0:T(8,128)S(1)}, f32[4,128,128]{2,1,0:T(8,128)S(1)}, u32[]{:S(2)}, u32[]{:S(2)}) collective-permute-start(f32[4,128,128]{2,1,0:T(8,128)S(1)} %multiply_add_fusion.1), channel_id=1, source_target_pairs={{0,256},{16,272},{32,288},{48,304},{64,320},{80,336},{96,352},{112... | collective-permute-start | bytes 786440 | tf_op jit(solution)/shard_map/ppermute | solution.py:47
  80.2 19.1 %copy-start.3 = (f32[512]{0:T(512)S(1)}, f32[512]{0:T(512)}, u32[]{:S(2)}) copy-start(f32[512]{0:T(512)} %param.12) | copy-start | bytes 6148
  80.3 19.0 %collective-permute-start.5 = (f32[4,128,128]{2,1,0:T(8,128)S(1)}, f32[4,128,128]{2,1,0:T(8,128)S(1)}, u32[]{:S(2)}, u32[]{:S(2)}) collective-permute-start(f32[4,128,128]{2,1,0:T(8,128)S(1)} %multiply_add_fusion), channel_id=1, source_target_pairs={{0,512},{16,528},{32,544},{48,560},{64,576},{80,592},{96,608},{112... | collective-permute-start | bytes 786440 | tf_op jit(solution)/shard_map/ppermute | solution.py:47
  105.8 21.0 %collective-permute-start.6 = (bf16[8,16,6144]{2,1,0:T(8,128)(2,1)}, bf16[8,16,6144]{2,1,0:T(8,128)(2,1)}, u32[]{:S(2)}, u32[]{:S(2)}) collective-permute-start(bf16[8,16,6144]{2,1,0:T(8,128)(2,1)} %dynamic-slice_bitcast_fusion), channel_id=1, source_target_pairs={{0,1},{1,0},{2,3},{3,2},{4,5},{5,4},{6,7},{7,6},{8,9},{9,8},{10,11... | collective-permute-start | bytes 4718600 | tf_op jit(solution)/shard_map/ppermute | solution.py:60
  128.8 8.1 %collective-permute-start.7 = (bf16[16,3072]{1,0:T(8,128)(2,1)S(1)}, bf16[16,3072]{1,0:T(8,128)(2,1)S(1)}, u32[]{:S(2)}, u32[]{:S(2)}) collective-permute-start(bf16[16,3072]{1,0:T(8,128)(2,1)S(1)} %fusion.41), channel_id=1, source_target_pairs={{0,2},{2,4},{4,6},{6,8},{8,10},{10,12},{12,14},{14,0},{1,3},{3,5},... | collective-permute-start | bytes 294920 | tf_op jit(solution)/shard_map/ppermute | solution.py:69
  130.8 8.1 %collective-permute-start.14 = (bf16[16,3072]{1,0:T(8,128)(2,1)S(1)}, bf16[16,3072]{1,0:T(8,128)(2,1)S(1)}, u32[]{:S(2)}, u32[]{:S(2)}) collective-permute-start(bf16[16,3072]{1,0:T(8,128)(2,1)S(1)} %fusion.42), channel_id=1, source_target_pairs={{0,14},{2,0},{4,2},{6,4},{8,6},{10,8},{12,10},{14,12},{1,15},{3,1}... | collective-permute-start | bytes 294920 | tf_op jit(solution)/shard_map/ppermute | solution.py:69
  137.0 7.7 %collective-permute-start.8 = (bf16[16,3072]{1,0:T(8,128)(2,1)S(1)}, bf16[16,3072]{1,0:T(8,128)(2,1)S(1)}, u32[]{:S(2)}, u32[]{:S(2)}) collective-permute-start(bf16[16,3072]{1,0:T(8,128)(2,1)S(1)} %fusion.38), channel_id=1, source_target_pairs={{0,2},{2,4},{4,6},{6,8},{8,10},{10,12},{12,14},{14,0},{1,3},{3,5},... | collective-permute-start | bytes 294920 | tf_op jit(solution)/shard_map/ppermute | solution.py:69
  139.0 7.7 %collective-permute-start.15 = (bf16[16,3072]{1,0:T(8,128)(2,1)S(1)}, bf16[16,3072]{1,0:T(8,128)(2,1)S(1)}, u32[]{:S(2)}, u32[]{:S(2)}) collective-permute-start(bf16[16,3072]{1,0:T(8,128)(2,1)S(1)} %fusion.32), channel_id=1, source_target_pairs={{0,14},{2,0},{4,2},{6,4},{8,6},{10,8},{12,10},{14,12},{1,15},{3,1}... | collective-permute-start | bytes 294920 | tf_op jit(solution)/shard_map/ppermute | solution.py:69
  144.7 7.7 %collective-permute-start.9 = (bf16[16,3072]{1,0:T(8,128)(2,1)S(1)}, bf16[16,3072]{1,0:T(8,128)(2,1)S(1)}, u32[]{:S(2)}, u32[]{:S(2)}) collective-permute-start(bf16[16,3072]{1,0:T(8,128)(2,1)S(1)} %fusion.37), channel_id=1, source_target_pairs={{0,2},{2,4},{4,6},{6,8},{8,10},{10,12},{12,14},{14,0},{1,3},{3,5},... | collective-permute-start | bytes 294920 | tf_op jit(solution)/shard_map/ppermute | solution.py:69
  146.7 7.7 %collective-permute-start.16 = (bf16[16,3072]{1,0:T(8,128)(2,1)S(1)}, bf16[16,3072]{1,0:T(8,128)(2,1)S(1)}, u32[]{:S(2)}, u32[]{:S(2)}) collective-permute-start(bf16[16,3072]{1,0:T(8,128)(2,1)S(1)} %fusion.31), channel_id=1, source_target_pairs={{0,14},{2,0},{4,2},{6,4},{8,6},{10,8},{12,10},{14,12},{1,15},{3,1}... | collective-permute-start | bytes 294920 | tf_op jit(solution)/shard_map/ppermute | solution.py:69
  152.5 7.7 %collective-permute-start.10 = (bf16[16,3072]{1,0:T(8,128)(2,1)S(1)}, bf16[16,3072]{1,0:T(8,128)(2,1)S(1)}, u32[]{:S(2)}, u32[]{:S(2)}) collective-permute-start(bf16[16,3072]{1,0:T(8,128)(2,1)S(1)} %fusion.36), channel_id=1, source_target_pairs={{0,2},{2,4},{4,6},{6,8},{8,10},{10,12},{12,14},{14,0},{1,3},{3,5},... | collective-permute-start | bytes 294920 | tf_op jit(solution)/shard_map/ppermute | solution.py:69
  154.4 7.7 %collective-permute-start.17 = (bf16[16,3072]{1,0:T(8,128)(2,1)S(1)}, bf16[16,3072]{1,0:T(8,128)(2,1)S(1)}, u32[]{:S(2)}, u32[]{:S(2)}) collective-permute-start(bf16[16,3072]{1,0:T(8,128)(2,1)S(1)} %fusion.30), channel_id=1, source_target_pairs={{0,14},{2,0},{4,2},{6,4},{8,6},{10,8},{12,10},{14,12},{1,15},{3,1}... | collective-permute-start | bytes 294920 | tf_op jit(solution)/shard_map/ppermute | solution.py:69
  160.2 7.7 %collective-permute-start.11 = (bf16[16,3072]{1,0:T(8,128)(2,1)S(1)}, bf16[16,3072]{1,0:T(8,128)(2,1)S(1)}, u32[]{:S(2)}, u32[]{:S(2)}) collective-permute-start(bf16[16,3072]{1,0:T(8,128)(2,1)S(1)} %fusion.35), channel_id=1, source_target_pairs={{0,2},{2,4},{4,6},{6,8},{8,10},{10,12},{12,14},{14,0},{1,3},{3,5},... | collective-permute-start | bytes 294920 | tf_op jit(solution)/shard_map/ppermute | solution.py:69
  162.2 7.7 %collective-permute-start.18 = (bf16[16,3072]{1,0:T(8,128)(2,1)S(1)}, bf16[16,3072]{1,0:T(8,128)(2,1)S(1)}, u32[]{:S(2)}, u32[]{:S(2)}) collective-permute-start(bf16[16,3072]{1,0:T(8,128)(2,1)S(1)} %fusion.29), channel_id=1, source_target_pairs={{0,14},{2,0},{4,2},{6,4},{8,6},{10,8},{12,10},{14,12},{1,15},{3,1}... | collective-permute-start | bytes 294920 | tf_op jit(solution)/shard_map/ppermute | solution.py:69
  168.0 8.3 %collective-permute-start.12 = (bf16[16,3072]{1,0:T(8,128)(2,1)S(1)}, bf16[16,3072]{1,0:T(8,128)(2,1)S(1)}, u32[]{:S(2)}, u32[]{:S(2)}) collective-permute-start(bf16[16,3072]{1,0:T(8,128)(2,1)S(1)} %fusion.34), channel_id=1, source_target_pairs={{0,2},{2,4},{4,6},{6,8},{8,10},{10,12},{12,14},{14,0},{1,3},{3,5},... | collective-permute-start | bytes 294920 | tf_op jit(solution)/shard_map/ppermute | solution.py:69
  169.9 8.3 %collective-permute-start.19 = (bf16[16,3072]{1,0:T(8,128)(2,1)S(1)}, bf16[16,3072]{1,0:T(8,128)(2,1)S(1)}, u32[]{:S(2)}, u32[]{:S(2)}) collective-permute-start(bf16[16,3072]{1,0:T(8,128)(2,1)S(1)} %fusion.28), channel_id=1, source_target_pairs={{0,14},{2,0},{4,2},{6,4},{8,6},{10,8},{12,10},{14,12},{1,15},{3,1}... | collective-permute-start | bytes 294920 | tf_op jit(solution)/shard_map/ppermute | solution.py:69
  176.3 7.7 %collective-permute-start.13 = (bf16[16,3072]{1,0:T(8,128)(2,1)S(1)}, bf16[16,3072]{1,0:T(8,128)(2,1)S(1)}, u32[]{:S(2)}, u32[]{:S(2)}) collective-permute-start(bf16[16,3072]{1,0:T(8,128)(2,1)S(1)} %fusion.33), channel_id=1, source_target_pairs={{0,2},{2,4},{4,6},{6,8},{8,10},{10,12},{12,14},{14,0},{1,3},{3,5},... | collective-permute-start | bytes 294920 | tf_op jit(solution)/shard_map/ppermute | solution.py:69
  178.3 7.5 %collective-permute-start.20 = (bf16[16,3072]{1,0:T(8,128)(2,1)S(1)}, bf16[16,3072]{1,0:T(8,128)(2,1)S(1)}, u32[]{:S(2)}, u32[]{:S(2)}) collective-permute-start(bf16[16,3072]{1,0:T(8,128)(2,1)S(1)} %fusion.27), channel_id=1, source_target_pairs={{0,14},{2,0},{4,2},{6,4},{8,6},{10,8},{12,10},{14,12},{1,15},{3,1}... | collective-permute-start | bytes 294920 | tf_op jit(solution)/shard_map/ppermute | solution.py:69

commit v5 on v2

--- a/solution.py
+++ b/solution.py
@@ -51,6 +51,42 @@
     return (total - local_state) * undo[:, None, None]
 
 
+def pack(values, squares):
+    hi = squares.astype(jnp.bfloat16)
+    lo = (squares - hi.astype(jnp.float32)).astype(jnp.bfloat16)
+    pad = jnp.zeros(squares.shape + (126,), jnp.bfloat16)
+    extra = jnp.concatenate([hi[..., None], lo[..., None], pad], axis=-1)
+    return jnp.concatenate([values.astype(jnp.bfloat16), extra], axis=-1)
+
+
+def unpack(packed, lanes):
+    squares = packed[..., lanes].astype(jnp.float32) + packed[..., lanes + 1].astype(jnp.float32)
+    return packed[..., :lanes].astype(jnp.float32), squares
+
+
+def fsdp_reduce(parts, squares):
+    chips = lax.axis_size("fy")
+    core = lax.axis_index("fc")
+    chip = lax.axis_index("fy")
+    lanes = parts.shape[-1]
+    keep = lax.dynamic_index_in_dim(parts, core, axis=1, keepdims=False)
+    keep_sq = lax.dynamic_index_in_dim(squares, core, axis=1, keepdims=False)
+    give = lax.dynamic_index_in_dim(parts, 1 - core, axis=1, keepdims=False)
+    give_sq = lax.dynamic_index_in_dim(squares, 1 - core, axis=1, keepdims=False)
+    got, got_sq = unpack(lax.ppermute(pack(give, give_sq), "fc", perm=[(0, 1), (1, 0)]), lanes)
+    mine = keep.astype(jnp.float32) + got
+    mine_sq = keep_sq + got_sq
+    pairs = [(j, (j + 1) % chips) for j in range(chips)]
+    cur = lax.dynamic_index_in_dim(mine, (chip - 1) % chips, axis=0, keepdims=False)
+    cur_sq = lax.dynamic_index_in_dim(mine_sq, (chip - 1) % chips, axis=0, keepdims=False)
+    for k in range(chips - 1):
+        recv, recv_sq = unpack(lax.ppermute(pack(cur, cur_sq), "fy", perm=pairs), lanes)
+        index = (chip - k - 2) % chips
+        cur = recv + lax.dynamic_index_in_dim(mine, index, axis=0, keepdims=False)
+        cur_sq = recv_sq + lax.dynamic_index_in_dim(mine_sq, index, axis=0, keepdims=False)
+    return cur, cur_sq
+
+
 def per_device(query_act, key_act, value_act, gate_act, rate_index, norm_gain, out_weight):
     tok_count = query_act.shape[0]
     heads_here = rate_index.shape[0]
@@ -71,14 +107,10 @@
     gated = attended * gain_table[None] * jax.nn.sigmoid(gate_rows.astype(jnp.float32))
     gated = gated.reshape(tok_count, -1).astype(jnp.bfloat16)
     projected = jnp.dot(gated, out_weight, preferred_element_type=jnp.float32).astype(jnp.bfloat16)
-    lanes = projected.shape[1]
-    cores = lax.axis_size("fc")
-    chips = lax.axis_size("fy")
-    projected = projected.reshape(chips, cores, tok_count // (chips * cores), lanes)
-    projected = projected.transpose(1, 0, 2, 3).reshape(tok_count, lanes)
-    summed = lax.psum_scatter(projected, "fc", scatter_dimension=0, tiled=True)
-    summed = lax.psum_scatter(summed, "fy", scatter_dimension=0, tiled=True)
-    square_sum = lax.psum_scatter(local_squares, ("fy", "fc"), scatter_dimension=0, tiled=True)
+    owned = tok_count // 16
+    summed, square_sum = fsdp_reduce(
+        projected.reshape(-1, 2, owned, projected.shape[1]), local_squares.reshape(-1, 2, owned)
+    )
     inv_rms = lax.rsqrt(square_sum / (HEADS * HEAD_DIM) + 1e-06)
     return (summed.astype(jnp.float32) * inv_rms[:, None]).astype(jnp.bfloat16)
 

time: 196 us -> 204 us (1.041)
  the two profiles are of different devices: /device:TPU:1 before, /device:TPU:256 now
where the time goes in v5:
time: 204 us; the launch traced here: 203 us
  waiting for transfers between devices  112 us (55%)
  starting transfers between devices  53.5 us (26%)
  other arithmetic  17.3 us (8%)
  local copies, waits for them, and re-layouts  12.2 us (6%)
  matrix products  7.65 us (4%)
    ppermute x6, waiting for transfers between devices, decayed_scan(): lax.ppermute(total, axis, perm=[(i, i + shift) for i in range(peers - shi...  58 us
    ppermute x7, waiting for transfers between devices, fsdp_reduce(): lax.ppermute(pack(cur, cur_sq), 'fy', perm=pairs)  50.1 us
    ppermute x6, starting transfers between devices, decayed_scan(): lax.ppermute(total, axis, perm=[(i, i + shift) for i in range(peers - shi...  36.6 us
    ppermute x7, starting transfers between devices, fsdp_reduce(): lax.ppermute(pack(cur, cur_sq), 'fy', perm=pairs)  15.1 us
    convert_element_type x6, other arithmetic, pack(): return jnp.concatenate([values.astype(jnp.bfloat16), extra], axis=-1)  6.27 us
    dot_general x1, matrix products, per_device(): jnp.dot(gated, out_weight, preferred_element_type=jnp.float32)  4.71 us
    concatenate x8, local copies, waits for them, and re-layouts, pack(): return jnp.concatenate([values.astype(jnp.bfloat16), extra], axis=-1)  4.34 us
    convert_element_type x8, other arithmetic, pack(): lo = (squares - hi.astype(jnp.float32)).astype(jnp.bfloat16)  4.2 us
  transfers between devices with their start and end apart: 14, of which 14 were waited for; matrix products, arithmetic and copies ran while one was open for 1% of the time, Pallas kernels for 0%

profile of v5, /device:TPU:256, one launch (start us, length us, event | category | flops | bytes accessed | tf_op | source)
XLA Modules:
  0.0 203.1 jit_solution(16426866719661508171)
XLA Ops:
  3.1 3.5 %collective-permute-start = (f32[4,128,128]{2,1,0:T(8,128)S(1)}, f32[4,128,128]{2,1,0:T(8,128)S(1)}, u32[]{:S(2)}, u32[]{:S(2)}) collective-permute-start(f32[4,128,128]{2,1,0:T(8,128)S(1)} %fusion.18), channel_id=1, source_target_pairs={{0,16},{16,32},{32,48},{48,64},{64,80},{80,96},{96,112},{112,128},... | collective-permute-start | bytes 786440 | tf_op jit(solution)/shard_map/ppermute | solution.py:47
  6.7 8.6 %collective-permute-done = f32[4,128,128]{2,1,0:T(8,128)S(1)} collective-permute-done((f32[4,128,128]{2,1,0:T(8,128)S(1)}, f32[4,128,128]{2,1,0:T(8,128)S(1)}, u32[]{:S(2)}, u32[]{:S(2)}) %collective-permute-start) | collective-permute-done | bytes 262176 | tf_op jit(solution)/shard_map/ppermute | solution.py:47
  15.4 2.2 %collective-permute-start.1 = (f32[4,128,128]{2,1,0:T(8,128)S(1)}, f32[4,128,128]{2,1,0:T(8,128)S(1)}, u32[]{:S(2)}, u32[]{:S(2)}) collective-permute-start(f32[4,128,128]{2,1,0:T(8,128)S(1)} %multiply_add_fusion.4), channel_id=1, source_target_pairs={{0,32},{16,48},{32,64},{48,80},{64,96},{80,112},{96,128},{112,144}... | collective-permute-start | bytes 786440 | tf_op jit(solution)/shard_map/ppermute | solution.py:47
  17.6 13.6 %collective-permute-done.1 = f32[4,128,128]{2,1,0:T(8,128)S(1)} collective-permute-done((f32[4,128,128]{2,1,0:T(8,128)S(1)}, f32[4,128,128]{2,1,0:T(8,128)S(1)}, u32[]{:S(2)}, u32[]{:S(2)}) %collective-permute-start.1) | collective-permute-done | bytes 262176 | tf_op jit(solution)/shard_map/ppermute | solution.py:47
  31.3 7.4 %collective-permute-start.2 = (f32[4,128,128]{2,1,0:T(8,128)S(1)}, f32[4,128,128]{2,1,0:T(8,128)S(1)}, u32[]{:S(2)}, u32[]{:S(2)}) collective-permute-start(f32[4,128,128]{2,1,0:T(8,128)S(1)} %multiply_add_fusion.3), channel_id=1, source_target_pairs={{0,64},{16,80},{32,96},{48,112},{64,128},{80,144},{96,160},{112,17... | collective-permute-start | bytes 786440 | tf_op jit(solution)/shard_map/ppermute | solution.py:47
  38.7 11.0 %collective-permute-done.2 = f32[4,128,128]{2,1,0:T(8,128)S(1)} collective-permute-done((f32[4,128,128]{2,1,0:T(8,128)S(1)}, f32[4,128,128]{2,1,0:T(8,128)S(1)}, u32[]{:S(2)}, u32[]{:S(2)}) %collective-permute-start.2) | collective-permute-done | bytes 262176 | tf_op jit(solution)/shard_map/ppermute | solution.py:47
  49.8 5.1 %collective-permute-start.3 = (f32[4,128,128]{2,1,0:T(8,128)S(1)}, f32[4,128,128]{2,1,0:T(8,128)S(1)}, u32[]{:S(2)}, u32[]{:S(2)}) collective-permute-start(f32[4,128,128]{2,1,0:T(8,128)S(1)} %multiply_add_fusion.2), channel_id=1, source_target_pairs={{0,128},{16,144},{32,160},{48,176},{64,192},{80,208},{96,224},{112... | collective-permute-start | bytes 786440 | tf_op jit(solution)/shard_map/ppermute | solution.py:47
  55.2 5.5 %collective-permute-done.3 = f32[4,128,128]{2,1,0:T(8,128)S(1)} collective-permute-done((f32[4,128,128]{2,1,0:T(8,128)S(1)}, f32[4,128,128]{2,1,0:T(8,128)S(1)}, u32[]{:S(2)}, u32[]{:S(2)}) %collective-permute-start.3) | collective-permute-done | bytes 262176 | tf_op jit(solution)/shard_map/ppermute | solution.py:47
  60.8 9.1 %collective-permute-start.4 = (f32[4,128,128]{2,1,0:T(8,128)S(1)}, f32[4,128,128]{2,1,0:T(8,128)S(1)}, u32[]{:S(2)}, u32[]{:S(2)}) collective-permute-start(f32[4,128,128]{2,1,0:T(8,128)S(1)} %multiply_add_fusion.1), channel_id=1, source_target_pairs={{0,256},{16,272},{32,288},{48,304},{64,320},{80,336},{96,352},{112... | collective-permute-start | bytes 786440 | tf_op jit(solution)/shard_map/ppermute | solution.py:47
  70.3 10.0 %collective-permute-done.4 = f32[4,128,128]{2,1,0:T(8,128)S(1)} collective-permute-done((f32[4,128,128]{2,1,0:T(8,128)S(1)}, f32[4,128,128]{2,1,0:T(8,128)S(1)}, u32[]{:S(2)}, u32[]{:S(2)}) %collective-permute-start.4) | collective-permute-done | bytes 262176 | tf_op jit(solution)/shard_map/ppermute | solution.py:47
  80.4 9.2 %collective-permute-start.5 = (f32[4,128,128]{2,1,0:T(8,128)S(1)}, f32[4,128,128]{2,1,0:T(8,128)S(1)}, u32[]{:S(2)}, u32[]{:S(2)}) collective-permute-start(f32[4,128,128]{2,1,0:T(8,128)S(1)} %multiply_add_fusion), channel_id=1, source_target_pairs={{0,512},{16,528},{32,544},{48,560},{64,576},{80,592},{96,608},{112... | collective-permute-start | bytes 786440 | tf_op jit(solution)/shard_map/ppermute | solution.py:47
  90.1 9.3 %collective-permute-done.5 = f32[4,128,128]{2,1,0:T(8,128)S(1)} collective-permute-done((f32[4,128,128]{2,1,0:T(8,128)S(1)}, f32[4,128,128]{2,1,0:T(8,128)S(1)}, u32[]{:S(2)}, u32[]{:S(2)}) %collective-permute-start.5) | collective-permute-done | bytes 262176 | tf_op jit(solution)/shard_map/ppermute | solution.py:47
  100.7 4.7 %convolution_convert_fusion = bf16[256,6144]{1,0:T(8,128)(2,1)S(1)} fusion(bf16[256,512]{0,1:T(8,128)(2,1)} %bitcast.136, bf16[512,6144]{1,0:T(8,128)(2,1)} %param.13), kind=kOutput, calls=%fused_computation | convolution fusion | flops 1612185600 | bytes 9699328 | tf_op jit(solution)/shard_map/dot_general | solution.py:109
  107.0 3.7 %concatenate.24 = bf16[8,16,6272]{2,1,0:T(8,128)(2,1)} concatenate(bf16[8,16,6144]{2,1,0:T(8,128)(2,1)} %dynamic-slice_bitcast_fusion, bf16[8,16,1]{2,1,0:T(8,128)(2,1)S(1)} %copy.84, bf16[8,16,1]{2,1,0:T(8,128)(2,1)S(1)} %copy.85, bf16[8,16,126]{2,1,0:T(8,128)(2,1)S(1)} %broadcast_in_dim.16), dimensions={2} | concatenate | bytes 3211264 | tf_op jit(solution)/shard_map/concatenate | solution.py:59
  110.7 1.9 collective-permute-start.6
  112.6 3.7 %collective-permute-done.6 = bf16[8,16,6272]{2,1,0:T(8,128)(2,1)} collective-permute-done((bf16[8,16,6272]{2,1,0:T(8,128)(2,1)}, bf16[8,16,6272]{2,1,0:T(8,128)(2,1)}, u32[]{:S(2)}, u32[]{:S(2)}) %collective-permute-start.6) | collective-permute-done | bytes 1605664 | tf_op jit(solution)/shard_map/ppermute | solution.py:76
  117.4 1.8 convert_add_fusion
  121.2 3.6 %collective-permute-start.7 = (bf16[16,6272]{1,0:T(8,128)(2,1)S(1)}, bf16[16,6272]{1,0:T(8,128)(2,1)S(1)}, u32[]{:S(2)}, u32[]{:S(2)}) collective-permute-start(bf16[16,6272]{1,0:T(8,128)(2,1)S(1)} %concatenate.25), channel_id=1, source_target_pairs={{0,2},{2,4},{4,6},{6,8},{8,10},{10,12},{12,14},{14,0},{1,3},{3,5},... | collective-permute-start | bytes 602120 | tf_op jit(solution)/shard_map/ppermute | solution.py:83
  124.8 8.1 %collective-permute-done.7 = bf16[16,6272]{1,0:T(8,128)(2,1)S(1)} collective-permute-done((bf16[16,6272]{1,0:T(8,128)(2,1)S(1)}, bf16[16,6272]{1,0:T(8,128)(2,1)S(1)}, u32[]{:S(2)}, u32[]{:S(2)}) %collective-permute-start.7) | collective-permute-done | bytes 200736 | tf_op jit(solution)/shard_map/ppermute | solution.py:83
  135.2 1.9 collective-permute-start.8
  137.1 7.7 %collective-permute-done.8 = bf16[16,6272]{1,0:T(8,128)(2,1)S(1)} collective-permute-done((bf16[16,6272]{1,0:T(8,128)(2,1)S(1)}, bf16[16,6272]{1,0:T(8,128)(2,1)S(1)}, u32[]{:S(2)}, u32[]{:S(2)}) %collective-permute-start.8) | collective-permute-done | bytes 200736 | tf_op jit(solution)/shard_map/ppermute | solution.py:83
  147.1 1.9 collective-permute-start.9
  149.1 6.9 %collective-permute-done.9 = bf16[16,6272]{1,0:T(8,128)(2,1)S(1)} collective-permute-done((bf16[16,6272]{1,0:T(8,128)(2,1)S(1)}, bf16[16,6272]{1,0:T(8,128)(2,1)S(1)}, u32[]{:S(2)}, u32[]{:S(2)}) %collective-permute-start.9) | collective-permute-done | bytes 200736 | tf_op jit(solution)/shard_map/ppermute | solution.py:83
  158.2 1.9 collective-permute-start.10
  160.2 6.9 %collective-permute-done.10 = bf16[16,6272]{1,0:T(8,128)(2,1)S(1)} collective-permute-done((bf16[16,6272]{1,0:T(8,128)(2,1)S(1)}, bf16[16,6272]{1,0:T(8,128)(2,1)S(1)}, u32[]{:S(2)}, u32[]{:S(2)}) %collective-permute-start.10) | collective-permute-done | bytes 200736 | tf_op jit(solution)/shard_map/ppermute | solution.py:83
  169.3 1.9 collective-permute-start.11
  171.3 6.9 %collective-permute-done.11 = bf16[16,6272]{1,0:T(8,128)(2,1)S(1)} collective-permute-done((bf16[16,6272]{1,0:T(8,128)(2,1)S(1)}, bf16[16,6272]{1,0:T(8,128)(2,1)S(1)}, u32[]{:S(2)}, u32[]{:S(2)}) %collective-permute-start.11) | collective-permute-done | bytes 200736 | tf_op jit(solution)/shard_map/ppermute | solution.py:83
  180.4 1.9 collective-permute-start.12
  182.4 6.9 %collective-permute-done.12 = bf16[16,6272]{1,0:T(8,128)(2,1)S(1)} collective-permute-done((bf16[16,6272]{1,0:T(8,128)(2,1)S(1)}, bf16[16,6272]{1,0:T(8,128)(2,1)S(1)}, u32[]{:S(2)}, u32[]{:S(2)}) %collective-permute-start.12) | collective-permute-done | bytes 200736 | tf_op jit(solution)/shard_map/ppermute | solution.py:83
  191.5 1.9 collective-permute-start.13
  193.5 6.9 %collective-permute-done.13 = bf16[16,6272]{1,0:T(8,128)(2,1)S(1)} collective-permute-done((bf16[16,6272]{1,0:T(8,128)(2,1)S(1)}, bf16[16,6272]{1,0:T(8,128)(2,1)S(1)}, u32[]{:S(2)}, u32[]{:S(2)}) %collective-permute-start.13) | collective-permute-done | bytes 200736 | tf_op jit(solution)/shard_map/ppermute | solution.py:83
  201.3 1.8 fusion.11
  (98 shorter events, 25.2 us)
Async XLA Ops:
  0.0 89.6 %copy-start = (bf16[256,512]{1,0:T(8,128)(2,1)S(1)}, bf16[256,512]{1,0:T(8,128)(2,1)}, u32[]{:S(2)}) copy-start(bf16[256,512]{1,0:T(8,128)(2,1)} %param.7) | copy-start | bytes 786436
  0.0 55.0 %copy-start.2 = (bf16[256,512]{1,0:T(8,128)(2,1)S(1)}, bf16[256,512]{1,0:T(8,128)(2,1)}, u32[]{:S(2)}) copy-start(bf16[256,512]{1,0:T(8,128)(2,1)} %param.10) | copy-start | bytes 786436
  3.1 86.5 %copy-start.3 = (bf16[256,512]{1,0:T(8,128)(2,1)S(1)}, bf16[256,512]{1,0:T(8,128)(2,1)}, u32[]{:S(2)}) copy-start(bf16[256,512]{1,0:T(8,128)(2,1)} %param.9) | copy-start | bytes 786436
  3.1 12.2 %collective-permute-start = (f32[4,128,128]{2,1,0:T(8,128)S(1)}, f32[4,128,128]{2,1,0:T(8,128)S(1)}, u32[]{:S(2)}, u32[]{:S(2)}) collective-permute-start(f32[4,128,128]{2,1,0:T(8,128)S(1)} %fusion.18), channel_id=1, source_target_pairs={{0,16},{16,32},{32,48},{48,64},{64,80},{80,96},{96,112},{112,128},... | collective-permute-start | bytes 786440 | tf_op jit(solution)/shard_map/ppermute | solution.py:47
  15.4 15.8 %collective-permute-start.1 = (f32[4,128,128]{2,1,0:T(8,128)S(1)}, f32[4,128,128]{2,1,0:T(8,128)S(1)}, u32[]{:S(2)}, u32[]{:S(2)}) collective-permute-start(f32[4,128,128]{2,1,0:T(8,128)S(1)} %multiply_add_fusion.4), channel_id=1, source_target_pairs={{0,32},{16,48},{32,64},{48,80},{64,96},{80,112},{96,128},{112,144}... | collective-permute-start | bytes 786440 | tf_op jit(solution)/shard_map/ppermute | solution.py:47
  31.3 18.4 %collective-permute-start.2 = (f32[4,128,128]{2,1,0:T(8,128)S(1)}, f32[4,128,128]{2,1,0:T(8,128)S(1)}, u32[]{:S(2)}, u32[]{:S(2)}) collective-permute-start(f32[4,128,128]{2,1,0:T(8,128)S(1)} %multiply_add_fusion.3), channel_id=1, source_target_pairs={{0,64},{16,80},{32,96},{48,112},{64,128},{80,144},{96,160},{112,17... | collective-permute-start | bytes 786440 | tf_op jit(solution)/shard_map/ppermute | solution.py:47
  49.8 49.6 %copy-start.5 = (f32[512]{0:T(512)S(1)}, f32[512]{0:T(512)}, u32[]{:S(2)}) copy-start(f32[512]{0:T(512)} %param.12) | copy-start | bytes 6148
  49.8 10.9 %collective-permute-start.3 = (f32[4,128,128]{2,1,0:T(8,128)S(1)}, f32[4,128,128]{2,1,0:T(8,128)S(1)}, u32[]{:S(2)}, u32[]{:S(2)}) collective-permute-start(f32[4,128,128]{2,1,0:T(8,128)S(1)} %multiply_add_fusion.2), channel_id=1, source_target_pairs={{0,128},{16,144},{32,160},{48,176},{64,192},{80,208},{96,224},{112... | collective-permute-start | bytes 786440 | tf_op jit(solution)/shard_map/ppermute | solution.py:47
  60.8 19.5 %collective-permute-start.4 = (f32[4,128,128]{2,1,0:T(8,128)S(1)}, f32[4,128,128]{2,1,0:T(8,128)S(1)}, u32[]{:S(2)}, u32[]{:S(2)}) collective-permute-start(f32[4,128,128]{2,1,0:T(8,128)S(1)} %multiply_add_fusion.1), channel_id=1, source_target_pairs={{0,256},{16,272},{32,288},{48,304},{64,320},{80,336},{96,352},{112... | collective-permute-start | bytes 786440 | tf_op jit(solution)/shard_map/ppermute | solution.py:47
  80.4 19.0 %collective-permute-start.5 = (f32[4,128,128]{2,1,0:T(8,128)S(1)}, f32[4,128,128]{2,1,0:T(8,128)S(1)}, u32[]{:S(2)}, u32[]{:S(2)}) collective-permute-start(f32[4,128,128]{2,1,0:T(8,128)S(1)} %multiply_add_fusion), channel_id=1, source_target_pairs={{0,512},{16,528},{32,544},{48,560},{64,576},{80,592},{96,608},{112... | collective-permute-start | bytes 786440 | tf_op jit(solution)/shard_map/ppermute | solution.py:47
  110.7 5.7 %collective-permute-start.6 = (bf16[8,16,6272]{2,1,0:T(8,128)(2,1)}, bf16[8,16,6272]{2,1,0:T(8,128)(2,1)}, u32[]{:S(2)}, u32[]{:S(2)}) collective-permute-start(bf16[8,16,6272]{2,1,0:T(8,128)(2,1)} %concatenate.24), channel_id=1, source_target_pairs={{0,1},{1,0},{2,3},{3,2},{4,5},{5,4},{6,7},{7,6},{8,9},{9,8},{10,11... | collective-permute-start | bytes 4816904 | tf_op jit(solution)/shard_map/ppermute | solution.py:76
  117.4 1.8 copy-start.4
  119.2 1.6 copy-start.1
  121.2 11.7 %collective-permute-start.7 = (bf16[16,6272]{1,0:T(8,128)(2,1)S(1)}, bf16[16,6272]{1,0:T(8,128)(2,1)S(1)}, u32[]{:S(2)}, u32[]{:S(2)}) collective-permute-start(bf16[16,6272]{1,0:T(8,128)(2,1)S(1)} %concatenate.25), channel_id=1, source_target_pairs={{0,2},{2,4},{4,6},{6,8},{8,10},{10,12},{12,14},{14,0},{1,3},{3,5},... | collective-permute-start | bytes 602120 | tf_op jit(solution)/shard_map/ppermute | solution.py:83
  135.2 9.6 %collective-permute-start.8 = (bf16[16,6272]{1,0:T(8,128)(2,1)S(1)}, bf16[16,6272]{1,0:T(8,128)(2,1)S(1)}, u32[]{:S(2)}, u32[]{:S(2)}) collective-permute-start(bf16[16,6272]{1,0:T(8,128)(2,1)S(1)} %concatenate.26), channel_id=1, source_target_pairs={{0,2},{2,4},{4,6},{6,8},{8,10},{10,12},{12,14},{14,0},{1,3},{3,5},... | collective-permute-start | bytes 602120 | tf_op jit(solution)/shard_map/ppermute | solution.py:83
  147.1 8.8 %collective-permute-start.9 = (bf16[16,6272]{1,0:T(8,128)(2,1)S(1)}, bf16[16,6272]{1,0:T(8,128)(2,1)S(1)}, u32[]{:S(2)}, u32[]{:S(2)}) collective-permute-start(bf16[16,6272]{1,0:T(8,128)(2,1)S(1)} %concatenate.27), channel_id=1, source_target_pairs={{0,2},{2,4},{4,6},{6,8},{8,10},{10,12},{12,14},{14,0},{1,3},{3,5},... | collective-permute-start | bytes 602120 | tf_op jit(solution)/shard_map/ppermute | solution.py:83
  158.2 8.8 %collective-permute-start.10 = (bf16[16,6272]{1,0:T(8,128)(2,1)S(1)}, bf16[16,6272]{1,0:T(8,128)(2,1)S(1)}, u32[]{:S(2)}, u32[]{:S(2)}) collective-permute-start(bf16[16,6272]{1,0:T(8,128)(2,1)S(1)} %concatenate.28), channel_id=1, source_target_pairs={{0,2},{2,4},{4,6},{6,8},{8,10},{10,12},{12,14},{14,0},{1,3},{3,5},... | collective-permute-start | bytes 602120 | tf_op jit(solution)/shard_map/ppermute | solution.py:83
  169.3 8.8 %collective-permute-start.11 = (bf16[16,6272]{1,0:T(8,128)(2,1)S(1)}, bf16[16,6272]{1,0:T(8,128)(2,1)S(1)}, u32[]{:S(2)}, u32[]{:S(2)}) collective-permute-start(bf16[16,6272]{1,0:T(8,128)(2,1)S(1)} %concatenate.29), channel_id=1, source_target_pairs={{0,2},{2,4},{4,6},{6,8},{8,10},{10,12},{12,14},{14,0},{1,3},{3,5},... | collective-permute-start | bytes 602120 | tf_op jit(solution)/shard_map/ppermute | solution.py:83
  180.4 8.8 %collective-permute-start.12 = (bf16[16,6272]{1,0:T(8,128)(2,1)S(1)}, bf16[16,6272]{1,0:T(8,128)(2,1)S(1)}, u32[]{:S(2)}, u32[]{:S(2)}) collective-permute-start(bf16[16,6272]{1,0:T(8,128)(2,1)S(1)} %concatenate.30), channel_id=1, source_target_pairs={{0,2},{2,4},{4,6},{6,8},{8,10},{10,12},{12,14},{14,0},{1,3},{3,5},... | collective-permute-start | bytes 602120 | tf_op jit(solution)/shard_map/ppermute | solution.py:83
  191.5 8.8 %collective-permute-start.13 = (bf16[16,6272]{1,0:T(8,128)(2,1)S(1)}, bf16[16,6272]{1,0:T(8,128)(2,1)S(1)}, u32[]{:S(2)}, u32[]{:S(2)}) collective-permute-start(bf16[16,6272]{1,0:T(8,128)(2,1)S(1)} %concatenate.31), channel_id=1, source_target_pairs={{0,2},{2,4},{4,6},{6,8},{8,10},{10,12},{12,14},{14,0},{1,3},{3,5},... | collective-permute-start | bytes 602120 | tf_op jit(solution)/shard_map/ppermute | solution.py:83

commit v6 on v5

--- a/solution.py
+++ b/solution.py
@@ -65,9 +65,7 @@
 
 
 def fsdp_reduce(parts, squares):
-    chips = lax.axis_size("fy")
     core = lax.axis_index("fc")
-    chip = lax.axis_index("fy")
     lanes = parts.shape[-1]
     keep = lax.dynamic_index_in_dim(parts, core, axis=1, keepdims=False)
     keep_sq = lax.dynamic_index_in_dim(squares, core, axis=1, keepdims=False)
@@ -76,14 +74,10 @@
     got, got_sq = unpack(lax.ppermute(pack(give, give_sq), "fc", perm=[(0, 1), (1, 0)]), lanes)
     mine = keep.astype(jnp.float32) + got
     mine_sq = keep_sq + got_sq
-    pairs = [(j, (j + 1) % chips) for j in range(chips)]
-    cur = lax.dynamic_index_in_dim(mine, (chip - 1) % chips, axis=0, keepdims=False)
-    cur_sq = lax.dynamic_index_in_dim(mine_sq, (chip - 1) % chips, axis=0, keepdims=False)
-    for k in range(chips - 1):
-        recv, recv_sq = unpack(lax.ppermute(pack(cur, cur_sq), "fy", perm=pairs), lanes)
-        index = (chip - k - 2) % chips
-        cur = recv + lax.dynamic_index_in_dim(mine, index, axis=0, keepdims=False)
-        cur_sq = recv_sq + lax.dynamic_index_in_dim(mine_sq, index, axis=0, keepdims=False)
+    moved = lax.all_to_all(pack(mine, mine_sq), "fy", 0, 0, tiled=True)
+    values, sums = unpack(moved, lanes)
+    cur = jnp.sum(values, axis=0)
+    cur_sq = jnp.sum(sums, axis=0)
     return cur, cur_sq
 
 

time: 204 us -> 173 us (0.85)
  the two profiles are of different devices: /device:TPU:256 before, /device:TPU:1 now
where the time goes in v6:
time: 173 us; the launch traced here: 171 us
  starting transfers between devices  65.7 us (38%)
  blocking collectives  47.3 us (27%)
  waiting for transfers between devices  33.4 us (19%)
  local copies, waits for them, and re-layouts  10.8 us (6%)
  matrix products  7.66 us (4%)
  other arithmetic  5.76 us (3%)
    ppermute x6, starting transfers between devices, decayed_scan(): lax.ppermute(total, axis, perm=[(i, i + shift) for i in range(peers - shi...  61.7 us
    all_to_all x1, blocking collectives, fsdp_reduce(): moved = lax.all_to_all(pack(mine, mine_sq), 'fy', 0, 0, tiled=True)  47.3 us
    ppermute x6, waiting for transfers between devices, decayed_scan(): lax.ppermute(total, axis, perm=[(i, i + shift) for i in range(peers - shi...  30.1 us
    concatenate x2, local copies, waits for them, and re-layouts, pack(): return jnp.concatenate([values.astype(jnp.bfloat16), extra], axis=-1)  6.02 us
    dot_general x1, matrix products, per_device(): jnp.dot(gated, out_weight, preferred_element_type=jnp.float32)  4.7 us
    ppermute x1, starting transfers between devices, fsdp_reduce(): lax.ppermute(pack(give, give_sq), 'fc', perm=[(0, 1), (1, 0)])  4.02 us
  transfers between devices with their start and end apart: 7, of which 7 were waited for; matrix products, arithmetic and copies ran while one was open for 1% of the time, Pallas kernels for 0%

profile of v6, /device:TPU:1, one launch (start us, length us, event | category | flops | bytes accessed | tf_op | source)
XLA Modules:
  0.0 170.8 jit_solution(9895827022332948629)
XLA Ops:
  0.0 0.7 multiply_exponential_fusion.3
  0.7 1.1 copy.63
  1.9 1.2 fusion.11
  3.1 4.0 %collective-permute-start = (f32[4,128,128]{2,1,0:T(8,128)S(1)}, f32[4,128,128]{2,1,0:T(8,128)S(1)}, u32[]{:S(2)}, u32[]{:S(2)}) collective-permute-start(f32[4,128,128]{2,1,0:T(8,128)S(1)} %fusion.11), channel_id=1, source_target_pairs={{0,16},{16,32},{32,48},{48,64},{64,80},{80,96},{96,112},{112,128},... | collective-permute-start | bytes 786440 | tf_op jit(solution)/shard_map/ppermute | solution.py:47
  7.1 3.9 %collective-permute-done = f32[4,128,128]{2,1,0:T(8,128)S(1)} collective-permute-done((f32[4,128,128]{2,1,0:T(8,128)S(1)}, f32[4,128,128]{2,1,0:T(8,128)S(1)}, u32[]{:S(2)}, u32[]{:S(2)}) %collective-permute-start) | collective-permute-done | bytes 262176 | tf_op jit(solution)/shard_map/ppermute | solution.py:47
  11.0 7.0 %collective-permute-start.1 = (f32[4,128,128]{2,1,0:T(8,128)S(1)}, f32[4,128,128]{2,1,0:T(8,128)S(1)}, u32[]{:S(2)}, u32[]{:S(2)}) collective-permute-start(f32[4,128,128]{2,1,0:T(8,128)S(1)} %multiply_add_fusion.4), channel_id=1, source_target_pairs={{0,32},{16,48},{32,64},{48,80},{64,96},{80,112},{96,128},{112,144}... | collective-permute-start | bytes 786440 | tf_op jit(solution)/shard_map/ppermute | solution.py:47
  18.1 11.1 %collective-permute-done.1 = f32[4,128,128]{2,1,0:T(8,128)S(1)} collective-permute-done((f32[4,128,128]{2,1,0:T(8,128)S(1)}, f32[4,128,128]{2,1,0:T(8,128)S(1)}, u32[]{:S(2)}, u32[]{:S(2)}) %collective-permute-start.1) | collective-permute-done | bytes 262176 | tf_op jit(solution)/shard_map/ppermute | solution.py:47
  29.3 6.0 %collective-permute-start.2 = (f32[4,128,128]{2,1,0:T(8,128)S(1)}, f32[4,128,128]{2,1,0:T(8,128)S(1)}, u32[]{:S(2)}, u32[]{:S(2)}) collective-permute-start(f32[4,128,128]{2,1,0:T(8,128)S(1)} %multiply_add_fusion.3), channel_id=1, source_target_pairs={{0,64},{16,80},{32,96},{48,112},{64,128},{80,144},{96,160},{112,17... | collective-permute-start | bytes 786440 | tf_op jit(solution)/shard_map/ppermute | solution.py:47
  35.3 4.4 %collective-permute-done.2 = f32[4,128,128]{2,1,0:T(8,128)S(1)} collective-permute-done((f32[4,128,128]{2,1,0:T(8,128)S(1)}, f32[4,128,128]{2,1,0:T(8,128)S(1)}, u32[]{:S(2)}, u32[]{:S(2)}) %collective-permute-start.2) | collective-permute-done | bytes 262176 | tf_op jit(solution)/shard_map/ppermute | solution.py:47
  39.8 13.4 %collective-permute-start.3 = (f32[4,128,128]{2,1,0:T(8,128)S(1)}, f32[4,128,128]{2,1,0:T(8,128)S(1)}, u32[]{:S(2)}, u32[]{:S(2)}) collective-permute-start(f32[4,128,128]{2,1,0:T(8,128)S(1)} %multiply_add_fusion.2), channel_id=1, source_target_pairs={{0,128},{16,144},{32,160},{48,176},{64,192},{80,208},{96,224},{112... | collective-permute-start | bytes 786440 | tf_op jit(solution)/shard_map/ppermute | solution.py:47
  53.3 0.1 add_divide_fusion
  53.4 3.1 %collective-permute-done.3 = f32[4,128,128]{2,1,0:T(8,128)S(1)} collective-permute-done((f32[4,128,128]{2,1,0:T(8,128)S(1)}, f32[4,128,128]{2,1,0:T(8,128)S(1)}, u32[]{:S(2)}, u32[]{:S(2)}) %collective-permute-start.3) | collective-permute-done | bytes 262176 | tf_op jit(solution)/shard_map/ppermute | solution.py:47
  56.6 11.8 %collective-permute-start.4 = (f32[4,128,128]{2,1,0:T(8,128)S(1)}, f32[4,128,128]{2,1,0:T(8,128)S(1)}, u32[]{:S(2)}, u32[]{:S(2)}) collective-permute-start(f32[4,128,128]{2,1,0:T(8,128)S(1)} %multiply_add_fusion.1), channel_id=1, source_target_pairs={{0,256},{16,272},{32,288},{48,304},{64,320},{80,336},{96,352},{112... | collective-permute-start | bytes 786440 | tf_op jit(solution)/shard_map/ppermute | solution.py:47
  68.6 0.2 copy.48
  68.9 3.8 %collective-permute-done.4 = f32[4,128,128]{2,1,0:T(8,128)S(1)} collective-permute-done((f32[4,128,128]{2,1,0:T(8,128)S(1)}, f32[4,128,128]{2,1,0:T(8,128)S(1)}, u32[]{:S(2)}, u32[]{:S(2)}) %collective-permute-start.4) | collective-permute-done | bytes 262176 | tf_op jit(solution)/shard_map/ppermute | solution.py:47
  72.8 19.4 %collective-permute-start.5 = (f32[4,128,128]{2,1,0:T(8,128)S(1)}, f32[4,128,128]{2,1,0:T(8,128)S(1)}, u32[]{:S(2)}, u32[]{:S(2)}) collective-permute-start(f32[4,128,128]{2,1,0:T(8,128)S(1)} %multiply_add_fusion), channel_id=1, source_target_pairs={{0,512},{16,528},{32,544},{48,560},{64,576},{80,592},{96,608},{112... | collective-permute-start | bytes 786440 | tf_op jit(solution)/shard_map/ppermute | solution.py:47
  92.3 0.5 convolution_bitcast_fusion.1
  92.8 3.8 %collective-permute-done.5 = f32[4,128,128]{2,1,0:T(8,128)S(1)} collective-permute-done((f32[4,128,128]{2,1,0:T(8,128)S(1)}, f32[4,128,128]{2,1,0:T(8,128)S(1)}, u32[]{:S(2)}, u32[]{:S(2)}) %collective-permute-start.5) | collective-permute-done | bytes 262176 | tf_op jit(solution)/shard_map/ppermute | solution.py:47
  96.6 1.3 multiply_reduce_fusion
  98.0 0.1 copy.51
  98.3 4.7 %convolution_convert_fusion = bf16[256,6144]{1,0:T(8,128)(2,1)S(1)} fusion(bf16[256,512]{0,1:T(8,128)(2,1)} %bitcast.56, bf16[512,6144]{1,0:T(8,128)(2,1)} %param.13), kind=kOutput, calls=%fused_computation | convolution fusion | flops 1612185600 | bytes 9699328 | tf_op jit(solution)/shard_map/dot_general | solution.py:103
  103.0 1.3 dynamic-slice_bitcast_fusion
  104.3 3.7 %concatenate.6 = bf16[8,16,6272]{2,1,0:T(8,128)(2,1)} concatenate(bf16[8,16,6144]{2,1,0:T(8,128)(2,1)} %dynamic-slice_bitcast_fusion, bf16[8,16,1]{2,1,0:T(8,128)(2,1)S(1)} %copy.50, bf16[8,16,1]{2,1,0:T(8,128)(2,1)S(1)} %copy.51, bf16[8,16,126]{2,1,0:T(8,128)(2,1)S(1)} %broadcast.161), dimensions={2} | concatenate | bytes 3211264 | tf_op jit(solution)/shard_map/concatenate | solution.py:59
  108.0 4.0 %collective-permute-start.6 = (bf16[8,16,6272]{2,1,0:T(8,128)(2,1)}, bf16[8,16,6272]{2,1,0:T(8,128)(2,1)S(1)}, u32[]{:S(2)}, u32[]{:S(2)}) collective-permute-start(bf16[8,16,6272]{2,1,0:T(8,128)(2,1)} %concatenate.6), channel_id=1, source_target_pairs={{0,1},{1,0},{2,3},{3,2},{4,5},{5,4},{6,7},{7,6},{8,9},{9,8},{10,11... | collective-permute-start | bytes 4816904 | tf_op jit(solution)/shard_map/ppermute | solution.py:74
  112.0 3.3 %collective-permute-done.6 = bf16[8,16,6272]{2,1,0:T(8,128)(2,1)S(1)} collective-permute-done((bf16[8,16,6272]{2,1,0:T(8,128)(2,1)}, bf16[8,16,6272]{2,1,0:T(8,128)(2,1)S(1)}, u32[]{:S(2)}, u32[]{:S(2)}) %collective-permute-start.6) | collective-permute-done | bytes 1605664 | tf_op jit(solution)/shard_map/ppermute | solution.py:74
  115.3 1.2 copy-done.1
  117.1 2.9 %fusion = bf16[8,16,6144]{2,1,0:T(8,128)(2,1)} fusion(bf16[8,16,6272]{2,1,0:T(8,128)(2,1)} %copy-done.1, bf16[8,2,16,6144]{3,2,1,0:T(8,128)(2,1)S(1)} %bitcast.54, s32[]{:T(128)S(6)} %select_n.15), kind=kLoop, calls=%fused_computation.2 | loop fusion | flops 3145728 | bytes 4718596 | tf_op jit(solution)/shard_map/convert_element_type | solution.py:59
  120.0 2.3 %concatenate.7 = bf16[8,16,6272]{2,1,0:T(8,128)(2,1)S(1)} concatenate(bf16[8,16,6144]{2,1,0:T(8,128)(2,1)} %fusion, bf16[8,16,1]{2,1,0:T(8,128)(2,1)S(1)} %copy.54, bf16[8,16,1]{2,1,0:T(8,128)(2,1)S(1)} %copy.55, bf16[8,16,126]{2,1,0:T(8,128)(2,1)S(1)} %broadcast.161), dimensions={2} | concatenate | bytes 3211264 | tf_op jit(solution)/shard_map/concatenate | solution.py:59
  122.4 47.3 %all_to_all.5 = bf16[8,16,6272]{2,1,0:T(8,128)(2,1)S(1)} all-to-all(bf16[8,16,6272]{2,1,0:T(8,128)(2,1)S(1)} %concatenate.7), channel_id=1, replica_groups=mesh['sz'=8,'sx'=8,'fy'=8,'fc'=2] {'fy'}, dimensions={0} | all-to-all | bytes 3211264 | tf_op jit(solution)/shard_map/all_to_all | solution.py:77
  169.6 0.2 add_reduce_fusion
  169.8 0.2 convert_reduce_fusion
  170.0 0.8 multiply_convert_fusion.2
  (32 shorter events, 1.7 us)
Async XLA Ops:
  0.0 92.3 %copy-start = (bf16[256,512]{1,0:T(8,128)(2,1)S(1)}, bf16[256,512]{1,0:T(8,128)(2,1)}, u32[]{:S(2)}) copy-start(bf16[256,512]{1,0:T(8,128)(2,1)} %param.7) | copy-start | bytes 786436
  1.8 51.4 %copy-start.2 = (bf16[256,512]{1,0:T(8,128)(2,1)S(1)}, bf16[256,512]{1,0:T(8,128)(2,1)}, u32[]{:S(2)}) copy-start(bf16[256,512]{1,0:T(8,128)(2,1)} %param.10) | copy-start | bytes 786436
  3.1 7.9 %collective-permute-start = (f32[4,128,128]{2,1,0:T(8,128)S(1)}, f32[4,128,128]{2,1,0:T(8,128)S(1)}, u32[]{:S(2)}, u32[]{:S(2)}) collective-permute-start(f32[4,128,128]{2,1,0:T(8,128)S(1)} %fusion.11), channel_id=1, source_target_pairs={{0,16},{16,32},{32,48},{48,64},{64,80},{80,96},{96,112},{112,128},... | collective-permute-start | bytes 786440 | tf_op jit(solution)/shard_map/ppermute | solution.py:47
  11.0 18.2 %collective-permute-start.1 = (f32[4,128,128]{2,1,0:T(8,128)S(1)}, f32[4,128,128]{2,1,0:T(8,128)S(1)}, u32[]{:S(2)}, u32[]{:S(2)}) collective-permute-start(f32[4,128,128]{2,1,0:T(8,128)S(1)} %multiply_add_fusion.4), channel_id=1, source_target_pairs={{0,32},{16,48},{32,64},{48,80},{64,96},{80,112},{96,128},{112,144}... | collective-permute-start | bytes 786440 | tf_op jit(solution)/shard_map/ppermute | solution.py:47
  29.3 10.4 %collective-permute-start.2 = (f32[4,128,128]{2,1,0:T(8,128)S(1)}, f32[4,128,128]{2,1,0:T(8,128)S(1)}, u32[]{:S(2)}, u32[]{:S(2)}) collective-permute-start(f32[4,128,128]{2,1,0:T(8,128)S(1)} %multiply_add_fusion.3), channel_id=1, source_target_pairs={{0,64},{16,80},{32,96},{48,112},{64,128},{80,144},{96,160},{112,17... | collective-permute-start | bytes 786440 | tf_op jit(solution)/shard_map/ppermute | solution.py:47
  39.8 16.7 %collective-permute-start.3 = (f32[4,128,128]{2,1,0:T(8,128)S(1)}, f32[4,128,128]{2,1,0:T(8,128)S(1)}, u32[]{:S(2)}, u32[]{:S(2)}) collective-permute-start(f32[4,128,128]{2,1,0:T(8,128)S(1)} %multiply_add_fusion.2), channel_id=1, source_target_pairs={{0,128},{16,144},{32,160},{48,176},{64,192},{80,208},{96,224},{112... | collective-permute-start | bytes 786440 | tf_op jit(solution)/shard_map/ppermute | solution.py:47
  53.4 38.9 %copy-start.3 = (bf16[256,512]{1,0:T(8,128)(2,1)S(1)}, bf16[256,512]{1,0:T(8,128)(2,1)}, u32[]{:S(2)}) copy-start(bf16[256,512]{1,0:T(8,128)(2,1)} %param.9) | copy-start | bytes 786436
  56.6 16.1 %collective-permute-start.4 = (f32[4,128,128]{2,1,0:T(8,128)S(1)}, f32[4,128,128]{2,1,0:T(8,128)S(1)}, u32[]{:S(2)}, u32[]{:S(2)}) collective-permute-start(f32[4,128,128]{2,1,0:T(8,128)S(1)} %multiply_add_fusion.1), channel_id=1, source_target_pairs={{0,256},{16,272},{32,288},{48,304},{64,320},{80,336},{96,352},{112... | collective-permute-start | bytes 786440 | tf_op jit(solution)/shard_map/ppermute | solution.py:47
  72.7 23.9 %copy-start.4 = (f32[512]{0:T(512)S(1)}, f32[512]{0:T(512)}, u32[]{:S(2)}) copy-start(f32[512]{0:T(512)} %param.12) | copy-start | bytes 6148
  72.8 23.8 %collective-permute-start.5 = (f32[4,128,128]{2,1,0:T(8,128)S(1)}, f32[4,128,128]{2,1,0:T(8,128)S(1)}, u32[]{:S(2)}, u32[]{:S(2)}) collective-permute-start(f32[4,128,128]{2,1,0:T(8,128)S(1)} %multiply_add_fusion), channel_id=1, source_target_pairs={{0,512},{16,528},{32,544},{48,560},{64,576},{80,592},{96,608},{112... | collective-permute-start | bytes 786440 | tf_op jit(solution)/shard_map/ppermute | solution.py:47
  108.0 7.3 %collective-permute-start.6 = (bf16[8,16,6272]{2,1,0:T(8,128)(2,1)}, bf16[8,16,6272]{2,1,0:T(8,128)(2,1)S(1)}, u32[]{:S(2)}, u32[]{:S(2)}) collective-permute-start(bf16[8,16,6272]{2,1,0:T(8,128)(2,1)} %concatenate.6), channel_id=1, source_target_pairs={{0,1},{1,0},{2,3},{3,2},{4,5},{5,4},{6,7},{7,6},{8,9},{9,8},{10,11... | collective-permute-start | bytes 4816904 | tf_op jit(solution)/shard_map/ppermute | solution.py:74
  115.3 1.2 copy-start.1

commit v7 on v6

--- a/solution.py
+++ b/solution.py
@@ -41,14 +41,19 @@
 def decayed_scan(local_state, slopes, tok_count, axis):
     peers = lax.axis_size(axis)
     total = local_state
+    earlier = jnp.zeros_like(local_state)
     shift = 1
     while shift < peers:
         decay = jnp.exp(-slopes * (tok_count * shift))
-        moved = lax.ppermute(total, axis, perm=[(i, i + shift) for i in range(peers - shift)])
-        total = total + decay[:, None, None] * moved
+        moved = lax.ppermute(
+            total.astype(jnp.bfloat16), axis, perm=[(i, i + shift) for i in range(peers - shift)]
+        )
+        part = decay[:, None, None] * moved.astype(jnp.float32)
+        earlier = earlier + part
+        total = total + part
         shift *= 2
     undo = jnp.exp(slopes * tok_count)
-    return (total - local_state) * undo[:, None, None]
+    return earlier * undo[:, None, None]
 
 
 def pack(values, squares):

time: 173 us -> 149 us (0.86)
  waiting for transfers between devices: 33.4 us -> 13.9 us
  starting transfers between devices: 65.7 us -> 62.2 us
    ppermute x6, waiting for transfers between devices: 30.1 us -> 10.6 us  [decayed_scan(): lax.ppermute(total.astype(jnp.bfloat16), axis, perm=[(i, i + shift) for i...]
    ppermute x6, starting transfers between devices: 61.7 us -> 57.1 us  [decayed_scan(): lax.ppermute(total.astype(jnp.bfloat16), axis, perm=[(i, i + shift) for i...]
where the time goes in v7:
time: 149 us; the launch traced here: 148 us
  starting transfers between devices  62.2 us (42%)
  blocking collectives  47.3 us (32%)
  waiting for transfers between devices  13.9 us (9%)
  local copies, waits for them, and re-layouts  10.8 us (7%)
  matrix products  7.71 us (5%)
  other arithmetic  5.92 us (4%)
    ppermute x6, starting transfers between devices, decayed_scan(): lax.ppermute(total.astype(jnp.bfloat16), axis, perm=[(i, i + shift) for i...  57.1 us
    all_to_all x1, blocking collectives, fsdp_reduce(): moved = lax.all_to_all(pack(mine, mine_sq), 'fy', 0, 0, tiled=True)  47.3 us
    ppermute x6, waiting for transfers between devices, decayed_scan(): lax.ppermute(total.astype(jnp.bfloat16), axis, perm=[(i, i + shift) for i...  10.6 us
    concatenate x2, local copies, waits for them, and re-layouts, pack(): return jnp.concatenate([values.astype(jnp.bfloat16), extra], axis=-1)  6.02 us
    ppermute x1, starting transfers between devices, fsdp_reduce(): lax.ppermute(pack(give, give_sq), 'fc', perm=[(0, 1), (1, 0)])  5.04 us
    dot_general x1, matrix products, per_device(): jnp.dot(gated, out_weight, preferred_element_type=jnp.float32)  4.7 us
    ppermute x1, waiting for transfers between devices, fsdp_reduce(): lax.ppermute(pack(give, give_sq), 'fc', perm=[(0, 1), (1, 0)])  3.27 us
  transfers between devices with their start and end apart: 7, of which 7 were waited for; matrix products, arithmetic and copies ran while one was open for 1% of the time, Pallas kernels for 0%

profile of v7, /device:TPU:1, one launch (start us, length us, event | category | flops | bytes accessed | tf_op | source)
XLA Modules:
  0.0 148.0 jit_solution(15615159328507497909)
XLA Ops:
  0.0 0.7 multiply_exponential_fusion.3
  0.7 1.1 copy.63
  1.9 1.2 fusion.52
  3.1 4.1 %collective-permute-start = (bf16[4,128,128]{2,1,0:T(8,128)(2,1)S(1)}, bf16[4,128,128]{2,1,0:T(8,128)(2,1)S(1)}, u32[]{:S(2)}, u32[]{:S(2)}) collective-permute-start(bf16[4,128,128]{2,1,0:T(8,128)(2,1)S(1)} %get-tuple-element.27), channel_id=1, source_target_pairs={{0,16},{16,32},{32,48},{48,64},{64,80},{80,96},{96,112},{112,128},... | collective-permute-start | bytes 393224 | tf_op jit(solution)/shard_map/ppermute | solution.py:48
  7.2 2.2 %collective-permute-done = bf16[4,128,128]{2,1,0:T(8,128)(2,1)S(1)} collective-permute-done((bf16[4,128,128]{2,1,0:T(8,128)(2,1)S(1)}, bf16[4,128,128]{2,1,0:T(8,128)(2,1)S(1)}, u32[]{:S(2)}, u32[]{:S(2)}) %collective-permute-start) | collective-permute-done | bytes 131104 | tf_op jit(solution)/shard_map/ppermute | solution.py:48
  9.5 5.5 %collective-permute-start.1 = (bf16[4,128,128]{2,1,0:T(8,128)(2,1)S(1)}, bf16[4,128,128]{2,1,0:T(8,128)(2,1)S(1)}, u32[]{:S(2)}, u32[]{:S(2)}) collective-permute-start(bf16[4,128,128]{2,1,0:T(8,128)(2,1)S(1)} %fusion.35), channel_id=1, source_target_pairs={{0,32},{16,48},{32,64},{48,80},{64,96},{80,112},{96,128},{112,144}... | collective-permute-start | bytes 393224 | tf_op jit(solution)/shard_map/ppermute | solution.py:48
  15.0 1.9 %collective-permute-done.1 = bf16[4,128,128]{2,1,0:T(8,128)(2,1)S(1)} collective-permute-done((bf16[4,128,128]{2,1,0:T(8,128)(2,1)S(1)}, bf16[4,128,128]{2,1,0:T(8,128)(2,1)S(1)}, u32[]{:S(2)}, u32[]{:S(2)}) %collective-permute-start.1) | collective-permute-done | bytes 131104 | tf_op jit(solution)/shard_map/ppermute | solution.py:48
  17.0 10.4 %collective-permute-start.2 = (bf16[4,128,128]{2,1,0:T(8,128)(2,1)S(1)}, bf16[4,128,128]{2,1,0:T(8,128)(2,1)S(1)}, u32[]{:S(2)}, u32[]{:S(2)}) collective-permute-start(bf16[4,128,128]{2,1,0:T(8,128)(2,1)S(1)} %get-tuple-element.9), channel_id=1, source_target_pairs={{0,64},{16,80},{32,96},{48,112},{64,128},{80,144},{96,160},{112,17... | collective-permute-start | bytes 393224 | tf_op jit(solution)/shard_map/ppermute | solution.py:48
  27.6 1.8 %collective-permute-done.2 = bf16[4,128,128]{2,1,0:T(8,128)(2,1)S(1)} collective-permute-done((bf16[4,128,128]{2,1,0:T(8,128)(2,1)S(1)}, bf16[4,128,128]{2,1,0:T(8,128)(2,1)S(1)}, u32[]{:S(2)}, u32[]{:S(2)}) %collective-permute-start.2) | collective-permute-done | bytes 131104 | tf_op jit(solution)/shard_map/ppermute | solution.py:48
  29.5 8.8 %collective-permute-start.3 = (bf16[4,128,128]{2,1,0:T(8,128)(2,1)S(1)}, bf16[4,128,128]{2,1,0:T(8,128)(2,1)S(1)}, u32[]{:S(2)}, u32[]{:S(2)}) collective-permute-start(bf16[4,128,128]{2,1,0:T(8,128)(2,1)S(1)} %fusion.36), channel_id=1, source_target_pairs={{0,128},{16,144},{32,160},{48,176},{64,192},{80,208},{96,224},{112... | collective-permute-start | bytes 393224 | tf_op jit(solution)/shard_map/ppermute | solution.py:48
  38.4 1.8 %collective-permute-done.3 = bf16[4,128,128]{2,1,0:T(8,128)(2,1)S(1)} collective-permute-done((bf16[4,128,128]{2,1,0:T(8,128)(2,1)S(1)}, bf16[4,128,128]{2,1,0:T(8,128)(2,1)S(1)}, u32[]{:S(2)}, u32[]{:S(2)}) %collective-permute-start.3) | collective-permute-done | bytes 131104 | tf_op jit(solution)/shard_map/ppermute | solution.py:48
  40.4 10.2 %collective-permute-start.4 = (bf16[4,128,128]{2,1,0:T(8,128)(2,1)S(1)}, bf16[4,128,128]{2,1,0:T(8,128)(2,1)S(1)}, u32[]{:S(2)}, u32[]{:S(2)}) collective-permute-start(bf16[4,128,128]{2,1,0:T(8,128)(2,1)S(1)} %fusion.48), channel_id=1, source_target_pairs={{0,256},{16,272},{32,288},{48,304},{64,320},{80,336},{96,352},{112... | collective-permute-start | bytes 393224 | tf_op jit(solution)/shard_map/ppermute | solution.py:48
  50.6 0.5 convolution_bitcast_fusion.1
  51.2 1.4 collective-permute-done.4
  52.5 0.2 add_convert_fusion
  52.7 18.1 %collective-permute-start.5 = (bf16[4,128,128]{2,1,0:T(8,128)(2,1)S(1)}, bf16[4,128,128]{2,1,0:T(8,128)(2,1)S(1)}, u32[]{:S(2)}, u32[]{:S(2)}) collective-permute-start(bf16[4,128,128]{2,1,0:T(8,128)(2,1)S(1)} %add_convert_fusion), channel_id=1, source_target_pairs={{0,512},{16,528},{32,544},{48,560},{64,576},{80,592},{96,608},{112... | collective-permute-start | bytes 393224 | tf_op jit(solution)/shard_map/ppermute | solution.py:48
  70.8 0.1 add_divide_fusion
  71.0 0.2 copy.48
  71.2 1.6 %collective-permute-done.5 = bf16[4,128,128]{2,1,0:T(8,128)(2,1)S(1)} collective-permute-done((bf16[4,128,128]{2,1,0:T(8,128)(2,1)S(1)}, bf16[4,128,128]{2,1,0:T(8,128)(2,1)S(1)}, u32[]{:S(2)}, u32[]{:S(2)}) %collective-permute-start.5) | collective-permute-done | bytes 131104 | tf_op jit(solution)/shard_map/ppermute | solution.py:48
  72.7 1.3 multiply_reduce_fusion
  74.5 4.7 %convolution_convert_fusion = bf16[256,6144]{1,0:T(8,128)(2,1)S(1)} fusion(bf16[256,512]{0,1:T(8,128)(2,1)} %bitcast.58, bf16[512,6144]{1,0:T(8,128)(2,1)} %param.13), kind=kOutput, calls=%fused_computation | convolution fusion | flops 1612185600 | bytes 9699328 | tf_op jit(solution)/shard_map/dot_general | solution.py:108
  79.2 1.3 dynamic-slice_bitcast_fusion
  80.4 3.7 %concatenate.6 = bf16[8,16,6272]{2,1,0:T(8,128)(2,1)} concatenate(bf16[8,16,6144]{2,1,0:T(8,128)(2,1)} %dynamic-slice_bitcast_fusion, bf16[8,16,1]{2,1,0:T(8,128)(2,1)S(1)} %copy.50, bf16[8,16,1]{2,1,0:T(8,128)(2,1)S(1)} %copy.51, bf16[8,16,126]{2,1,0:T(8,128)(2,1)S(1)} %broadcast.161), dimensions={2} | concatenate | bytes 3211264 | tf_op jit(solution)/shard_map/concatenate | solution.py:64
  84.1 5.0 %collective-permute-start.6 = (bf16[8,16,6272]{2,1,0:T(8,128)(2,1)}, bf16[8,16,6272]{2,1,0:T(8,128)(2,1)S(1)}, u32[]{:S(2)}, u32[]{:S(2)}) collective-permute-start(bf16[8,16,6272]{2,1,0:T(8,128)(2,1)} %concatenate.6), channel_id=1, source_target_pairs={{0,1},{1,0},{2,3},{3,2},{4,5},{5,4},{6,7},{7,6},{8,9},{9,8},{10,11... | collective-permute-start | bytes 4816904 | tf_op jit(solution)/shard_map/ppermute | solution.py:79
  89.2 3.3 %collective-permute-done.6 = bf16[8,16,6272]{2,1,0:T(8,128)(2,1)S(1)} collective-permute-done((bf16[8,16,6272]{2,1,0:T(8,128)(2,1)}, bf16[8,16,6272]{2,1,0:T(8,128)(2,1)S(1)}, u32[]{:S(2)}, u32[]{:S(2)}) %collective-permute-start.6) | collective-permute-done | bytes 1605664 | tf_op jit(solution)/shard_map/ppermute | solution.py:79
  92.5 1.2 copy-done.1
  94.3 2.9 %fusion = bf16[8,16,6144]{2,1,0:T(8,128)(2,1)} fusion(bf16[8,16,6272]{2,1,0:T(8,128)(2,1)} %copy-done.1, bf16[8,2,16,6144]{3,2,1,0:T(8,128)(2,1)S(1)} %bitcast.56, s32[]{:T(128)S(6)} %select_n.15), kind=kLoop, calls=%fused_computation.2 | loop fusion | flops 3145728 | bytes 4718596 | tf_op jit(solution)/shard_map/convert_element_type | solution.py:64
  97.2 2.3 %concatenate.7 = bf16[8,16,6272]{2,1,0:T(8,128)(2,1)S(1)} concatenate(bf16[8,16,6144]{2,1,0:T(8,128)(2,1)} %fusion, bf16[8,16,1]{2,1,0:T(8,128)(2,1)S(1)} %copy.54, bf16[8,16,1]{2,1,0:T(8,128)(2,1)S(1)} %copy.55, bf16[8,16,126]{2,1,0:T(8,128)(2,1)S(1)} %broadcast.161), dimensions={2} | concatenate | bytes 3211264 | tf_op jit(solution)/shard_map/concatenate | solution.py:64
  99.5 47.3 %all_to_all.5 = bf16[8,16,6272]{2,1,0:T(8,128)(2,1)S(1)} all-to-all(bf16[8,16,6272]{2,1,0:T(8,128)(2,1)S(1)} %concatenate.7), channel_id=1, replica_groups=mesh['sz'=8,'sx'=8,'fy'=8,'fc'=2] {'fy'}, dimensions={0} | all-to-all | bytes 3211264 | tf_op jit(solution)/shard_map/all_to_all | solution.py:82
  146.8 0.2 add_reduce_fusion
  147.0 0.2 convert_reduce_fusion
  147.3 0.8 multiply_convert_fusion.2
  (32 shorter events, 1.8 us)
Async XLA Ops:
  0.0 50.6 %copy-start = (bf16[256,512]{1,0:T(8,128)(2,1)S(1)}, bf16[256,512]{1,0:T(8,128)(2,1)}, u32[]{:S(2)}) copy-start(bf16[256,512]{1,0:T(8,128)(2,1)} %param.7) | copy-start | bytes 786436
  3.1 47.5 %copy-start.2 = (bf16[256,512]{1,0:T(8,128)(2,1)S(1)}, bf16[256,512]{1,0:T(8,128)(2,1)}, u32[]{:S(2)}) copy-start(bf16[256,512]{1,0:T(8,128)(2,1)} %param.9) | copy-start | bytes 786436
  3.1 6.3 %collective-permute-start = (bf16[4,128,128]{2,1,0:T(8,128)(2,1)S(1)}, bf16[4,128,128]{2,1,0:T(8,128)(2,1)S(1)}, u32[]{:S(2)}, u32[]{:S(2)}) collective-permute-start(bf16[4,128,128]{2,1,0:T(8,128)(2,1)S(1)} %get-tuple-element.27), channel_id=1, source_target_pairs={{0,16},{16,32},{32,48},{48,64},{64,80},{80,96},{96,112},{112,128},... | collective-permute-start | bytes 393224 | tf_op jit(solution)/shard_map/ppermute | solution.py:48
  9.5 7.4 %collective-permute-start.1 = (bf16[4,128,128]{2,1,0:T(8,128)(2,1)S(1)}, bf16[4,128,128]{2,1,0:T(8,128)(2,1)S(1)}, u32[]{:S(2)}, u32[]{:S(2)}) collective-permute-start(bf16[4,128,128]{2,1,0:T(8,128)(2,1)S(1)} %fusion.35), channel_id=1, source_target_pairs={{0,32},{16,48},{32,64},{48,80},{64,96},{80,112},{96,128},{112,144}... | collective-permute-start | bytes 393224 | tf_op jit(solution)/shard_map/ppermute | solution.py:48
  17.0 12.4 %collective-permute-start.2 = (bf16[4,128,128]{2,1,0:T(8,128)(2,1)S(1)}, bf16[4,128,128]{2,1,0:T(8,128)(2,1)S(1)}, u32[]{:S(2)}, u32[]{:S(2)}) collective-permute-start(bf16[4,128,128]{2,1,0:T(8,128)(2,1)S(1)} %get-tuple-element.9), channel_id=1, source_target_pairs={{0,64},{16,80},{32,96},{48,112},{64,128},{80,144},{96,160},{112,17... | collective-permute-start | bytes 393224 | tf_op jit(solution)/shard_map/ppermute | solution.py:48
  29.5 10.7 %collective-permute-start.3 = (bf16[4,128,128]{2,1,0:T(8,128)(2,1)S(1)}, bf16[4,128,128]{2,1,0:T(8,128)(2,1)S(1)}, u32[]{:S(2)}, u32[]{:S(2)}) collective-permute-start(bf16[4,128,128]{2,1,0:T(8,128)(2,1)S(1)} %fusion.36), channel_id=1, source_target_pairs={{0,128},{16,144},{32,160},{48,176},{64,192},{80,208},{96,224},{112... | collective-permute-start | bytes 393224 | tf_op jit(solution)/shard_map/ppermute | solution.py:48
  40.4 30.5 %copy-start.3 = (bf16[256,512]{1,0:T(8,128)(2,1)S(1)}, bf16[256,512]{1,0:T(8,128)(2,1)}, u32[]{:S(2)}) copy-start(bf16[256,512]{1,0:T(8,128)(2,1)} %param.10) | copy-start | bytes 786436
  40.4 12.1 %collective-permute-start.4 = (bf16[4,128,128]{2,1,0:T(8,128)(2,1)S(1)}, bf16[4,128,128]{2,1,0:T(8,128)(2,1)S(1)}, u32[]{:S(2)}, u32[]{:S(2)}) collective-permute-start(bf16[4,128,128]{2,1,0:T(8,128)(2,1)S(1)} %fusion.48), channel_id=1, source_target_pairs={{0,256},{16,272},{32,288},{48,304},{64,320},{80,336},{96,352},{112... | collective-permute-start | bytes 393224 | tf_op jit(solution)/shard_map/ppermute | solution.py:48
  51.1 21.6 %copy-start.4 = (f32[512]{0:T(512)S(1)}, f32[512]{0:T(512)}, u32[]{:S(2)}) copy-start(f32[512]{0:T(512)} %param.12) | copy-start | bytes 6148
  52.7 20.1 %collective-permute-start.5 = (bf16[4,128,128]{2,1,0:T(8,128)(2,1)S(1)}, bf16[4,128,128]{2,1,0:T(8,128)(2,1)S(1)}, u32[]{:S(2)}, u32[]{:S(2)}) collective-permute-start(bf16[4,128,128]{2,1,0:T(8,128)(2,1)S(1)} %add_convert_fusion), channel_id=1, source_target_pairs={{0,512},{16,528},{32,544},{48,560},{64,576},{80,592},{96,608},{112... | collective-permute-start | bytes 393224 | tf_op jit(solution)/shard_map/ppermute | solution.py:48
  84.1 8.3 %collective-permute-start.6 = (bf16[8,16,6272]{2,1,0:T(8,128)(2,1)}, bf16[8,16,6272]{2,1,0:T(8,128)(2,1)S(1)}, u32[]{:S(2)}, u32[]{:S(2)}) collective-permute-start(bf16[8,16,6272]{2,1,0:T(8,128)(2,1)} %concatenate.6), channel_id=1, source_target_pairs={{0,1},{1,0},{2,3},{3,2},{4,5},{5,4},{6,7},{7,6},{8,9},{9,8},{10,11... | collective-permute-start | bytes 4816904 | tf_op jit(solution)/shard_map/ppermute | solution.py:79
  92.4 1.2 copy-start.1

commit v8 on v7

--- a/solution.py
+++ b/solution.py
@@ -69,21 +69,26 @@
     return packed[..., :lanes].astype(jnp.float32), squares
 
 
-def fsdp_reduce(parts, squares):
+def fsdp_reduce(gated, squares, weight):
     core = lax.axis_index("fc")
-    lanes = parts.shape[-1]
-    keep = lax.dynamic_index_in_dim(parts, core, axis=1, keepdims=False)
+    chips, _, rows, features = gated.shape
+    lanes = weight.shape[1]
+
+    def project(block):
+        flat = jnp.dot(block.reshape(-1, features), weight, preferred_element_type=jnp.float32)
+        return flat.astype(jnp.bfloat16).reshape(chips, rows, lanes)
+
+    give = project(lax.dynamic_index_in_dim(gated, 1 - core, axis=1, keepdims=False))
+    give_sq = lax.dynamic_index_in_dim(squares, 1 - core, axis=1, keepdims=False)
+    sent = lax.ppermute(pack(give, give_sq), "fc", perm=[(0, 1), (1, 0)])
+    keep = project(lax.dynamic_index_in_dim(gated, core, axis=1, keepdims=False))
     keep_sq = lax.dynamic_index_in_dim(squares, core, axis=1, keepdims=False)
-    give = lax.dynamic_index_in_dim(parts, 1 - core, axis=1, keepdims=False)
-    give_sq = lax.dynamic_index_in_dim(squares, 1 - core, axis=1, keepdims=False)
-    got, got_sq = unpack(lax.ppermute(pack(give, give_sq), "fc", perm=[(0, 1), (1, 0)]), lanes)
+    got, got_sq = unpack(sent, lanes)
     mine = keep.astype(jnp.float32) + got
     mine_sq = keep_sq + got_sq
     moved = lax.all_to_all(pack(mine, mine_sq), "fy", 0, 0, tiled=True)
     values, sums = unpack(moved, lanes)
-    cur = jnp.sum(values, axis=0)
-    cur_sq = jnp.sum(sums, axis=0)
-    return cur, cur_sq
+    return jnp.sum(values, axis=0), jnp.sum(sums, axis=0)
 
 
 def per_device(query_act, key_act, value_act, gate_act, rate_index, norm_gain, out_weight):
@@ -105,10 +110,9 @@
     local_squares = jnp.sum(attended * attended, axis=(1, 2))
     gated = attended * gain_table[None] * jax.nn.sigmoid(gate_rows.astype(jnp.float32))
     gated = gated.reshape(tok_count, -1).astype(jnp.bfloat16)
-    projected = jnp.dot(gated, out_weight, preferred_element_type=jnp.float32).astype(jnp.bfloat16)
     owned = tok_count // 16
     summed, square_sum = fsdp_reduce(
-        projected.reshape(-1, 2, owned, projected.shape[1]), local_squares.reshape(-1, 2, owned)
+        gated.reshape(-1, 2, owned, gated.shape[1]), local_squares.reshape(-1, 2, owned), out_weight
     )
     inv_rms = lax.rsqrt(square_sum / (HEADS * HEAD_DIM) + 1e-06)
     return (summed.astype(jnp.float32) * inv_rms[:, None]).astype(jnp.bfloat16)

time: 149 us -> 142 us (0.953)
  local copies, waits for them, and re-layouts: 10.8 us -> 5.45 us
  waiting for transfers between devices: 13.9 us -> 10.6 us
  matrix products: 7.71 us -> 9.95 us
    concatenate x2, local copies, waits for them, and re-layouts: 6.02 us -> 1.01 us  [pack(): return jnp.concatenate([values.astype(jnp.bfloat16), extra], axis=-1)]
    ppermute x1, waiting for transfers between devices: 3.27 us -> 0.01 us  [fsdp_reduce(): sent = lax.ppermute(pack(give, give_sq), 'fc', perm=[(0, 1), (1, 0)])]
    dot_general x1 -> x2, matrix products: 4.7 us -> 7.63 us  [project(): jnp.dot(block.reshape(-1, features), weight, preferred_element_type=jnp.f...]
  transfers between devices with their start and end apart: 7 -> 7, of which waited for: 7 -> 6; matrix products, arithmetic and copies ran while one was open for 1% -> 4% of each run, Pallas kernels for 0% -> 0%
where the time goes in v8:
time: 142 us; the launch traced here: 141 us
  starting transfers between devices  62.2 us (44%)
  blocking collectives  47.9 us (34%)
  waiting for transfers between devices  10.6 us (7%)
  matrix products  9.95 us (7%)
  local copies, waits for them, and re-layouts  5.45 us (4%)
  other arithmetic  4.77 us (3%)
    ppermute x6, starting transfers between devices, decayed_scan(): lax.ppermute(total.astype(jnp.bfloat16), axis, perm=[(i, i + shift) for i...  57.1 us
    all_to_all x1, blocking collectives, fsdp_reduce(): moved = lax.all_to_all(pack(mine, mine_sq), 'fy', 0, 0, tiled=True)  47.9 us
    ppermute x6, waiting for transfers between devices, decayed_scan(): lax.ppermute(total.astype(jnp.bfloat16), axis, perm=[(i, i + shift) for i...  10.6 us
    dot_general x2, matrix products, project(): jnp.dot(block.reshape(-1, features), weight, preferred_element_type=jnp.f...  7.63 us
    ppermute x1, starting transfers between devices, fsdp_reduce(): sent = lax.ppermute(pack(give, give_sq), 'fc', perm=[(0, 1), (1, 0)])  5.06 us
  transfers between devices with their start and end apart: 7, of which 6 were waited for; matrix products, arithmetic and copies ran while one was open for 4% of the time, Pallas kernels for 0%

profile of v8, /device:TPU:1, one launch (start us, length us, event | category | flops | bytes accessed | tf_op | source)
XLA Modules:
  0.0 141.2 jit_solution(11639347095784962500)
XLA Ops:
  0.0 0.7 multiply_exponential_fusion.3
  0.7 1.1 copy.63
  1.9 1.2 fusion.52
  3.1 4.1 %collective-permute-start = (bf16[4,128,128]{2,1,0:T(8,128)(2,1)S(1)}, bf16[4,128,128]{2,1,0:T(8,128)(2,1)S(1)}, u32[]{:S(2)}, u32[]{:S(2)}) collective-permute-start(bf16[4,128,128]{2,1,0:T(8,128)(2,1)S(1)} %get-tuple-element.29), channel_id=1, source_target_pairs={{0,16},{16,32},{32,48},{48,64},{64,80},{80,96},{96,112},{112,128},... | collective-permute-start | bytes 393224 | tf_op jit(solution)/shard_map/ppermute | solution.py:48
  7.2 2.2 %collective-permute-done = bf16[4,128,128]{2,1,0:T(8,128)(2,1)S(1)} collective-permute-done((bf16[4,128,128]{2,1,0:T(8,128)(2,1)S(1)}, bf16[4,128,128]{2,1,0:T(8,128)(2,1)S(1)}, u32[]{:S(2)}, u32[]{:S(2)}) %collective-permute-start) | collective-permute-done | bytes 131104 | tf_op jit(solution)/shard_map/ppermute | solution.py:48
  9.5 5.5 %collective-permute-start.1 = (bf16[4,128,128]{2,1,0:T(8,128)(2,1)S(1)}, bf16[4,128,128]{2,1,0:T(8,128)(2,1)S(1)}, u32[]{:S(2)}, u32[]{:S(2)}) collective-permute-start(bf16[4,128,128]{2,1,0:T(8,128)(2,1)S(1)} %fusion.35), channel_id=1, source_target_pairs={{0,32},{16,48},{32,64},{48,80},{64,96},{80,112},{96,128},{112,144}... | collective-permute-start | bytes 393224 | tf_op jit(solution)/shard_map/ppermute | solution.py:48
  15.0 1.9 %collective-permute-done.1 = bf16[4,128,128]{2,1,0:T(8,128)(2,1)S(1)} collective-permute-done((bf16[4,128,128]{2,1,0:T(8,128)(2,1)S(1)}, bf16[4,128,128]{2,1,0:T(8,128)(2,1)S(1)}, u32[]{:S(2)}, u32[]{:S(2)}) %collective-permute-start.1) | collective-permute-done | bytes 131104 | tf_op jit(solution)/shard_map/ppermute | solution.py:48
  17.0 10.4 %collective-permute-start.2 = (bf16[4,128,128]{2,1,0:T(8,128)(2,1)S(1)}, bf16[4,128,128]{2,1,0:T(8,128)(2,1)S(1)}, u32[]{:S(2)}, u32[]{:S(2)}) collective-permute-start(bf16[4,128,128]{2,1,0:T(8,128)(2,1)S(1)} %get-tuple-element.9), channel_id=1, source_target_pairs={{0,64},{16,80},{32,96},{48,112},{64,128},{80,144},{96,160},{112,17... | collective-permute-start | bytes 393224 | tf_op jit(solution)/shard_map/ppermute | solution.py:48
  27.6 1.8 %collective-permute-done.2 = bf16[4,128,128]{2,1,0:T(8,128)(2,1)S(1)} collective-permute-done((bf16[4,128,128]{2,1,0:T(8,128)(2,1)S(1)}, bf16[4,128,128]{2,1,0:T(8,128)(2,1)S(1)}, u32[]{:S(2)}, u32[]{:S(2)}) %collective-permute-start.2) | collective-permute-done | bytes 131104 | tf_op jit(solution)/shard_map/ppermute | solution.py:48
  29.5 8.8 %collective-permute-start.3 = (bf16[4,128,128]{2,1,0:T(8,128)(2,1)S(1)}, bf16[4,128,128]{2,1,0:T(8,128)(2,1)S(1)}, u32[]{:S(2)}, u32[]{:S(2)}) collective-permute-start(bf16[4,128,128]{2,1,0:T(8,128)(2,1)S(1)} %fusion.36), channel_id=1, source_target_pairs={{0,128},{16,144},{32,160},{48,176},{64,192},{80,208},{96,224},{112... | collective-permute-start | bytes 393224 | tf_op jit(solution)/shard_map/ppermute | solution.py:48
  38.4 1.8 %collective-permute-done.3 = bf16[4,128,128]{2,1,0:T(8,128)(2,1)S(1)} collective-permute-done((bf16[4,128,128]{2,1,0:T(8,128)(2,1)S(1)}, bf16[4,128,128]{2,1,0:T(8,128)(2,1)S(1)}, u32[]{:S(2)}, u32[]{:S(2)}) %collective-permute-start.3) | collective-permute-done | bytes 131104 | tf_op jit(solution)/shard_map/ppermute | solution.py:48
  40.4 10.2 %collective-permute-start.4 = (bf16[4,128,128]{2,1,0:T(8,128)(2,1)S(1)}, bf16[4,128,128]{2,1,0:T(8,128)(2,1)S(1)}, u32[]{:S(2)}, u32[]{:S(2)}) collective-permute-start(bf16[4,128,128]{2,1,0:T(8,128)(2,1)S(1)} %fusion.48), channel_id=1, source_target_pairs={{0,256},{16,272},{32,288},{48,304},{64,320},{80,336},{96,352},{112... | collective-permute-start | bytes 393224 | tf_op jit(solution)/shard_map/ppermute | solution.py:48
  50.6 0.5 convolution_bitcast_fusion.1
  51.2 1.4 collective-permute-done.4
  52.5 0.2 add_convert_fusion
  52.7 18.1 %collective-permute-start.5 = (bf16[4,128,128]{2,1,0:T(8,128)(2,1)S(1)}, bf16[4,128,128]{2,1,0:T(8,128)(2,1)S(1)}, u32[]{:S(2)}, u32[]{:S(2)}) collective-permute-start(bf16[4,128,128]{2,1,0:T(8,128)(2,1)S(1)} %add_convert_fusion), channel_id=1, source_target_pairs={{0,512},{16,528},{32,544},{48,560},{64,576},{80,592},{96,608},{112... | collective-permute-start | bytes 393224 | tf_op jit(solution)/shard_map/ppermute | solution.py:48
  71.0 0.2 copy.49
  71.2 1.6 %collective-permute-done.5 = bf16[4,128,128]{2,1,0:T(8,128)(2,1)S(1)} collective-permute-done((bf16[4,128,128]{2,1,0:T(8,128)(2,1)S(1)}, bf16[4,128,128]{2,1,0:T(8,128)(2,1)S(1)}, u32[]{:S(2)}, u32[]{:S(2)}) %collective-permute-start.5) | collective-permute-done | bytes 131104 | tf_op jit(solution)/shard_map/ppermute | solution.py:48
  72.7 0.6 multiply_reduce_fusion
  73.4 0.2 copy.50
  73.7 0.7 constant_dynamic-slice_fusion.2
  74.7 3.8 %convolution_convert_fusion = bf16[128,6144]{1,0:T(8,128)(2,1)S(1)} fusion(bf16[128,512]{1,0:T(8,128)(2,1)S(1)} %bitcast.59, bf16[512,6144]{1,0:T(8,128)(2,1)} %param.13), kind=kOutput, calls=%fused_computation | convolution fusion | flops 806092800 | bytes 7995392 | tf_op jit(solution)/shard_map/dot_general | solution.py:78
  78.5 0.5 concatenate.6
  79.0 5.1 %collective-permute-start.6 = (bf16[8,16,6272]{2,1,0:T(8,128)(2,1)S(1)}, bf16[8,16,6272]{2,1,0:T(8,128)(2,1)S(1)}, u32[]{:S(2)}, u32[]{:S(2)}) collective-permute-start(bf16[8,16,6272]{2,1,0:T(8,128)(2,1)S(1)} %concatenate.6), channel_id=1, source_target_pairs={{0,1},{1,0},{2,3},{3,2},{4,5},{5,4},{6,7},{7,6},{8,9},{9,8},{10,11... | collective-permute-start | bytes 4816904 | tf_op jit(solution)/shard_map/ppermute | solution.py:83
  84.1 3.9 %convolution_convert_fusion.1 = bf16[128,6144]{1,0:T(8,128)(2,1)S(1)} fusion(bf16[128,512]{1,0:T(8,128)(2,1)} %bitcast.58, bf16[512,6144]{1,0:T(8,128)(2,1)} %param.13), kind=kOutput, calls=%fused_computation.1 | convolution fusion | flops 806092800 | bytes 7995392 | tf_op jit(solution)/shard_map/dot_general | solution.py:78
  88.0 1.2 copy-done.1
  89.8 1.8 %fusion = bf16[8,16,6144]{2,1,0:T(8,128)(2,1)S(1)} fusion(bf16[8,16,6144]{2,1,0:T(8,128)(2,1)S(1)} %bitcast.54, bf16[8,16,6272]{2,1,0:T(8,128)(2,1)} %copy-done.1), kind=kLoop, calls=%fused_computation.3 | loop fusion | flops 3145728 | bytes 4718592 | tf_op jit(solution)/shard_map/convert_element_type | solution.py:64
  91.6 0.5 concatenate.7
  92.1 47.9 %all_to_all.5 = bf16[8,16,6272]{2,1,0:T(8,128)(2,1)S(1)} all-to-all(bf16[8,16,6272]{2,1,0:T(8,128)(2,1)S(1)} %concatenate.7), channel_id=1, replica_groups=mesh['sz'=8,'sx'=8,'fy'=8,'fc'=2] {'fy'}, dimensions={0} | all-to-all | bytes 3211264 | tf_op jit(solution)/shard_map/all_to_all | solution.py:89
  140.0 0.2 add_reduce_fusion
  140.2 0.2 convert_reduce_fusion
  140.4 0.8 multiply_convert_fusion.2
  (35 shorter events, 2.1 us)
Async XLA Ops:
  0.0 50.6 %copy-start = (bf16[256,512]{1,0:T(8,128)(2,1)S(1)}, bf16[256,512]{1,0:T(8,128)(2,1)}, u32[]{:S(2)}) copy-start(bf16[256,512]{1,0:T(8,128)(2,1)} %param.7) | copy-start | bytes 786436
  3.1 47.5 %copy-start.2 = (bf16[256,512]{1,0:T(8,128)(2,1)S(1)}, bf16[256,512]{1,0:T(8,128)(2,1)}, u32[]{:S(2)}) copy-start(bf16[256,512]{1,0:T(8,128)(2,1)} %param.9) | copy-start | bytes 786436
  3.1 6.3 %collective-permute-start = (bf16[4,128,128]{2,1,0:T(8,128)(2,1)S(1)}, bf16[4,128,128]{2,1,0:T(8,128)(2,1)S(1)}, u32[]{:S(2)}, u32[]{:S(2)}) collective-permute-start(bf16[4,128,128]{2,1,0:T(8,128)(2,1)S(1)} %get-tuple-element.29), channel_id=1, source_target_pairs={{0,16},{16,32},{32,48},{48,64},{64,80},{80,96},{96,112},{112,128},... | collective-permute-start | bytes 393224 | tf_op jit(solution)/shard_map/ppermute | solution.py:48
  9.5 7.4 %collective-permute-start.1 = (bf16[4,128,128]{2,1,0:T(8,128)(2,1)S(1)}, bf16[4,128,128]{2,1,0:T(8,128)(2,1)S(1)}, u32[]{:S(2)}, u32[]{:S(2)}) collective-permute-start(bf16[4,128,128]{2,1,0:T(8,128)(2,1)S(1)} %fusion.35), channel_id=1, source_target_pairs={{0,32},{16,48},{32,64},{48,80},{64,96},{80,112},{96,128},{112,144}... | collective-permute-start | bytes 393224 | tf_op jit(solution)/shard_map/ppermute | solution.py:48
  17.0 12.4 %collective-permute-start.2 = (bf16[4,128,128]{2,1,0:T(8,128)(2,1)S(1)}, bf16[4,128,128]{2,1,0:T(8,128)(2,1)S(1)}, u32[]{:S(2)}, u32[]{:S(2)}) collective-permute-start(bf16[4,128,128]{2,1,0:T(8,128)(2,1)S(1)} %get-tuple-element.9), channel_id=1, source_target_pairs={{0,64},{16,80},{32,96},{48,112},{64,128},{80,144},{96,160},{112,17... | collective-permute-start | bytes 393224 | tf_op jit(solution)/shard_map/ppermute | solution.py:48
  29.5 10.7 %collective-permute-start.3 = (bf16[4,128,128]{2,1,0:T(8,128)(2,1)S(1)}, bf16[4,128,128]{2,1,0:T(8,128)(2,1)S(1)}, u32[]{:S(2)}, u32[]{:S(2)}) collective-permute-start(bf16[4,128,128]{2,1,0:T(8,128)(2,1)S(1)} %fusion.36), channel_id=1, source_target_pairs={{0,128},{16,144},{32,160},{48,176},{64,192},{80,208},{96,224},{112... | collective-permute-start | bytes 393224 | tf_op jit(solution)/shard_map/ppermute | solution.py:48
  40.4 30.5 %copy-start.3 = (bf16[256,512]{1,0:T(8,128)(2,1)S(1)}, bf16[256,512]{1,0:T(8,128)(2,1)}, u32[]{:S(2)}) copy-start(bf16[256,512]{1,0:T(8,128)(2,1)} %param.10) | copy-start | bytes 786436
  40.4 12.1 %collective-permute-start.4 = (bf16[4,128,128]{2,1,0:T(8,128)(2,1)S(1)}, bf16[4,128,128]{2,1,0:T(8,128)(2,1)S(1)}, u32[]{:S(2)}, u32[]{:S(2)}) collective-permute-start(bf16[4,128,128]{2,1,0:T(8,128)(2,1)S(1)} %fusion.48), channel_id=1, source_target_pairs={{0,256},{16,272},{32,288},{48,304},{64,320},{80,336},{96,352},{112... | collective-permute-start | bytes 393224 | tf_op jit(solution)/shard_map/ppermute | solution.py:48
  51.1 21.6 %copy-start.4 = (f32[512]{0:T(512)S(1)}, f32[512]{0:T(512)}, u32[]{:S(2)}) copy-start(f32[512]{0:T(512)} %param.12) | copy-start | bytes 6148
  52.7 20.1 %collective-permute-start.5 = (bf16[4,128,128]{2,1,0:T(8,128)(2,1)S(1)}, bf16[4,128,128]{2,1,0:T(8,128)(2,1)S(1)}, u32[]{:S(2)}, u32[]{:S(2)}) collective-permute-start(bf16[4,128,128]{2,1,0:T(8,128)(2,1)S(1)} %add_convert_fusion), channel_id=1, source_target_pairs={{0,512},{16,528},{32,544},{48,560},{64,576},{80,592},{96,608},{112... | collective-permute-start | bytes 393224 | tf_op jit(solution)/shard_map/ppermute | solution.py:48
  79.0 8.9 %collective-permute-start.6 = (bf16[8,16,6272]{2,1,0:T(8,128)(2,1)S(1)}, bf16[8,16,6272]{2,1,0:T(8,128)(2,1)S(1)}, u32[]{:S(2)}, u32[]{:S(2)}) collective-permute-start(bf16[8,16,6272]{2,1,0:T(8,128)(2,1)S(1)} %concatenate.6), channel_id=1, source_target_pairs={{0,1},{1,0},{2,3},{3,2},{4,5},{5,4},{6,7},{7,6},{8,9},{9,8},{10,11... | collective-permute-start | bytes 4816904 | tf_op jit(solution)/shard_map/ppermute | solution.py:83
  88.0 1.2 copy-start.1

commit v9 on v8

--- a/solution.py
+++ b/solution.py
@@ -86,9 +86,37 @@
     got, got_sq = unpack(sent, lanes)
     mine = keep.astype(jnp.float32) + got
     mine_sq = keep_sq + got_sq
-    moved = lax.all_to_all(pack(mine, mine_sq), "fy", 0, 0, tiled=True)
-    values, sums = unpack(moved, lanes)
-    return jnp.sum(values, axis=0), jnp.sum(sums, axis=0)
+    return chip_ring(mine, mine_sq, lanes)
+
+
+def chip_ring(mine, mine_sq, lanes):
+    n = lax.axis_size("fy")
+    i = lax.axis_index("fy")
+
+    def block(j):
+        return (
+            lax.dynamic_index_in_dim(mine, j % n, axis=0, keepdims=False),
+            lax.dynamic_index_in_dim(mine_sq, j % n, axis=0, keepdims=False),
+        )
+
+    ahead = [(j, (j + 1) % n) for j in range(n)]
+    behind = [(j, (j - 1) % n) for j in range(n)]
+    far = n // 2
+    near = n - 1 - far
+    cw, cw_sq = block(i + far)
+    ccw, ccw_sq = block(i - near)
+    for k in range(far):
+        recv, recv_sq = unpack(lax.ppermute(pack(cw, cw_sq), "fy", perm=ahead), lanes)
+        own, own_sq = block(i + far - 1 - k)
+        cw, cw_sq = recv + own, recv_sq + own_sq
+        if k < near:
+            recv, recv_sq = unpack(lax.ppermute(pack(ccw, ccw_sq), "fy", perm=behind), lanes)
+            if k < near - 1:
+                own, own_sq = block(i - near + 1 + k)
+                ccw, ccw_sq = recv + own, recv_sq + own_sq
+            else:
+                ccw, ccw_sq = recv, recv_sq
+    return cw + ccw, cw_sq + ccw_sq
 
 
 def per_device(query_act, key_act, value_act, gate_act, rate_index, norm_gain, out_weight):

time: 142 us -> 171 us (1.20); the launches traced: 141 us -> 168 us
  blocking collectives: 47.9 us -> 0 us
  waiting for transfers between devices: 10.6 us -> 38.2 us
  local copies, waits for them, and re-layouts: 5.45 us -> 26.1 us
  starting transfers between devices: 62.2 us -> 82.6 us
  other arithmetic: 4.77 us -> 10.9 us
    all_to_all x1 -> x0, blocking collectives: 47.9 us -> none  [fsdp_reduce(): moved = lax.all_to_all(pack(mine, mine_sq), 'fy', 0, 0, tiled=True)]
    ppermute x0 -> x7, waiting for transfers between devices: none -> 27.6 us  [the longest x4 20.6 us: chip_ring(): lax.ppermute(pack(cw, cw_sq), 'fy', perm=ahead)]
    ppermute x0 -> x7, starting transfers between devices: none -> 20.5 us  [the longest x3 11.5 us: chip_ring(): lax.ppermute(pack(ccw, ccw_sq), 'fy', perm=behind)]
    concatenate x2 -> x8, local copies, waits for them, and re-layouts: 1.01 us -> 13.8 us  [pack(): return jnp.concatenate([values.astype(jnp.bfloat16), extra], axis=-1)]
    slice x1 -> x7, local copies, waits for them, and re-layouts: 0.08 us -> 5.8 us  [unpack(): packed[..., lanes].astype(jnp.float32)]
    convert_element_type x1 -> x3, other arithmetic: 1.79 us -> 5.31 us  [pack(): return jnp.concatenate([values.astype(jnp.bfloat16), extra], axis=-1)]
    add x0 -> x3, other arithmetic: none -> 1.94 us  [the longest x1 1.78 us: fsdp_reduce(): mine = keep.astype(jnp.float32) + got]
  transfers between devices with their start and end apart: 7 -> 14, of which waited for: 6 -> 11; matrix products, arithmetic and copies ran while one was open for 4% -> 7% of each run, Pallas kernels for 0% -> 0%
where the time goes in v9:
time: 171 us; the launch traced here: 168 us
  starting transfers between devices  82.6 us (48%)
  waiting for transfers between devices  38.2 us (22%)
  local copies, waits for them, and re-layouts  26.1 us (15%)
  other arithmetic  10.9 us (6%)
  matrix products  9.88 us (6%)
    ppermute x6, starting transfers between devices, decayed_scan(): lax.ppermute(total.astype(jnp.bfloat16), axis, perm=[(i, i + shift) for i...  57 us
    ppermute x4, waiting for transfers between devices, chip_ring(): lax.ppermute(pack(cw, cw_sq), 'fy', perm=ahead)  20.6 us
    concatenate x8, local copies, waits for them, and re-layouts, pack(): return jnp.concatenate([values.astype(jnp.bfloat16), extra], axis=-1)  13.8 us
    ppermute x3, starting transfers between devices, chip_ring(): lax.ppermute(pack(ccw, ccw_sq), 'fy', perm=behind)  11.5 us
    ppermute x6, waiting for transfers between devices, decayed_scan(): lax.ppermute(total.astype(jnp.bfloat16), axis, perm=[(i, i + shift) for i...  10.6 us
    ppermute x4, starting transfers between devices, chip_ring(): lax.ppermute(pack(cw, cw_sq), 'fy', perm=ahead)  9.04 us
    dot_general x2, matrix products, project(): jnp.dot(block.reshape(-1, features), weight, preferred_element_type=jnp.f...  7.55 us
    ppermute x3, waiting for transfers between devices, chip_ring(): lax.ppermute(pack(ccw, ccw_sq), 'fy', perm=behind)  6.98 us
  transfers between devices with their start and end apart: 14, of which 11 were waited for; matrix products, arithmetic and copies ran while one was open for 7% of the time, Pallas kernels for 0%

profile of v9, /device:TPU:1, one launch (start us, length us, event | category | flops | bytes accessed | tf_op | source)
XLA Modules:
  0.0 168.2 jit_solution(5397612653152484816)
XLA Ops:
  3.1 4.1 %collective-permute-start = (bf16[4,128,128]{2,1,0:T(8,128)(2,1)S(1)}, bf16[4,128,128]{2,1,0:T(8,128)(2,1)S(1)}, u32[]{:S(2)}, u32[]{:S(2)}) collective-permute-start(bf16[4,128,128]{2,1,0:T(8,128)(2,1)S(1)} %get-tuple-element.60), channel_id=1, source_target_pairs={{0,16},{16,32},{32,48},{48,64},{64,80},{80,96},{96,112},{112,128},... | collective-permute-start | bytes 393224 | tf_op jit(solution)/shard_map/ppermute | solution.py:48
  7.2 2.2 %collective-permute-done = bf16[4,128,128]{2,1,0:T(8,128)(2,1)S(1)} collective-permute-done((bf16[4,128,128]{2,1,0:T(8,128)(2,1)S(1)}, bf16[4,128,128]{2,1,0:T(8,128)(2,1)S(1)}, u32[]{:S(2)}, u32[]{:S(2)}) %collective-permute-start) | collective-permute-done | bytes 131104 | tf_op jit(solution)/shard_map/ppermute | solution.py:48
  9.5 5.5 %collective-permute-start.1 = (bf16[4,128,128]{2,1,0:T(8,128)(2,1)S(1)}, bf16[4,128,128]{2,1,0:T(8,128)(2,1)S(1)}, u32[]{:S(2)}, u32[]{:S(2)}) collective-permute-start(bf16[4,128,128]{2,1,0:T(8,128)(2,1)S(1)} %fusion.44), channel_id=1, source_target_pairs={{0,32},{16,48},{32,64},{48,80},{64,96},{80,112},{96,128},{112,144}... | collective-permute-start | bytes 393224 | tf_op jit(solution)/shard_map/ppermute | solution.py:48
  15.0 1.9 %collective-permute-done.1 = bf16[4,128,128]{2,1,0:T(8,128)(2,1)S(1)} collective-permute-done((bf16[4,128,128]{2,1,0:T(8,128)(2,1)S(1)}, bf16[4,128,128]{2,1,0:T(8,128)(2,1)S(1)}, u32[]{:S(2)}, u32[]{:S(2)}) %collective-permute-start.1) | collective-permute-done | bytes 131104 | tf_op jit(solution)/shard_map/ppermute | solution.py:48
  17.0 10.4 %collective-permute-start.2 = (bf16[4,128,128]{2,1,0:T(8,128)(2,1)S(1)}, bf16[4,128,128]{2,1,0:T(8,128)(2,1)S(1)}, u32[]{:S(2)}, u32[]{:S(2)}) collective-permute-start(bf16[4,128,128]{2,1,0:T(8,128)(2,1)S(1)} %get-tuple-element.19), channel_id=1, source_target_pairs={{0,64},{16,80},{32,96},{48,112},{64,128},{80,144},{96,160},{112,17... | collective-permute-start | bytes 393224 | tf_op jit(solution)/shard_map/ppermute | solution.py:48
  27.6 1.8 %collective-permute-done.2 = bf16[4,128,128]{2,1,0:T(8,128)(2,1)S(1)} collective-permute-done((bf16[4,128,128]{2,1,0:T(8,128)(2,1)S(1)}, bf16[4,128,128]{2,1,0:T(8,128)(2,1)S(1)}, u32[]{:S(2)}, u32[]{:S(2)}) %collective-permute-start.2) | collective-permute-done | bytes 131104 | tf_op jit(solution)/shard_map/ppermute | solution.py:48
  29.5 8.8 %collective-permute-start.3 = (bf16[4,128,128]{2,1,0:T(8,128)(2,1)S(1)}, bf16[4,128,128]{2,1,0:T(8,128)(2,1)S(1)}, u32[]{:S(2)}, u32[]{:S(2)}) collective-permute-start(bf16[4,128,128]{2,1,0:T(8,128)(2,1)S(1)} %fusion.45), channel_id=1, source_target_pairs={{0,128},{16,144},{32,160},{48,176},{64,192},{80,208},{96,224},{112... | collective-permute-start | bytes 393224 | tf_op jit(solution)/shard_map/ppermute | solution.py:48
  38.4 1.8 %collective-permute-done.3 = bf16[4,128,128]{2,1,0:T(8,128)(2,1)S(1)} collective-permute-done((bf16[4,128,128]{2,1,0:T(8,128)(2,1)S(1)}, bf16[4,128,128]{2,1,0:T(8,128)(2,1)S(1)}, u32[]{:S(2)}, u32[]{:S(2)}) %collective-permute-start.3) | collective-permute-done | bytes 131104 | tf_op jit(solution)/shard_map/ppermute | solution.py:48
  40.3 10.1 %collective-permute-start.4 = (bf16[4,128,128]{2,1,0:T(8,128)(2,1)S(1)}, bf16[4,128,128]{2,1,0:T(8,128)(2,1)S(1)}, u32[]{:S(2)}, u32[]{:S(2)}) collective-permute-start(bf16[4,128,128]{2,1,0:T(8,128)(2,1)S(1)} %fusion.73), channel_id=1, source_target_pairs={{0,256},{16,272},{32,288},{48,304},{64,320},{80,336},{96,352},{112... | collective-permute-start | bytes 393224 | tf_op jit(solution)/shard_map/ppermute | solution.py:48
  52.5 18.1 %collective-permute-start.5 = (bf16[4,128,128]{2,1,0:T(8,128)(2,1)S(1)}, bf16[4,128,128]{2,1,0:T(8,128)(2,1)S(1)}, u32[]{:S(2)}, u32[]{:S(2)}) collective-permute-start(bf16[4,128,128]{2,1,0:T(8,128)(2,1)S(1)} %add_convert_fusion), channel_id=1, source_target_pairs={{0,512},{16,528},{32,544},{48,560},{64,576},{80,592},{96,608},{112... | collective-permute-start | bytes 393224 | tf_op jit(solution)/shard_map/ppermute | solution.py:48
  74.0 3.8 %convolution_convert_fusion = bf16[128,6144]{1,0:T(8,128)(2,1)S(1)} fusion(bf16[128,512]{1,0:T(8,128)(2,1)S(1)} %bitcast.142, bf16[512,6144]{1,0:T(8,128)(2,1)} %param.13), kind=kOutput, calls=%fused_computation | convolution fusion | flops 806092800 | bytes 7995392 | tf_op jit(solution)/shard_map/dot_general | solution.py:78
  77.8 1.9 %concatenate.24 = bf16[8,16,6272]{2,1,0:T(8,128)(2,1)} concatenate(bf16[8,16,6144]{2,1,0:T(8,128)(2,1)S(1)} %bitcast.136, bf16[8,16,1]{2,1,0:T(8,128)(2,1)S(1)} %copy.101, bf16[8,16,1]{2,1,0:T(8,128)(2,1)S(1)} %copy.102, bf16[8,16,126]{2,1,0:T(8,128)(2,1)S(1)} %broadcast_in_dim.16), dimensions={2} | concatenate | bytes 3211264 | tf_op jit(solution)/shard_map/concatenate | solution.py:64
  79.7 5.0 %collective-permute-start.6 = (bf16[8,16,6272]{2,1,0:T(8,128)(2,1)}, bf16[8,16,6272]{2,1,0:T(8,128)(2,1)S(1)}, u32[]{:S(2)}, u32[]{:S(2)}) collective-permute-start(bf16[8,16,6272]{2,1,0:T(8,128)(2,1)} %concatenate.24), channel_id=1, source_target_pairs={{0,1},{1,0},{2,3},{3,2},{4,5},{5,4},{6,7},{7,6},{8,9},{9,8},{10,11... | collective-permute-start | bytes 4816904 | tf_op jit(solution)/shard_map/ppermute | solution.py:83
  84.8 3.8 %convolution_convert_fusion.1 = bf16[128,6144]{1,0:T(8,128)(2,1)S(1)} fusion(bf16[128,512]{1,0:T(8,128)(2,1)S(1)} %bitcast.141, bf16[512,6144]{1,0:T(8,128)(2,1)} %param.13), kind=kOutput, calls=%fused_computation.1 | convolution fusion | flops 806092800 | bytes 7995392 | tf_op jit(solution)/shard_map/dot_general | solution.py:78
  89.8 1.8 %convert_add_fusion = f32[8,16,6144]{2,1,0:T(8,128)S(1)} fusion(bf16[8,16,6144]{2,1,0:T(8,128)(2,1)S(1)} %bitcast.137, bf16[8,16,6272]{2,1,0:T(8,128)(2,1)} %copy-done.1), kind=kLoop, calls=%fused_computation.2 | loop fusion | flops 2359296 | bytes 6291456 | tf_op jit(solution)/shard_map/add | solution.py:87
  94.3 3.3 %collective-permute-start.7 = (bf16[16,6272]{1,0:T(8,128)(2,1)}, bf16[16,6272]{1,0:T(8,128)(2,1)}, u32[]{:S(2)}, u32[]{:S(2)}) collective-permute-start(bf16[16,6272]{1,0:T(8,128)(2,1)} %concatenate.25), channel_id=1, source_target_pairs={{0,2},{2,4},{4,6},{6,8},{8,10},{10,12},{12,14},{14,0},{1,3},{3,5},... | collective-permute-start | bytes 602120 | tf_op jit(solution)/shard_map/ppermute | solution.py:109
  97.6 8.2 %collective-permute-done.7 = bf16[16,6272]{1,0:T(8,128)(2,1)} collective-permute-done((bf16[16,6272]{1,0:T(8,128)(2,1)}, bf16[16,6272]{1,0:T(8,128)(2,1)}, u32[]{:S(2)}, u32[]{:S(2)}) %collective-permute-start.7) | collective-permute-done | bytes 200736 | tf_op jit(solution)/shard_map/ppermute | solution.py:109
  110.4 1.9 %collective-permute-start.8 = (bf16[16,6272]{1,0:T(8,128)(2,1)}, bf16[16,6272]{1,0:T(8,128)(2,1)}, u32[]{:S(2)}, u32[]{:S(2)}) collective-permute-start(bf16[16,6272]{1,0:T(8,128)(2,1)} %concatenate.26), channel_id=1, source_target_pairs={{0,2},{2,4},{4,6},{6,8},{8,10},{10,12},{12,14},{14,0},{1,3},{3,5},... | collective-permute-start | bytes 602120 | tf_op jit(solution)/shard_map/ppermute | solution.py:109
  112.4 7.3 %collective-permute-done.8 = bf16[16,6272]{1,0:T(8,128)(2,1)} collective-permute-done((bf16[16,6272]{1,0:T(8,128)(2,1)}, bf16[16,6272]{1,0:T(8,128)(2,1)}, u32[]{:S(2)}, u32[]{:S(2)}) %collective-permute-start.8) | collective-permute-done | bytes 200736 | tf_op jit(solution)/shard_map/ppermute | solution.py:109
  120.9 1.7 %concatenate.29 = bf16[16,6272]{1,0:T(8,128)(2,1)} concatenate(bf16[16,6144]{1,0:T(8,128)(2,1)} %get-tuple-element.26, bf16[16,1]{1,0:T(8,128)(2,1)S(1)} %copy.117, bf16[16,1]{1,0:T(8,128)(2,1)S(1)} %copy.118, bf16[16,126]{1,0:T(8,128)(2,1)S(1)} %broadcast.163), dimensions={1} | concatenate | bytes 401408 | tf_op jit(solution)/shard_map/concatenate | solution.py:64
  122.6 1.9 %collective-permute-start.11 = (bf16[16,6272]{1,0:T(8,128)(2,1)}, bf16[16,6272]{1,0:T(8,128)(2,1)}, u32[]{:S(2)}, u32[]{:S(2)}) collective-permute-start(bf16[16,6272]{1,0:T(8,128)(2,1)} %concatenate.29), channel_id=1, source_target_pairs={{0,14},{2,0},{4,2},{6,4},{8,6},{10,8},{12,10},{14,12},{1,15},{3,1}... | collective-permute-start | bytes 602120 | tf_op jit(solution)/shard_map/ppermute | solution.py:113
  124.7 5.1 %collective-permute-done.11 = bf16[16,6272]{1,0:T(8,128)(2,1)} collective-permute-done((bf16[16,6272]{1,0:T(8,128)(2,1)}, bf16[16,6272]{1,0:T(8,128)(2,1)}, u32[]{:S(2)}, u32[]{:S(2)}) %collective-permute-start.11) | collective-permute-done | bytes 200736 | tf_op jit(solution)/shard_map/ppermute | solution.py:113
  129.8 1.8 %fusion.16 = (bf16[16,6144]{1,0:T(8,128)(2,1)}, bf16[16,6144]{1,0:T(8,128)(2,1)}) fusion(f32[8,16,6144]{2,1,0:T(8,128)S(1)} %convert_add_fusion, s32[]{:T(128)S(6)} %select_n.107, bf16[16,6272]{1,0:T(8,128)(2,1)} %collective-permute-done.8, s32[]{:T(128)S(6)} %select_n.115, bf16[16,6272]{1,0:T(8,128)(2,1)} %collective-permute-done.11), kind=kLoop, calls=%fused_computation.31 | loop fusion | flops 589824 | bytes 1572872 | tf_op jit(solution)/shard_map/convert_element_type | solution.py:64
  133.3 1.9 %collective-permute-start.9 = (bf16[16,6272]{1,0:T(8,128)(2,1)}, bf16[16,6272]{1,0:T(8,128)(2,1)}, u32[]{:S(2)}, u32[]{:S(2)}) collective-permute-start(bf16[16,6272]{1,0:T(8,128)(2,1)} %concatenate.27), channel_id=1, source_target_pairs={{0,2},{2,4},{4,6},{6,8},{8,10},{10,12},{12,14},{14,0},{1,3},{3,5},... | collective-permute-start | bytes 602120 | tf_op jit(solution)/shard_map/ppermute | solution.py:109
  136.5 1.7 %concatenate.30 = bf16[16,6272]{1,0:T(8,128)(2,1)} concatenate(bf16[16,6144]{1,0:T(8,128)(2,1)} %get-tuple-element.24, bf16[16,1]{1,0:T(8,128)(2,1)S(1)} %copy.121, bf16[16,1]{1,0:T(8,128)(2,1)S(1)} %copy.122, bf16[16,126]{1,0:T(8,128)(2,1)S(1)} %broadcast.163), dimensions={1} | concatenate | bytes 401408 | tf_op jit(solution)/shard_map/concatenate | solution.py:64
  138.2 4.6 %collective-permute-start.12 = (bf16[16,6272]{1,0:T(8,128)(2,1)}, bf16[16,6272]{1,0:T(8,128)(2,1)}, u32[]{:S(2)}, u32[]{:S(2)}) collective-permute-start(bf16[16,6272]{1,0:T(8,128)(2,1)} %concatenate.30), channel_id=1, source_target_pairs={{0,14},{2,0},{4,2},{6,4},{8,6},{10,8},{12,10},{14,12},{1,15},{3,1}... | collective-permute-start | bytes 602120 | tf_op jit(solution)/shard_map/ppermute | solution.py:113
  143.8 1.9 %collective-permute-done.12 = bf16[16,6272]{1,0:T(8,128)(2,1)} collective-permute-done((bf16[16,6272]{1,0:T(8,128)(2,1)}, bf16[16,6272]{1,0:T(8,128)(2,1)}, u32[]{:S(2)}, u32[]{:S(2)}) %collective-permute-start.12) | collective-permute-done | bytes 200736 | tf_op jit(solution)/shard_map/ppermute | solution.py:113
  146.9 1.8 %fusion.15 = (bf16[16,6144]{1,0:T(8,128)(2,1)}, bf16[16,6144]{1,0:T(8,128)(2,1)}) fusion(f32[8,16,6144]{2,1,0:T(8,128)S(1)} %convert_add_fusion, s32[]{:T(128)S(6)} %select_n.109, bf16[16,6272]{1,0:T(8,128)(2,1)} %collective-permute-done.9, s32[]{:T(128)S(6)} %select_n.117, bf16[16,6272]{1,0:T(8,128)(2,1)} %collective-permute-done.12), kind=kLoop, calls=%fused_computation.29 | loop fusion | flops 589824 | bytes 1572872 | tf_op jit(solution)/shard_map/convert_element_type | solution.py:64
  150.4 5.0 %collective-permute-start.13 = (bf16[16,6272]{1,0:T(8,128)(2,1)}, bf16[16,6272]{1,0:T(8,128)(2,1)}, u32[]{:S(2)}, u32[]{:S(2)}) collective-permute-start(bf16[16,6272]{1,0:T(8,128)(2,1)} %concatenate.31), channel_id=1, source_target_pairs={{0,14},{2,0},{4,2},{6,4},{8,6},{10,8},{12,10},{14,12},{1,15},{3,1}... | collective-permute-start | bytes 602120 | tf_op jit(solution)/shard_map/ppermute | solution.py:113
  157.3 1.9 %collective-permute-start.10 = (bf16[16,6272]{1,0:T(8,128)(2,1)}, bf16[16,6272]{1,0:T(8,128)(2,1)}, u32[]{:S(2)}, u32[]{:S(2)}) collective-permute-start(bf16[16,6272]{1,0:T(8,128)(2,1)} %concatenate.28), channel_id=1, source_target_pairs={{0,2},{2,4},{4,6},{6,8},{8,10},{10,12},{12,14},{14,0},{1,3},{3,5},... | collective-permute-start | bytes 602120 | tf_op jit(solution)/shard_map/ppermute | solution.py:109
  160.3 5.0 %collective-permute-done.10 = bf16[16,6272]{1,0:T(8,128)(2,1)} collective-permute-done((bf16[16,6272]{1,0:T(8,128)(2,1)}, bf16[16,6272]{1,0:T(8,128)(2,1)}, u32[]{:S(2)}, u32[]{:S(2)}) %collective-permute-start.10) | collective-permute-done | bytes 200736 | tf_op jit(solution)/shard_map/ppermute | solution.py:109
  166.4 1.8 %fusion.14 = bf16[16,6144]{1,0:T(8,128)(2,1)} fusion(f32[8,16,6144]{2,1,0:T(8,128)S(1)} %convert_add_fusion, s32[]{:T(128)S(6)} %select_n.111, bf16[16,6272]{1,0:T(8,128)(2,1)} %collective-permute-done.13, bf16[16,6272]{1,0:T(8,128)(2,1)} %collective-permute-done.10, f32[16]{0:T(128)S(1)} %rsqrt_bitcast_fusion), kind=kLoop, calls=%fused_computation.27 | loop fusion | flops 589824 | bytes 983108 | tf_op jit(solution)/shard_map/convert_element_type | solution.py:146
  (94 shorter events, 29.6 us)
Async XLA Ops:
  0.0 50.5 %copy-start = (bf16[256,512]{1,0:T(8,128)(2,1)S(1)}, bf16[256,512]{1,0:T(8,128)(2,1)}, u32[]{:S(2)}) copy-start(bf16[256,512]{1,0:T(8,128)(2,1)} %param.7) | copy-start | bytes 786436
  0.0 50.5 %copy-start.2 = (bf16[256,512]{1,0:T(8,128)(2,1)S(1)}, bf16[256,512]{1,0:T(8,128)(2,1)}, u32[]{:S(2)}) copy-start(bf16[256,512]{1,0:T(8,128)(2,1)} %param.9) | copy-start | bytes 786436
  3.1 67.6 %copy-start.3 = (bf16[256,512]{1,0:T(8,128)(2,1)S(1)}, bf16[256,512]{1,0:T(8,128)(2,1)}, u32[]{:S(2)}) copy-start(bf16[256,512]{1,0:T(8,128)(2,1)} %param.10) | copy-start | bytes 786436
  3.1 6.3 %collective-permute-start = (bf16[4,128,128]{2,1,0:T(8,128)(2,1)S(1)}, bf16[4,128,128]{2,1,0:T(8,128)(2,1)S(1)}, u32[]{:S(2)}, u32[]{:S(2)}) collective-permute-start(bf16[4,128,128]{2,1,0:T(8,128)(2,1)S(1)} %get-tuple-element.60), channel_id=1, source_target_pairs={{0,16},{16,32},{32,48},{48,64},{64,80},{80,96},{96,112},{112,128},... | collective-permute-start | bytes 393224 | tf_op jit(solution)/shard_map/ppermute | solution.py:48
  9.5 7.4 %collective-permute-start.1 = (bf16[4,128,128]{2,1,0:T(8,128)(2,1)S(1)}, bf16[4,128,128]{2,1,0:T(8,128)(2,1)S(1)}, u32[]{:S(2)}, u32[]{:S(2)}) collective-permute-start(bf16[4,128,128]{2,1,0:T(8,128)(2,1)S(1)} %fusion.44), channel_id=1, source_target_pairs={{0,32},{16,48},{32,64},{48,80},{64,96},{80,112},{96,128},{112,144}... | collective-permute-start | bytes 393224 | tf_op jit(solution)/shard_map/ppermute | solution.py:48
  17.0 12.4 %collective-permute-start.2 = (bf16[4,128,128]{2,1,0:T(8,128)(2,1)S(1)}, bf16[4,128,128]{2,1,0:T(8,128)(2,1)S(1)}, u32[]{:S(2)}, u32[]{:S(2)}) collective-permute-start(bf16[4,128,128]{2,1,0:T(8,128)(2,1)S(1)} %get-tuple-element.19), channel_id=1, source_target_pairs={{0,64},{16,80},{32,96},{48,112},{64,128},{80,144},{96,160},{112,17... | collective-permute-start | bytes 393224 | tf_op jit(solution)/shard_map/ppermute | solution.py:48
  29.4 43.2 %copy-start.4 = (f32[512]{0:T(512)S(1)}, f32[512]{0:T(512)}, u32[]{:S(2)}) copy-start(f32[512]{0:T(512)} %param.12) | copy-start | bytes 6148
  29.5 10.7 %collective-permute-start.3 = (bf16[4,128,128]{2,1,0:T(8,128)(2,1)S(1)}, bf16[4,128,128]{2,1,0:T(8,128)(2,1)S(1)}, u32[]{:S(2)}, u32[]{:S(2)}) collective-permute-start(bf16[4,128,128]{2,1,0:T(8,128)(2,1)S(1)} %fusion.45), channel_id=1, source_target_pairs={{0,128},{16,144},{32,160},{48,176},{64,192},{80,208},{96,224},{112... | collective-permute-start | bytes 393224 | tf_op jit(solution)/shard_map/ppermute | solution.py:48
  40.3 12.0 %collective-permute-start.4 = (bf16[4,128,128]{2,1,0:T(8,128)(2,1)S(1)}, bf16[4,128,128]{2,1,0:T(8,128)(2,1)S(1)}, u32[]{:S(2)}, u32[]{:S(2)}) collective-permute-start(bf16[4,128,128]{2,1,0:T(8,128)(2,1)S(1)} %fusion.73), channel_id=1, source_target_pairs={{0,256},{16,272},{32,288},{48,304},{64,320},{80,336},{96,352},{112... | collective-permute-start | bytes 393224 | tf_op jit(solution)/shard_map/ppermute | solution.py:48
  52.5 20.1 %collective-permute-start.5 = (bf16[4,128,128]{2,1,0:T(8,128)(2,1)S(1)}, bf16[4,128,128]{2,1,0:T(8,128)(2,1)S(1)}, u32[]{:S(2)}, u32[]{:S(2)}) collective-permute-start(bf16[4,128,128]{2,1,0:T(8,128)(2,1)S(1)} %add_convert_fusion), channel_id=1, source_target_pairs={{0,512},{16,528},{32,544},{48,560},{64,576},{80,592},{96,608},{112... | collective-permute-start | bytes 393224 | tf_op jit(solution)/shard_map/ppermute | solution.py:48
  79.7 8.9 %collective-permute-start.6 = (bf16[8,16,6272]{2,1,0:T(8,128)(2,1)}, bf16[8,16,6272]{2,1,0:T(8,128)(2,1)S(1)}, u32[]{:S(2)}, u32[]{:S(2)}) collective-permute-start(bf16[8,16,6272]{2,1,0:T(8,128)(2,1)} %concatenate.24), channel_id=1, source_target_pairs={{0,1},{1,0},{2,3},{3,2},{4,5},{5,4},{6,7},{7,6},{8,9},{9,8},{10,11... | collective-permute-start | bytes 4816904 | tf_op jit(solution)/shard_map/ppermute | solution.py:83
  88.6 1.2 copy-start.1
  94.3 11.6 %collective-permute-start.7 = (bf16[16,6272]{1,0:T(8,128)(2,1)}, bf16[16,6272]{1,0:T(8,128)(2,1)}, u32[]{:S(2)}, u32[]{:S(2)}) collective-permute-start(bf16[16,6272]{1,0:T(8,128)(2,1)} %concatenate.25), channel_id=1, source_target_pairs={{0,2},{2,4},{4,6},{6,8},{8,10},{10,12},{12,14},{14,0},{1,3},{3,5},... | collective-permute-start | bytes 602120 | tf_op jit(solution)/shard_map/ppermute | solution.py:109
  110.4 9.4 %collective-permute-start.8 = (bf16[16,6272]{1,0:T(8,128)(2,1)}, bf16[16,6272]{1,0:T(8,128)(2,1)}, u32[]{:S(2)}, u32[]{:S(2)}) collective-permute-start(bf16[16,6272]{1,0:T(8,128)(2,1)} %concatenate.26), channel_id=1, source_target_pairs={{0,2},{2,4},{4,6},{6,8},{8,10},{10,12},{12,14},{14,0},{1,3},{3,5},... | collective-permute-start | bytes 602120 | tf_op jit(solution)/shard_map/ppermute | solution.py:109
  122.6 7.2 %collective-permute-start.11 = (bf16[16,6272]{1,0:T(8,128)(2,1)}, bf16[16,6272]{1,0:T(8,128)(2,1)}, u32[]{:S(2)}, u32[]{:S(2)}) collective-permute-start(bf16[16,6272]{1,0:T(8,128)(2,1)} %concatenate.29), channel_id=1, source_target_pairs={{0,14},{2,0},{4,2},{6,4},{8,6},{10,8},{12,10},{14,12},{1,15},{3,1}... | collective-permute-start | bytes 602120 | tf_op jit(solution)/shard_map/ppermute | solution.py:113
  133.3 9.4 %collective-permute-start.9 = (bf16[16,6272]{1,0:T(8,128)(2,1)}, bf16[16,6272]{1,0:T(8,128)(2,1)}, u32[]{:S(2)}, u32[]{:S(2)}) collective-permute-start(bf16[16,6272]{1,0:T(8,128)(2,1)} %concatenate.27), channel_id=1, source_target_pairs={{0,2},{2,4},{4,6},{6,8},{8,10},{10,12},{12,14},{14,0},{1,3},{3,5},... | collective-permute-start | bytes 602120 | tf_op jit(solution)/shard_map/ppermute | solution.py:109
  138.2 7.5 %collective-permute-start.12 = (bf16[16,6272]{1,0:T(8,128)(2,1)}, bf16[16,6272]{1,0:T(8,128)(2,1)}, u32[]{:S(2)}, u32[]{:S(2)}) collective-permute-start(bf16[16,6272]{1,0:T(8,128)(2,1)} %concatenate.30), channel_id=1, source_target_pairs={{0,14},{2,0},{4,2},{6,4},{8,6},{10,8},{12,10},{14,12},{1,15},{3,1}... | collective-permute-start | bytes 602120 | tf_op jit(solution)/shard_map/ppermute | solution.py:113
  150.4 8.8 %collective-permute-start.13 = (bf16[16,6272]{1,0:T(8,128)(2,1)}, bf16[16,6272]{1,0:T(8,128)(2,1)}, u32[]{:S(2)}, u32[]{:S(2)}) collective-permute-start(bf16[16,6272]{1,0:T(8,128)(2,1)} %concatenate.31), channel_id=1, source_target_pairs={{0,14},{2,0},{4,2},{6,4},{8,6},{10,8},{12,10},{14,12},{1,15},{3,1}... | collective-permute-start | bytes 602120 | tf_op jit(solution)/shard_map/ppermute | solution.py:113
  157.3 8.0 %collective-permute-start.10 = (bf16[16,6272]{1,0:T(8,128)(2,1)}, bf16[16,6272]{1,0:T(8,128)(2,1)}, u32[]{:S(2)}, u32[]{:S(2)}) collective-permute-start(bf16[16,6272]{1,0:T(8,128)(2,1)} %concatenate.28), channel_id=1, source_target_pairs={{0,2},{2,4},{4,6},{6,8},{8,10},{10,12},{12,14},{14,0},{1,3},{3,5},... | collective-permute-start | bytes 602120 | tf_op jit(solution)/shard_map/ppermute | solution.py:109

commit v10 on v8

--- a/solution.py
+++ b/solution.py
@@ -45,9 +45,17 @@
     shift = 1
     while shift < peers:
         decay = jnp.exp(-slopes * (tok_count * shift))
-        moved = lax.ppermute(
-            total.astype(jnp.bfloat16), axis, perm=[(i, i + shift) for i in range(peers - shift)]
-        )
+        sent = total.astype(jnp.bfloat16)
+        if shift * 2 == peers and lax.axis_size("sz") == 8:
+            half = sent.shape[0] // 2
+            ring = lax.axis_size("sz")
+            hop = ring // 2
+            direct = lax.ppermute(sent[:half], "sz", perm=[(z, z + hop) for z in range(hop)])
+            back = lax.ppermute(sent[half:], "sz", perm=[(z, (z - 1) % ring) for z in range(hop)])
+            back = lax.ppermute(back, "sz", perm=[((z - 1) % ring, z + hop) for z in range(hop)])
+            moved = jnp.concatenate([direct, back], axis=0)
+        else:
+            moved = lax.ppermute(sent, axis, perm=[(i, i + shift) for i in range(peers - shift)])
         part = decay[:, None, None] * moved.astype(jnp.float32)
         earlier = earlier + part
         total = total + part

time: 142 us -> 144 us (1.014)
  waiting for transfers between devices: 10.6 us -> 12.5 us
    ppermute x6 -> x8, waiting for transfers between devices: 10.6 us -> 12.5 us  [the longest x5 9.6 us: decayed_scan(): lax.ppermute(sent, axis, perm=[(i, i + shift) for i in range(peers - shif...]
    ppermute x6 -> x8, starting transfers between devices: 57.1 us -> 58.9 us  [the longest x5 38.8 us: decayed_scan(): lax.ppermute(sent, axis, perm=[(i, i + shift) for i in range(peers - shif...]
  transfers between devices with their start and end apart: 7 -> 9, of which waited for: 6 -> 6; matrix products, arithmetic and copies ran while one was open for 4% -> 3% of each run, Pallas kernels for 0% -> 0%
where the time goes in v10:
time: 144 us
  starting transfers between devices  62.6 us (43%)
  blocking collectives  47.9 us (33%)
  waiting for transfers between devices  12.5 us (9%)
  matrix products  9.94 us (7%)
  local copies, waits for them, and re-layouts  5.46 us (4%)
  other arithmetic  4.78 us (3%)
    all_to_all x1, blocking collectives, fsdp_reduce(): moved = lax.all_to_all(pack(mine, mine_sq), 'fy', 0, 0, tiled=True)  47.9 us
    ppermute x5, starting transfers between devices, decayed_scan(): lax.ppermute(sent, axis, perm=[(i, i + shift) for i in range(peers - shif...  38.8 us
    ppermute x1, starting transfers between devices, decayed_scan(): lax.ppermute(sent[half:], 'sz', perm=[(z, (z - 1) % ring) for z in range(...  13.8 us
    ppermute x5, waiting for transfers between devices, decayed_scan(): lax.ppermute(sent, axis, perm=[(i, i + shift) for i in range(peers - shif...  9.6 us
    dot_general x2, matrix products, project(): jnp.dot(block.reshape(-1, features), weight, preferred_element_type=jnp.f...  7.63 us
    ppermute x1, starting transfers between devices, decayed_scan(): lax.ppermute(sent[:half], 'sz', perm=[(z, z + hop) for z in range(hop)])  5.01 us
    ppermute x1, starting transfers between devices, fsdp_reduce(): sent = lax.ppermute(pack(give, give_sq), 'fc', perm=[(0, 1), (1, 0)])  3.74 us
    ppermute x1, waiting for transfers between devices, decayed_scan(): lax.ppermute(back, 'sz', perm=[((z - 1) % ring, z + hop) for z in range(h...  2.91 us
  transfers between devices with their start and end apart: 9, of which 6 were waited for; matrix products, arithmetic and copies ran while one was open for 3% of the time, Pallas kernels for 0%

profile of v10, /device:TPU:1, one launch (start us, length us, event | category | flops | bytes accessed | tf_op | source)
XLA Modules:
  0.0 143.6 jit_solution(7201646831309586801)
XLA Ops:
  0.0 0.7 multiply_exponential_fusion.3
  0.7 1.1 copy.63
  1.9 1.2 fusion.57
  3.1 4.0 %collective-permute-start = (bf16[4,128,128]{2,1,0:T(8,128)(2,1)S(1)}, bf16[4,128,128]{2,1,0:T(8,128)(2,1)S(1)}, u32[]{:S(2)}, u32[]{:S(2)}) collective-permute-start(bf16[4,128,128]{2,1,0:T(8,128)(2,1)S(1)} %get-tuple-element.31), channel_id=1, source_target_pairs={{0,16},{16,32},{32,48},{48,64},{64,80},{80,96},{96,112},{112,128},... | collective-permute-start | bytes 393224 | tf_op jit(solution)/shard_map/ppermute | solution.py:58
  7.1 2.1 %collective-permute-done = bf16[4,128,128]{2,1,0:T(8,128)(2,1)S(1)} collective-permute-done((bf16[4,128,128]{2,1,0:T(8,128)(2,1)S(1)}, bf16[4,128,128]{2,1,0:T(8,128)(2,1)S(1)}, u32[]{:S(2)}, u32[]{:S(2)}) %collective-permute-start) | collective-permute-done | bytes 131104 | tf_op jit(solution)/shard_map/ppermute | solution.py:58
  9.3 5.5 %collective-permute-start.1 = (bf16[4,128,128]{2,1,0:T(8,128)(2,1)S(1)}, bf16[4,128,128]{2,1,0:T(8,128)(2,1)S(1)}, u32[]{:S(2)}, u32[]{:S(2)}) collective-permute-start(bf16[4,128,128]{2,1,0:T(8,128)(2,1)S(1)} %fusion.35), channel_id=1, source_target_pairs={{0,32},{16,48},{32,64},{48,80},{64,96},{80,112},{96,128},{112,144}... | collective-permute-start | bytes 393224 | tf_op jit(solution)/shard_map/ppermute | solution.py:58
  14.8 1.9 %collective-permute-done.1 = bf16[4,128,128]{2,1,0:T(8,128)(2,1)S(1)} collective-permute-done((bf16[4,128,128]{2,1,0:T(8,128)(2,1)S(1)}, bf16[4,128,128]{2,1,0:T(8,128)(2,1)S(1)}, u32[]{:S(2)}, u32[]{:S(2)}) %collective-permute-start.1) | collective-permute-done | bytes 131104 | tf_op jit(solution)/shard_map/ppermute | solution.py:58
  16.8 10.5 %collective-permute-start.2 = (bf16[4,128,128]{2,1,0:T(8,128)(2,1)S(1)}, bf16[4,128,128]{2,1,0:T(8,128)(2,1)S(1)}, u32[]{:S(2)}, u32[]{:S(2)}) collective-permute-start(bf16[4,128,128]{2,1,0:T(8,128)(2,1)S(1)} %get-tuple-element.9), channel_id=1, source_target_pairs={{0,64},{16,80},{32,96},{48,112},{64,128},{80,144},{96,160},{112,17... | collective-permute-start | bytes 393224 | tf_op jit(solution)/shard_map/ppermute | solution.py:58
  27.3 1.9 %collective-permute-done.2 = bf16[4,128,128]{2,1,0:T(8,128)(2,1)S(1)} collective-permute-done((bf16[4,128,128]{2,1,0:T(8,128)(2,1)S(1)}, bf16[4,128,128]{2,1,0:T(8,128)(2,1)S(1)}, u32[]{:S(2)}, u32[]{:S(2)}) %collective-permute-start.2) | collective-permute-done | bytes 131104 | tf_op jit(solution)/shard_map/ppermute | solution.py:58
  29.3 8.8 %collective-permute-start.3 = (bf16[4,128,128]{2,1,0:T(8,128)(2,1)S(1)}, bf16[4,128,128]{2,1,0:T(8,128)(2,1)S(1)}, u32[]{:S(2)}, u32[]{:S(2)}) collective-permute-start(bf16[4,128,128]{2,1,0:T(8,128)(2,1)S(1)} %fusion.36), channel_id=1, source_target_pairs={{0,128},{16,144},{32,160},{48,176},{64,192},{80,208},{96,224},{112... | collective-permute-start | bytes 393224 | tf_op jit(solution)/shard_map/ppermute | solution.py:58
  38.2 1.8 %collective-permute-done.3 = bf16[4,128,128]{2,1,0:T(8,128)(2,1)S(1)} collective-permute-done((bf16[4,128,128]{2,1,0:T(8,128)(2,1)S(1)}, bf16[4,128,128]{2,1,0:T(8,128)(2,1)S(1)}, u32[]{:S(2)}, u32[]{:S(2)}) %collective-permute-start.3) | collective-permute-done | bytes 131104 | tf_op jit(solution)/shard_map/ppermute | solution.py:58
  40.2 10.1 %collective-permute-start.4 = (bf16[4,128,128]{2,1,0:T(8,128)(2,1)S(1)}, bf16[4,128,128]{2,1,0:T(8,128)(2,1)S(1)}, u32[]{:S(2)}, u32[]{:S(2)}) collective-permute-start(bf16[4,128,128]{2,1,0:T(8,128)(2,1)S(1)} %fusion.52), channel_id=1, source_target_pairs={{0,256},{16,272},{32,288},{48,304},{64,320},{80,336},{96,352},{112... | collective-permute-start | bytes 393224 | tf_op jit(solution)/shard_map/ppermute | solution.py:58
  50.4 1.8 %collective-permute-done.4 = bf16[4,128,128]{2,1,0:T(8,128)(2,1)S(1)} collective-permute-done((bf16[4,128,128]{2,1,0:T(8,128)(2,1)S(1)}, bf16[4,128,128]{2,1,0:T(8,128)(2,1)S(1)}, u32[]{:S(2)}, u32[]{:S(2)}) %collective-permute-start.4) | collective-permute-done | bytes 131104 | tf_op jit(solution)/shard_map/ppermute | solution.py:58
  52.4 13.8 %collective-permute-start.6 = (bf16[2,128,128]{2,1,0:T(8,128)(2,1)S(1)}, bf16[2,128,128]{2,1,0:T(8,128)(2,1)S(1)}, u32[]{:S(2)}, u32[]{:S(2)}) collective-permute-start(bf16[2,128,128]{2,1,0:T(8,128)(2,1)S(1)} %get-tuple-element.18), channel_id=1, source_target_pairs={{0,896},{128,0},{256,128},{384,256},{1,897},{129,1},{257,129},{385... | collective-permute-start | bytes 196616 | tf_op jit(solution)/shard_map/ppermute | solution.py:54
  66.2 0.5 convolution_bitcast_fusion.1
  66.8 5.0 %collective-permute-start.5 = (bf16[2,128,128]{2,1,0:T(8,128)(2,1)S(1)}, bf16[2,128,128]{2,1,0:T(8,128)(2,1)S(1)}, u32[]{:S(2)}, u32[]{:S(2)}) collective-permute-start(bf16[2,128,128]{2,1,0:T(8,128)(2,1)S(1)} %get-tuple-element.17), channel_id=1, source_target_pairs={{0,512},{128,640},{256,768},{384,896},{1,513},{129,641},{257,769},... | collective-permute-start | bytes 196616 | tf_op jit(solution)/shard_map/ppermute | solution.py:53
  71.8 1.3 collective-permute-start.7
  73.3 0.2 copy.49
  73.5 2.9 %collective-permute-done.7 = bf16[2,128,128]{2,1,0:T(8,128)(2,1)S(1)} collective-permute-done((bf16[2,128,128]{2,1,0:T(8,128)(2,1)S(1)}, bf16[2,128,128]{2,1,0:T(8,128)(2,1)S(1)}, u32[]{:S(2)}, u32[]{:S(2)}) %collective-permute-start.7) | collective-permute-done | bytes 65568 | tf_op jit(solution)/shard_map/ppermute | solution.py:55
  76.4 0.6 multiply_reduce_fusion
  77.4 0.7 constant_dynamic-slice_fusion.2
  78.4 3.8 %convolution_convert_fusion = bf16[128,6144]{1,0:T(8,128)(2,1)S(1)} fusion(bf16[128,512]{1,0:T(8,128)(2,1)S(1)} %bitcast.59, bf16[512,6144]{1,0:T(8,128)(2,1)} %param.13), kind=kOutput, calls=%fused_computation | convolution fusion | flops 806092800 | bytes 7995392 | tf_op jit(solution)/shard_map/dot_general | solution.py:86
  82.2 0.5 concatenate.10
  82.7 3.7 %collective-permute-start.8 = (bf16[8,16,6272]{2,1,0:T(8,128)(2,1)S(1)}, bf16[8,16,6272]{2,1,0:T(8,128)(2,1)S(1)}, u32[]{:S(2)}, u32[]{:S(2)}) collective-permute-start(bf16[8,16,6272]{2,1,0:T(8,128)(2,1)S(1)} %concatenate.10), channel_id=1, source_target_pairs={{0,1},{1,0},{2,3},{3,2},{4,5},{5,4},{6,7},{7,6},{8,9},{9,8},{10,11... | collective-permute-start | bytes 4816904 | tf_op jit(solution)/shard_map/ppermute | solution.py:91
  86.5 3.9 %convolution_convert_fusion.1 = bf16[128,6144]{1,0:T(8,128)(2,1)S(1)} fusion(bf16[128,512]{1,0:T(8,128)(2,1)} %bitcast.58, bf16[512,6144]{1,0:T(8,128)(2,1)} %param.13), kind=kOutput, calls=%fused_computation.1 | convolution fusion | flops 806092800 | bytes 7995392 | tf_op jit(solution)/shard_map/dot_general | solution.py:86
  90.3 1.2 copy-done.1
  92.1 1.8 %fusion = bf16[8,16,6144]{2,1,0:T(8,128)(2,1)S(1)} fusion(bf16[8,16,6144]{2,1,0:T(8,128)(2,1)S(1)} %bitcast.54, bf16[8,16,6272]{2,1,0:T(8,128)(2,1)} %copy-done.1), kind=kLoop, calls=%fused_computation.3 | loop fusion | flops 3145728 | bytes 4718592 | tf_op jit(solution)/shard_map/convert_element_type | solution.py:72
  93.9 0.5 concatenate.11
  94.5 47.9 %all_to_all.5 = bf16[8,16,6272]{2,1,0:T(8,128)(2,1)S(1)} all-to-all(bf16[8,16,6272]{2,1,0:T(8,128)(2,1)S(1)} %concatenate.11), channel_id=1, replica_groups=mesh['sz'=8,'sx'=8,'fy'=8,'fc'=2] {'fy'}, dimensions={0} | all-to-all | bytes 3211264 | tf_op jit(solution)/shard_map/all_to_all | solution.py:97
  142.4 0.2 add_reduce_fusion
  142.6 0.2 convert_reduce_fusion
  142.8 0.8 multiply_convert_fusion.2
  (40 shorter events, 2.4 us)
Async XLA Ops:
  0.0 66.2 %copy-start = (bf16[256,512]{1,0:T(8,128)(2,1)S(1)}, bf16[256,512]{1,0:T(8,128)(2,1)}, u32[]{:S(2)}) copy-start(bf16[256,512]{1,0:T(8,128)(2,1)} %param.7) | copy-start | bytes 786436
  3.1 6.1 %collective-permute-start = (bf16[4,128,128]{2,1,0:T(8,128)(2,1)S(1)}, bf16[4,128,128]{2,1,0:T(8,128)(2,1)S(1)}, u32[]{:S(2)}, u32[]{:S(2)}) collective-permute-start(bf16[4,128,128]{2,1,0:T(8,128)(2,1)S(1)} %get-tuple-element.31), channel_id=1, source_target_pairs={{0,16},{16,32},{32,48},{48,64},{64,80},{80,96},{96,112},{112,128},... | collective-permute-start | bytes 393224 | tf_op jit(solution)/shard_map/ppermute | solution.py:58
  9.3 7.4 %collective-permute-start.1 = (bf16[4,128,128]{2,1,0:T(8,128)(2,1)S(1)}, bf16[4,128,128]{2,1,0:T(8,128)(2,1)S(1)}, u32[]{:S(2)}, u32[]{:S(2)}) collective-permute-start(bf16[4,128,128]{2,1,0:T(8,128)(2,1)S(1)} %fusion.35), channel_id=1, source_target_pairs={{0,32},{16,48},{32,64},{48,80},{64,96},{80,112},{96,128},{112,144}... | collective-permute-start | bytes 393224 | tf_op jit(solution)/shard_map/ppermute | solution.py:58
  16.7 49.5 %copy-start.2 = (bf16[256,512]{1,0:T(8,128)(2,1)S(1)}, bf16[256,512]{1,0:T(8,128)(2,1)}, u32[]{:S(2)}) copy-start(bf16[256,512]{1,0:T(8,128)(2,1)} %param.9) | copy-start | bytes 786436
  16.8 12.4 %collective-permute-start.2 = (bf16[4,128,128]{2,1,0:T(8,128)(2,1)S(1)}, bf16[4,128,128]{2,1,0:T(8,128)(2,1)S(1)}, u32[]{:S(2)}, u32[]{:S(2)}) collective-permute-start(bf16[4,128,128]{2,1,0:T(8,128)(2,1)S(1)} %get-tuple-element.9), channel_id=1, source_target_pairs={{0,64},{16,80},{32,96},{48,112},{64,128},{80,144},{96,160},{112,17... | collective-permute-start | bytes 393224 | tf_op jit(solution)/shard_map/ppermute | solution.py:58
  29.3 10.7 %collective-permute-start.3 = (bf16[4,128,128]{2,1,0:T(8,128)(2,1)S(1)}, bf16[4,128,128]{2,1,0:T(8,128)(2,1)S(1)}, u32[]{:S(2)}, u32[]{:S(2)}) collective-permute-start(bf16[4,128,128]{2,1,0:T(8,128)(2,1)S(1)} %fusion.36), channel_id=1, source_target_pairs={{0,128},{16,144},{32,160},{48,176},{64,192},{80,208},{96,224},{112... | collective-permute-start | bytes 393224 | tf_op jit(solution)/shard_map/ppermute | solution.py:58
  40.2 12.0 %collective-permute-start.4 = (bf16[4,128,128]{2,1,0:T(8,128)(2,1)S(1)}, bf16[4,128,128]{2,1,0:T(8,128)(2,1)S(1)}, u32[]{:S(2)}, u32[]{:S(2)}) collective-permute-start(bf16[4,128,128]{2,1,0:T(8,128)(2,1)S(1)} %fusion.52), channel_id=1, source_target_pairs={{0,256},{16,272},{32,288},{48,304},{64,320},{80,336},{96,352},{112... | collective-permute-start | bytes 393224 | tf_op jit(solution)/shard_map/ppermute | solution.py:58
  52.2 20.9 %copy-start.3 = (bf16[256,512]{1,0:T(8,128)(2,1)S(1)}, bf16[256,512]{1,0:T(8,128)(2,1)}, u32[]{:S(2)}) copy-start(bf16[256,512]{1,0:T(8,128)(2,1)} %param.10) | copy-start | bytes 786436
  52.4 24.0 %copy-start.4 = (f32[512]{0:T(512)S(1)}, f32[512]{0:T(512)}, u32[]{:S(2)}) copy-start(f32[512]{0:T(512)} %param.12) | copy-start | bytes 6148
  52.4 19.4 %collective-permute-start.6 = (bf16[2,128,128]{2,1,0:T(8,128)(2,1)S(1)}, bf16[2,128,128]{2,1,0:T(8,128)(2,1)S(1)}, u32[]{:S(2)}, u32[]{:S(2)}) collective-permute-start(bf16[2,128,128]{2,1,0:T(8,128)(2,1)S(1)} %get-tuple-element.18), channel_id=1, source_target_pairs={{0,896},{128,0},{256,128},{384,256},{1,897},{129,1},{257,129},{385... | collective-permute-start | bytes 196616 | tf_op jit(solution)/shard_map/ppermute | solution.py:54
  66.8 6.7 %collective-permute-start.5 = (bf16[2,128,128]{2,1,0:T(8,128)(2,1)S(1)}, bf16[2,128,128]{2,1,0:T(8,128)(2,1)S(1)}, u32[]{:S(2)}, u32[]{:S(2)}) collective-permute-start(bf16[2,128,128]{2,1,0:T(8,128)(2,1)S(1)} %get-tuple-element.17), channel_id=1, source_target_pairs={{0,512},{128,640},{256,768},{384,896},{1,513},{129,641},{257,769},... | collective-permute-start | bytes 196616 | tf_op jit(solution)/shard_map/ppermute | solution.py:53
  71.8 4.6 %collective-permute-start.7 = (bf16[2,128,128]{2,1,0:T(8,128)(2,1)S(1)}, bf16[2,128,128]{2,1,0:T(8,128)(2,1)S(1)}, u32[]{:S(2)}, u32[]{:S(2)}) collective-permute-start(bf16[2,128,128]{2,1,0:T(8,128)(2,1)S(1)} %collective-permute-done.6), channel_id=1, source_target_pairs={{896,512},{0,640},{128,768},{256,896},{897,513},{1,641},{129,769},... | collective-permute-start | bytes 196616 | tf_op jit(solution)/shard_map/ppermute | solution.py:55
  82.7 7.6 %collective-permute-start.8 = (bf16[8,16,6272]{2,1,0:T(8,128)(2,1)S(1)}, bf16[8,16,6272]{2,1,0:T(8,128)(2,1)S(1)}, u32[]{:S(2)}, u32[]{:S(2)}) collective-permute-start(bf16[8,16,6272]{2,1,0:T(8,128)(2,1)S(1)} %concatenate.10), channel_id=1, source_target_pairs={{0,1},{1,0},{2,3},{3,2},{4,5},{5,4},{6,7},{7,6},{8,9},{9,8},{10,11... | collective-permute-start | bytes 4816904 | tf_op jit(solution)/shard_map/ppermute | solution.py:91
  90.3 1.2 copy-start.1

commit v11 on v8

--- a/solution.py
+++ b/solution.py
@@ -86,9 +86,9 @@
     got, got_sq = unpack(sent, lanes)
     mine = keep.astype(jnp.float32) + got
     mine_sq = keep_sq + got_sq
-    moved = lax.all_to_all(pack(mine, mine_sq), "fy", 0, 0, tiled=True)
-    values, sums = unpack(moved, lanes)
-    return jnp.sum(values, axis=0), jnp.sum(sums, axis=0)
+    values = lax.all_to_all(mine.astype(jnp.bfloat16), "fy", 0, 0, tiled=True)
+    sums = lax.all_to_all(mine_sq, "fy", 0, 0, tiled=True)
+    return jnp.sum(values.astype(jnp.float32), axis=0), jnp.sum(sums, axis=0)
 
 
 def per_device(query_act, key_act, value_act, gate_act, rate_index, norm_gain, out_weight):

time: 142 us -> 147 us (1.035)
  blocking collectives: 47.9 us -> 0 us
  waiting for transfers between devices: 10.6 us -> 53.5 us
  starting transfers between devices: 62.2 us -> 73.1 us
    all_to_all x1 -> x0, blocking collectives: 47.9 us -> none  [fsdp_reduce(): moved = lax.all_to_all(pack(mine, mine_sq), 'fy', 0, 0, tiled=True)]
    all_to_all x0 -> x2, waiting for transfers between devices: none -> 42.9 us  [the longest x1 38 us: fsdp_reduce(): values = lax.all_to_all(mine.astype(jnp.bfloat16), 'fy', 0, 0, tiled=True)]
    all_to_all x0 -> x2, starting transfers between devices: none -> 10.9 us  [the longest x1 7.3 us: fsdp_reduce(): sums = lax.all_to_all(mine_sq, 'fy', 0, 0, tiled=True)]
  transfers between devices with their start and end apart: 7 -> 9, of which waited for: 6 -> 8; matrix products, arithmetic and copies ran while one was open for 4% -> 4% of each run, Pallas kernels for 0% -> 0%
where the time goes in v11:
time: 147 us
  starting transfers between devices  73.1 us (50%)
  waiting for transfers between devices  53.5 us (36%)
  matrix products  10 us (7%)
  other arithmetic  4.99 us (3%)
  local copies, waits for them, and re-layouts  4.93 us (3%)
    ppermute x6, starting transfers between devices, decayed_scan(): lax.ppermute(total.astype(jnp.bfloat16), axis, perm=[(i, i + shift) for i...  57.1 us
    all_to_all x1, waiting for transfers between devices, fsdp_reduce(): values = lax.all_to_all(mine.astype(jnp.bfloat16), 'fy', 0, 0, tiled=True)  38 us
    ppermute x6, waiting for transfers between devices, decayed_scan(): lax.ppermute(total.astype(jnp.bfloat16), axis, perm=[(i, i + shift) for i...  10.6 us
    dot_general x2, matrix products, project(): jnp.dot(block.reshape(-1, features), weight, preferred_element_type=jnp.f...  7.72 us
    all_to_all x1, starting transfers between devices, fsdp_reduce(): sums = lax.all_to_all(mine_sq, 'fy', 0, 0, tiled=True)  7.3 us
    ppermute x1, starting transfers between devices, fsdp_reduce(): sent = lax.ppermute(pack(give, give_sq), 'fc', perm=[(0, 1), (1, 0)])  5.04 us
    all_to_all x1, waiting for transfers between devices, fsdp_reduce(): sums = lax.all_to_all(mine_sq, 'fy', 0, 0, tiled=True)  4.9 us
    all_to_all x1, starting transfers between devices, fsdp_reduce(): values = lax.all_to_all(mine.astype(jnp.bfloat16), 'fy', 0, 0, tiled=True)  3.58 us
  transfers between devices with their start and end apart: 9, of which 8 were waited for; matrix products, arithmetic and copies ran while one was open for 4% of the time, Pallas kernels for 0%

profile of v11, /device:TPU:1, one launch (start us, length us, event | category | flops | bytes accessed | tf_op | source)
XLA Modules:
  0.0 146.8 jit_solution(15251929835686201684)
XLA Ops:
  0.0 0.7 multiply_exponential_fusion.3
  0.7 1.1 copy.62
  1.9 1.2 fusion.51
  3.1 4.1 %collective-permute-start = (bf16[4,128,128]{2,1,0:T(8,128)(2,1)S(1)}, bf16[4,128,128]{2,1,0:T(8,128)(2,1)S(1)}, u32[]{:S(2)}, u32[]{:S(2)}) collective-permute-start(bf16[4,128,128]{2,1,0:T(8,128)(2,1)S(1)} %get-tuple-element.25), channel_id=1, source_target_pairs={{0,16},{16,32},{32,48},{48,64},{64,80},{80,96},{96,112},{112,128},... | collective-permute-start | bytes 393224 | tf_op jit(solution)/shard_map/ppermute | solution.py:48
  7.2 2.2 %collective-permute-done = bf16[4,128,128]{2,1,0:T(8,128)(2,1)S(1)} collective-permute-done((bf16[4,128,128]{2,1,0:T(8,128)(2,1)S(1)}, bf16[4,128,128]{2,1,0:T(8,128)(2,1)S(1)}, u32[]{:S(2)}, u32[]{:S(2)}) %collective-permute-start) | collective-permute-done | bytes 131104 | tf_op jit(solution)/shard_map/ppermute | solution.py:48
  9.5 5.5 %collective-permute-start.1 = (bf16[4,128,128]{2,1,0:T(8,128)(2,1)S(1)}, bf16[4,128,128]{2,1,0:T(8,128)(2,1)S(1)}, u32[]{:S(2)}, u32[]{:S(2)}) collective-permute-start(bf16[4,128,128]{2,1,0:T(8,128)(2,1)S(1)} %fusion.35), channel_id=1, source_target_pairs={{0,32},{16,48},{32,64},{48,80},{64,96},{80,112},{96,128},{112,144}... | collective-permute-start | bytes 393224 | tf_op jit(solution)/shard_map/ppermute | solution.py:48
  15.0 1.9 %collective-permute-done.1 = bf16[4,128,128]{2,1,0:T(8,128)(2,1)S(1)} collective-permute-done((bf16[4,128,128]{2,1,0:T(8,128)(2,1)S(1)}, bf16[4,128,128]{2,1,0:T(8,128)(2,1)S(1)}, u32[]{:S(2)}, u32[]{:S(2)}) %collective-permute-start.1) | collective-permute-done | bytes 131104 | tf_op jit(solution)/shard_map/ppermute | solution.py:48
  17.0 10.4 %collective-permute-start.2 = (bf16[4,128,128]{2,1,0:T(8,128)(2,1)S(1)}, bf16[4,128,128]{2,1,0:T(8,128)(2,1)S(1)}, u32[]{:S(2)}, u32[]{:S(2)}) collective-permute-start(bf16[4,128,128]{2,1,0:T(8,128)(2,1)S(1)} %get-tuple-element.9), channel_id=1, source_target_pairs={{0,64},{16,80},{32,96},{48,112},{64,128},{80,144},{96,160},{112,17... | collective-permute-start | bytes 393224 | tf_op jit(solution)/shard_map/ppermute | solution.py:48
  27.6 1.8 %collective-permute-done.2 = bf16[4,128,128]{2,1,0:T(8,128)(2,1)S(1)} collective-permute-done((bf16[4,128,128]{2,1,0:T(8,128)(2,1)S(1)}, bf16[4,128,128]{2,1,0:T(8,128)(2,1)S(1)}, u32[]{:S(2)}, u32[]{:S(2)}) %collective-permute-start.2) | collective-permute-done | bytes 131104 | tf_op jit(solution)/shard_map/ppermute | solution.py:48
  29.5 8.8 %collective-permute-start.3 = (bf16[4,128,128]{2,1,0:T(8,128)(2,1)S(1)}, bf16[4,128,128]{2,1,0:T(8,128)(2,1)S(1)}, u32[]{:S(2)}, u32[]{:S(2)}) collective-permute-start(bf16[4,128,128]{2,1,0:T(8,128)(2,1)S(1)} %fusion.36), channel_id=1, source_target_pairs={{0,128},{16,144},{32,160},{48,176},{64,192},{80,208},{96,224},{112... | collective-permute-start | bytes 393224 | tf_op jit(solution)/shard_map/ppermute | solution.py:48
  38.4 1.8 %collective-permute-done.3 = bf16[4,128,128]{2,1,0:T(8,128)(2,1)S(1)} collective-permute-done((bf16[4,128,128]{2,1,0:T(8,128)(2,1)S(1)}, bf16[4,128,128]{2,1,0:T(8,128)(2,1)S(1)}, u32[]{:S(2)}, u32[]{:S(2)}) %collective-permute-start.3) | collective-permute-done | bytes 131104 | tf_op jit(solution)/shard_map/ppermute | solution.py:48
  40.4 10.2 %collective-permute-start.4 = (bf16[4,128,128]{2,1,0:T(8,128)(2,1)S(1)}, bf16[4,128,128]{2,1,0:T(8,128)(2,1)S(1)}, u32[]{:S(2)}, u32[]{:S(2)}) collective-permute-start(bf16[4,128,128]{2,1,0:T(8,128)(2,1)S(1)} %fusion.47), channel_id=1, source_target_pairs={{0,256},{16,272},{32,288},{48,304},{64,320},{80,336},{96,352},{112... | collective-permute-start | bytes 393224 | tf_op jit(solution)/shard_map/ppermute | solution.py:48
  50.6 0.5 convolution_bitcast_fusion.1
  51.2 1.4 collective-permute-done.4
  52.7 18.1 %collective-permute-start.5 = (bf16[4,128,128]{2,1,0:T(8,128)(2,1)S(1)}, bf16[4,128,128]{2,1,0:T(8,128)(2,1)S(1)}, u32[]{:S(2)}, u32[]{:S(2)}) collective-permute-start(bf16[4,128,128]{2,1,0:T(8,128)(2,1)S(1)} %add_convert_fusion), channel_id=1, source_target_pairs={{0,512},{16,528},{32,544},{48,560},{64,576},{80,592},{96,608},{112... | collective-permute-start | bytes 393224 | tf_op jit(solution)/shard_map/ppermute | solution.py:48
  71.0 0.2 copy.49
  71.2 1.6 %collective-permute-done.5 = bf16[4,128,128]{2,1,0:T(8,128)(2,1)S(1)} collective-permute-done((bf16[4,128,128]{2,1,0:T(8,128)(2,1)S(1)}, bf16[4,128,128]{2,1,0:T(8,128)(2,1)S(1)}, u32[]{:S(2)}, u32[]{:S(2)}) %collective-permute-start.5) | collective-permute-done | bytes 131104 | tf_op jit(solution)/shard_map/ppermute | solution.py:48
  72.7 0.6 multiply_reduce_fusion
  73.4 0.2 copy.50
  74.1 0.7 constant_dynamic-slice_fusion.1
  74.7 3.9 %convolution_convert_fusion = bf16[128,6144]{1,0:T(8,128)(2,1)S(1)} fusion(bf16[128,512]{1,0:T(8,128)(2,1)S(1)} %bitcast.61, bf16[512,6144]{1,0:T(8,128)(2,1)} %param.13), kind=kOutput, calls=%fused_computation | convolution fusion | flops 806092800 | bytes 7995392 | tf_op jit(solution)/shard_map/dot_general | solution.py:78
  78.6 1.9 %concatenate.3 = bf16[8,16,6272]{2,1,0:T(8,128)(2,1)} concatenate(bf16[8,16,6144]{2,1,0:T(8,128)(2,1)S(1)} %bitcast.55, bf16[8,16,1]{2,1,0:T(8,128)(2,1)S(1)} %copy.51, bf16[8,16,1]{2,1,0:T(8,128)(2,1)S(1)} %copy.52, bf16[8,16,126]{2,1,0:T(8,128)(2,1)S(1)} %broadcast_in_dim.16), dimensions={2} | concatenate | bytes 3211264 | tf_op jit(solution)/shard_map/concatenate | solution.py:64
  80.6 5.0 %collective-permute-start.6 = (bf16[8,16,6272]{2,1,0:T(8,128)(2,1)}, bf16[8,16,6272]{2,1,0:T(8,128)(2,1)S(1)}, u32[]{:S(2)}, u32[]{:S(2)}) collective-permute-start(bf16[8,16,6272]{2,1,0:T(8,128)(2,1)} %concatenate.3), channel_id=1, source_target_pairs={{0,1},{1,0},{2,3},{3,2},{4,5},{5,4},{6,7},{7,6},{8,9},{9,8},{10,11... | collective-permute-start | bytes 4816904 | tf_op jit(solution)/shard_map/ppermute | solution.py:83
  85.6 3.9 %convolution_convert_fusion.1 = bf16[128,6144]{1,0:T(8,128)(2,1)S(1)} fusion(bf16[128,512]{1,0:T(8,128)(2,1)} %bitcast.60, bf16[512,6144]{1,0:T(8,128)(2,1)} %param.13), kind=kOutput, calls=%fused_computation.1 | convolution fusion | flops 806092800 | bytes 7995392 | tf_op jit(solution)/shard_map/dot_general | solution.py:78
  89.8 0.6 dynamic-slice_add_fusion
  90.5 7.3 %all-to-all-start.1 = ((f32[8,1,16]{2,1,0:T(1,128)}), f32[8,1,16]{2,1,0:T(1,128)S(1)}, u32[]{:S(2)}, u32[]{:S(2)}) async-start(f32[8,1,16]{2,1,0:T(1,128)} %dynamic-slice_add_fusion), calls=%async_computation.1 | async-start | bytes 8192 | tf_op jit(solution)/shard_map/all_to_all | solution.py:90
  97.8 1.6 %fusion = bf16[8,16,6144]{2,1,0:T(8,128)(2,1)} fusion(bf16[8,16,6144]{2,1,0:T(8,128)(2,1)S(1)} %bitcast.56, bf16[8,16,6272]{2,1,0:T(8,128)(2,1)S(1)} %collective-permute-done.6), kind=kLoop, calls=%fused_computation.3 | loop fusion | flops 3145728 | bytes 4718592 | tf_op jit(solution)/shard_map/convert_element_type | solution.py:89
  99.3 4.9 %all-to-all-done.1 = f32[8,1,16]{2,1,0:T(1,128)S(1)} async-done(((f32[8,1,16]{2,1,0:T(1,128)}), f32[8,1,16]{2,1,0:T(1,128)S(1)}, u32[]{:S(2)}, u32[]{:S(2)}) %all-to-all-start.1) | async-done | bytes 544 | tf_op jit(solution)/shard_map/all_to_all | solution.py:90
  104.2 3.6 %all-to-all-start = ((bf16[8,16,6144]{2,1,0:T(8,128)(2,1)}), bf16[8,16,6144]{2,1,0:T(8,128)(2,1)S(1)}, u32[]{:S(2)}, u32[]{:S(2)}) async-start(bf16[8,16,6144]{2,1,0:T(8,128)(2,1)} %fusion), calls=%async_computation | async-start | bytes 3145728 | tf_op jit(solution)/shard_map/all_to_all | solution.py:89
  107.8 38.0 %all-to-all-done = bf16[8,16,6144]{2,1,0:T(8,128)(2,1)S(1)} async-done(((bf16[8,16,6144]{2,1,0:T(8,128)(2,1)}), bf16[8,16,6144]{2,1,0:T(8,128)(2,1)S(1)}, u32[]{:S(2)}, u32[]{:S(2)}) %all-to-all-start) | async-done | bytes 1572896 | tf_op jit(solution)/shard_map/all_to_all | solution.py:89
  145.9 0.2 convert_reduce_fusion
  146.1 0.8 multiply_convert_fusion.2
  (34 shorter events, 2.0 us)
Async XLA Ops:
  0.0 50.6 %copy-start = (bf16[256,512]{1,0:T(8,128)(2,1)S(1)}, bf16[256,512]{1,0:T(8,128)(2,1)}, u32[]{:S(2)}) copy-start(bf16[256,512]{1,0:T(8,128)(2,1)} %param.7) | copy-start | bytes 786436
  3.1 47.5 %copy-start.1 = (bf16[256,512]{1,0:T(8,128)(2,1)S(1)}, bf16[256,512]{1,0:T(8,128)(2,1)}, u32[]{:S(2)}) copy-start(bf16[256,512]{1,0:T(8,128)(2,1)} %param.9) | copy-start | bytes 786436
  3.1 6.3 %collective-permute-start = (bf16[4,128,128]{2,1,0:T(8,128)(2,1)S(1)}, bf16[4,128,128]{2,1,0:T(8,128)(2,1)S(1)}, u32[]{:S(2)}, u32[]{:S(2)}) collective-permute-start(bf16[4,128,128]{2,1,0:T(8,128)(2,1)S(1)} %get-tuple-element.25), channel_id=1, source_target_pairs={{0,16},{16,32},{32,48},{48,64},{64,80},{80,96},{96,112},{112,128},... | collective-permute-start | bytes 393224 | tf_op jit(solution)/shard_map/ppermute | solution.py:48
  9.5 7.4 %collective-permute-start.1 = (bf16[4,128,128]{2,1,0:T(8,128)(2,1)S(1)}, bf16[4,128,128]{2,1,0:T(8,128)(2,1)S(1)}, u32[]{:S(2)}, u32[]{:S(2)}) collective-permute-start(bf16[4,128,128]{2,1,0:T(8,128)(2,1)S(1)} %fusion.35), channel_id=1, source_target_pairs={{0,32},{16,48},{32,64},{48,80},{64,96},{80,112},{96,128},{112,144}... | collective-permute-start | bytes 393224 | tf_op jit(solution)/shard_map/ppermute | solution.py:48
  17.0 12.4 %collective-permute-start.2 = (bf16[4,128,128]{2,1,0:T(8,128)(2,1)S(1)}, bf16[4,128,128]{2,1,0:T(8,128)(2,1)S(1)}, u32[]{:S(2)}, u32[]{:S(2)}) collective-permute-start(bf16[4,128,128]{2,1,0:T(8,128)(2,1)S(1)} %get-tuple-element.9), channel_id=1, source_target_pairs={{0,64},{16,80},{32,96},{48,112},{64,128},{80,144},{96,160},{112,17... | collective-permute-start | bytes 393224 | tf_op jit(solution)/shard_map/ppermute | solution.py:48
  29.5 10.7 %collective-permute-start.3 = (bf16[4,128,128]{2,1,0:T(8,128)(2,1)S(1)}, bf16[4,128,128]{2,1,0:T(8,128)(2,1)S(1)}, u32[]{:S(2)}, u32[]{:S(2)}) collective-permute-start(bf16[4,128,128]{2,1,0:T(8,128)(2,1)S(1)} %fusion.36), channel_id=1, source_target_pairs={{0,128},{16,144},{32,160},{48,176},{64,192},{80,208},{96,224},{112... | collective-permute-start | bytes 393224 | tf_op jit(solution)/shard_map/ppermute | solution.py:48
  40.4 30.5 %copy-start.2 = (bf16[256,512]{1,0:T(8,128)(2,1)S(1)}, bf16[256,512]{1,0:T(8,128)(2,1)}, u32[]{:S(2)}) copy-start(bf16[256,512]{1,0:T(8,128)(2,1)} %param.10) | copy-start | bytes 786436
  40.4 12.1 %collective-permute-start.4 = (bf16[4,128,128]{2,1,0:T(8,128)(2,1)S(1)}, bf16[4,128,128]{2,1,0:T(8,128)(2,1)S(1)}, u32[]{:S(2)}, u32[]{:S(2)}) collective-permute-start(bf16[4,128,128]{2,1,0:T(8,128)(2,1)S(1)} %fusion.47), channel_id=1, source_target_pairs={{0,256},{16,272},{32,288},{48,304},{64,320},{80,336},{96,352},{112... | collective-permute-start | bytes 393224 | tf_op jit(solution)/shard_map/ppermute | solution.py:48
  51.1 21.6 %copy-start.3 = (f32[512]{0:T(512)S(1)}, f32[512]{0:T(512)}, u32[]{:S(2)}) copy-start(f32[512]{0:T(512)} %param.12) | copy-start | bytes 6148
  52.7 20.1 %collective-permute-start.5 = (bf16[4,128,128]{2,1,0:T(8,128)(2,1)S(1)}, bf16[4,128,128]{2,1,0:T(8,128)(2,1)S(1)}, u32[]{:S(2)}, u32[]{:S(2)}) collective-permute-start(bf16[4,128,128]{2,1,0:T(8,128)(2,1)S(1)} %add_convert_fusion), channel_id=1, source_target_pairs={{0,512},{16,528},{32,544},{48,560},{64,576},{80,592},{96,608},{112... | collective-permute-start | bytes 393224 | tf_op jit(solution)/shard_map/ppermute | solution.py:48
  80.6 8.9 %collective-permute-start.6 = (bf16[8,16,6272]{2,1,0:T(8,128)(2,1)}, bf16[8,16,6272]{2,1,0:T(8,128)(2,1)S(1)}, u32[]{:S(2)}, u32[]{:S(2)}) collective-permute-start(bf16[8,16,6272]{2,1,0:T(8,128)(2,1)} %concatenate.3), channel_id=1, source_target_pairs={{0,1},{1,0},{2,3},{3,2},{4,5},{5,4},{6,7},{7,6},{8,9},{9,8},{10,11... | collective-permute-start | bytes 4816904 | tf_op jit(solution)/shard_map/ppermute | solution.py:83
  90.5 13.8 %all-to-all-start.1 = ((f32[8,1,16]{2,1,0:T(1,128)}), f32[8,1,16]{2,1,0:T(1,128)S(1)}, u32[]{:S(2)}, u32[]{:S(2)}) async-start(f32[8,1,16]{2,1,0:T(1,128)} %dynamic-slice_add_fusion), calls=%async_computation.1 | async-start | bytes 8192 | tf_op jit(solution)/shard_map/all_to_all | solution.py:90
  104.2 41.6 %all-to-all-start = ((bf16[8,16,6144]{2,1,0:T(8,128)(2,1)}), bf16[8,16,6144]{2,1,0:T(8,128)(2,1)S(1)}, u32[]{:S(2)}, u32[]{:S(2)}) async-start(bf16[8,16,6144]{2,1,0:T(8,128)(2,1)} %fusion), calls=%async_computation | async-start | bytes 3145728 | tf_op jit(solution)/shard_map/all_to_all | solution.py:89

commit v12 on v11

--- a/solution.py
+++ b/solution.py
@@ -86,9 +86,12 @@
     got, got_sq = unpack(sent, lanes)
     mine = keep.astype(jnp.float32) + got
     mine_sq = keep_sq + got_sq
-    values = lax.all_to_all(mine.astype(jnp.bfloat16), "fy", 0, 0, tiled=True)
-    sums = lax.all_to_all(mine_sq, "fy", 0, 0, tiled=True)
-    return jnp.sum(values.astype(jnp.float32), axis=0), jnp.sum(sums, axis=0)
+    half = lanes // 2
+    first = lax.all_to_all(pack(mine[:, :, :half], mine_sq), "fy", 0, 0, tiled=True)
+    second = lax.all_to_all(mine[:, :, half:].astype(jnp.bfloat16), "fy", 0, 0, tiled=True)
+    values, sums = unpack(first, half)
+    out = jnp.concatenate([jnp.sum(values, axis=0), jnp.sum(second.astype(jnp.float32), axis=0)], axis=-1)
+    return out, jnp.sum(sums, axis=0)
 
 
 def per_device(query_act, key_act, value_act, gate_act, rate_index, norm_gain, out_weight):

time: 147 us -> 151 us (1.027)
  waiting for transfers between devices: 53.5 us -> 56.7 us
  local copies, waits for them, and re-layouts: 4.93 us -> 7.31 us
  other arithmetic: 4.99 us -> 3.39 us
    all_to_all x2, waiting for transfers between devices: 42.9 us -> 46.1 us  [the longest x1 24.1 us: fsdp_reduce(): lax.all_to_all(pack(mine[:, :, :half], mine_sq), 'fy', 0, 0, tiled=True)]
    convert_element_type x1 -> x0, other arithmetic: 1.56 us -> none  [fsdp_reduce(): values = lax.all_to_all(mine.astype(jnp.bfloat16), 'fy', 0, 0, tiled=True)]
    concatenate x1 -> x2, local copies, waits for them, and re-layouts: 1.94 us -> 3.02 us  [pack(): return jnp.concatenate([values.astype(jnp.bfloat16), extra], axis=-1)]
where the time goes in v12:
time: 151 us
  starting transfers between devices  73 us (48%)
  waiting for transfers between devices  56.7 us (38%)
  matrix products  9.94 us (7%)
  local copies, waits for them, and re-layouts  7.31 us (5%)
  other arithmetic  3.39 us (2%)
    ppermute x6, starting transfers between devices, decayed_scan(): lax.ppermute(total.astype(jnp.bfloat16), axis, perm=[(i, i + shift) for i...  57.1 us
    all_to_all x1, waiting for transfers between devices, fsdp_reduce(): lax.all_to_all(pack(mine[:, :, :half], mine_sq), 'fy', 0, 0, tiled=True)  24.1 us
    all_to_all x1, waiting for transfers between devices, fsdp_reduce(): lax.all_to_all(mine[:, :, half:].astype(jnp.bfloat16), 'fy', 0, 0, tiled=...  21.9 us
    ppermute x6, waiting for transfers between devices, decayed_scan(): lax.ppermute(total.astype(jnp.bfloat16), axis, perm=[(i, i + shift) for i...  10.6 us
    dot_general x2, matrix products, project(): jnp.dot(block.reshape(-1, features), weight, preferred_element_type=jnp.f...  7.63 us
    all_to_all x1, starting transfers between devices, fsdp_reduce(): lax.all_to_all(mine[:, :, half:].astype(jnp.bfloat16), 'fy', 0, 0, tiled=...  7.3 us
    ppermute x1, starting transfers between devices, fsdp_reduce(): sent = lax.ppermute(pack(give, give_sq), 'fc', perm=[(0, 1), (1, 0)])  5.05 us
    all_to_all x1, starting transfers between devices, fsdp_reduce(): lax.all_to_all(pack(mine[:, :, :half], mine_sq), 'fy', 0, 0, tiled=True)  3.55 us
  transfers between devices with their start and end apart: 9, of which 8 were waited for; matrix products, arithmetic and copies ran while one was open for 4% of the time, Pallas kernels for 0%

profile of v12, /device:TPU:1, one launch (start us, length us, event | category | flops | bytes accessed | tf_op | source)
XLA Modules:
  0.0 150.7 jit_solution(11365826339677718566)
XLA Ops:
  0.0 0.7 multiply_exponential_fusion.3
  0.7 1.1 copy.67
  1.9 1.2 fusion.54
  3.1 4.1 %collective-permute-start = (bf16[4,128,128]{2,1,0:T(8,128)(2,1)S(1)}, bf16[4,128,128]{2,1,0:T(8,128)(2,1)S(1)}, u32[]{:S(2)}, u32[]{:S(2)}) collective-permute-start(bf16[4,128,128]{2,1,0:T(8,128)(2,1)S(1)} %get-tuple-element.31), channel_id=1, source_target_pairs={{0,16},{16,32},{32,48},{48,64},{64,80},{80,96},{96,112},{112,128},... | collective-permute-start | bytes 393224 | tf_op jit(solution)/shard_map/ppermute | solution.py:48
  7.2 2.2 %collective-permute-done = bf16[4,128,128]{2,1,0:T(8,128)(2,1)S(1)} collective-permute-done((bf16[4,128,128]{2,1,0:T(8,128)(2,1)S(1)}, bf16[4,128,128]{2,1,0:T(8,128)(2,1)S(1)}, u32[]{:S(2)}, u32[]{:S(2)}) %collective-permute-start) | collective-permute-done | bytes 131104 | tf_op jit(solution)/shard_map/ppermute | solution.py:48
  9.5 5.5 %collective-permute-start.1 = (bf16[4,128,128]{2,1,0:T(8,128)(2,1)S(1)}, bf16[4,128,128]{2,1,0:T(8,128)(2,1)S(1)}, u32[]{:S(2)}, u32[]{:S(2)}) collective-permute-start(bf16[4,128,128]{2,1,0:T(8,128)(2,1)S(1)} %fusion.36), channel_id=1, source_target_pairs={{0,32},{16,48},{32,64},{48,80},{64,96},{80,112},{96,128},{112,144}... | collective-permute-start | bytes 393224 | tf_op jit(solution)/shard_map/ppermute | solution.py:48
  15.0 1.9 %collective-permute-done.1 = bf16[4,128,128]{2,1,0:T(8,128)(2,1)S(1)} collective-permute-done((bf16[4,128,128]{2,1,0:T(8,128)(2,1)S(1)}, bf16[4,128,128]{2,1,0:T(8,128)(2,1)S(1)}, u32[]{:S(2)}, u32[]{:S(2)}) %collective-permute-start.1) | collective-permute-done | bytes 131104 | tf_op jit(solution)/shard_map/ppermute | solution.py:48
  17.0 10.4 %collective-permute-start.2 = (bf16[4,128,128]{2,1,0:T(8,128)(2,1)S(1)}, bf16[4,128,128]{2,1,0:T(8,128)(2,1)S(1)}, u32[]{:S(2)}, u32[]{:S(2)}) collective-permute-start(bf16[4,128,128]{2,1,0:T(8,128)(2,1)S(1)} %get-tuple-element.9), channel_id=1, source_target_pairs={{0,64},{16,80},{32,96},{48,112},{64,128},{80,144},{96,160},{112,17... | collective-permute-start | bytes 393224 | tf_op jit(solution)/shard_map/ppermute | solution.py:48
  27.6 1.8 %collective-permute-done.2 = bf16[4,128,128]{2,1,0:T(8,128)(2,1)S(1)} collective-permute-done((bf16[4,128,128]{2,1,0:T(8,128)(2,1)S(1)}, bf16[4,128,128]{2,1,0:T(8,128)(2,1)S(1)}, u32[]{:S(2)}, u32[]{:S(2)}) %collective-permute-start.2) | collective-permute-done | bytes 131104 | tf_op jit(solution)/shard_map/ppermute | solution.py:48
  29.5 8.8 %collective-permute-start.3 = (bf16[4,128,128]{2,1,0:T(8,128)(2,1)S(1)}, bf16[4,128,128]{2,1,0:T(8,128)(2,1)S(1)}, u32[]{:S(2)}, u32[]{:S(2)}) collective-permute-start(bf16[4,128,128]{2,1,0:T(8,128)(2,1)S(1)} %fusion.37), channel_id=1, source_target_pairs={{0,128},{16,144},{32,160},{48,176},{64,192},{80,208},{96,224},{112... | collective-permute-start | bytes 393224 | tf_op jit(solution)/shard_map/ppermute | solution.py:48
  38.4 1.8 %collective-permute-done.3 = bf16[4,128,128]{2,1,0:T(8,128)(2,1)S(1)} collective-permute-done((bf16[4,128,128]{2,1,0:T(8,128)(2,1)S(1)}, bf16[4,128,128]{2,1,0:T(8,128)(2,1)S(1)}, u32[]{:S(2)}, u32[]{:S(2)}) %collective-permute-start.3) | collective-permute-done | bytes 131104 | tf_op jit(solution)/shard_map/ppermute | solution.py:48
  40.4 10.2 %collective-permute-start.4 = (bf16[4,128,128]{2,1,0:T(8,128)(2,1)S(1)}, bf16[4,128,128]{2,1,0:T(8,128)(2,1)S(1)}, u32[]{:S(2)}, u32[]{:S(2)}) collective-permute-start(bf16[4,128,128]{2,1,0:T(8,128)(2,1)S(1)} %fusion.49), channel_id=1, source_target_pairs={{0,256},{16,272},{32,288},{48,304},{64,320},{80,336},{96,352},{112... | collective-permute-start | bytes 393224 | tf_op jit(solution)/shard_map/ppermute | solution.py:48
  50.6 0.5 convolution_bitcast_fusion.1
  51.2 1.4 collective-permute-done.4
  52.7 18.1 %collective-permute-start.5 = (bf16[4,128,128]{2,1,0:T(8,128)(2,1)S(1)}, bf16[4,128,128]{2,1,0:T(8,128)(2,1)S(1)}, u32[]{:S(2)}, u32[]{:S(2)}) collective-permute-start(bf16[4,128,128]{2,1,0:T(8,128)(2,1)S(1)} %add_convert_fusion), channel_id=1, source_target_pairs={{0,512},{16,528},{32,544},{48,560},{64,576},{80,592},{96,608},{112... | collective-permute-start | bytes 393224 | tf_op jit(solution)/shard_map/ppermute | solution.py:48
  71.0 0.2 copy.50
  71.2 1.6 %collective-permute-done.5 = bf16[4,128,128]{2,1,0:T(8,128)(2,1)S(1)} collective-permute-done((bf16[4,128,128]{2,1,0:T(8,128)(2,1)S(1)}, bf16[4,128,128]{2,1,0:T(8,128)(2,1)S(1)}, u32[]{:S(2)}, u32[]{:S(2)}) %collective-permute-start.5) | collective-permute-done | bytes 131104 | tf_op jit(solution)/shard_map/ppermute | solution.py:48
  72.7 0.6 multiply_reduce_fusion
  73.7 0.7 constant_dynamic-slice_fusion.2
  74.7 3.8 %convolution_convert_fusion = bf16[128,6144]{1,0:T(8,128)(2,1)S(1)} fusion(bf16[128,512]{1,0:T(8,128)(2,1)S(1)} %bitcast.59, bf16[512,6144]{1,0:T(8,128)(2,1)} %param.13), kind=kOutput, calls=%fused_computation | convolution fusion | flops 806092800 | bytes 7995392 | tf_op jit(solution)/shard_map/dot_general | solution.py:78
  78.5 1.9 %concatenate.9 = bf16[8,16,6272]{2,1,0:T(8,128)(2,1)} concatenate(bf16[8,16,6144]{2,1,0:T(8,128)(2,1)S(1)} %bitcast.53, bf16[8,16,1]{2,1,0:T(8,128)(2,1)S(1)} %copy.52, bf16[8,16,1]{2,1,0:T(8,128)(2,1)S(1)} %copy.53, bf16[8,16,126]{2,1,0:T(8,128)(2,1)S(1)} %broadcast.161), dimensions={2} | concatenate | bytes 3211264 | tf_op jit(solution)/shard_map/concatenate | solution.py:64
  80.5 5.0 %collective-permute-start.6 = (bf16[8,16,6272]{2,1,0:T(8,128)(2,1)}, bf16[8,16,6272]{2,1,0:T(8,128)(2,1)S(1)}, u32[]{:S(2)}, u32[]{:S(2)}) collective-permute-start(bf16[8,16,6272]{2,1,0:T(8,128)(2,1)} %concatenate.9), channel_id=1, source_target_pairs={{0,1},{1,0},{2,3},{3,2},{4,5},{5,4},{6,7},{7,6},{8,9},{9,8},{10,11... | collective-permute-start | bytes 4816904 | tf_op jit(solution)/shard_map/ppermute | solution.py:83
  85.5 3.9 %convolution_convert_fusion.1 = bf16[128,6144]{1,0:T(8,128)(2,1)S(1)} fusion(bf16[128,512]{1,0:T(8,128)(2,1)} %bitcast.58, bf16[512,6144]{1,0:T(8,128)(2,1)} %param.13), kind=kOutput, calls=%fused_computation.1 | convolution fusion | flops 806092800 | bytes 7995392 | tf_op jit(solution)/shard_map/dot_general | solution.py:78
  89.4 0.4 fusion
  89.8 1.0 fusion.53
  90.8 7.3 %all-to-all-start.1 = ((bf16[8,16,3072]{2,1,0:T(8,128)(2,1)}), bf16[8,16,3072]{2,1,0:T(8,128)(2,1)S(1)}, u32[]{:S(2)}, u32[]{:S(2)}) async-start(bf16[8,16,3072]{2,1,0:T(8,128)(2,1)} %get-tuple-element.14), calls=%async_computation.1 | async-start | bytes 1572864 | tf_op jit(solution)/shard_map/all_to_all | solution.py:91
  98.8 1.1 concatenate.10
  99.8 21.9 %all-to-all-done.1 = bf16[8,16,3072]{2,1,0:T(8,128)(2,1)S(1)} async-done(((bf16[8,16,3072]{2,1,0:T(8,128)(2,1)}), bf16[8,16,3072]{2,1,0:T(8,128)(2,1)S(1)}, u32[]{:S(2)}, u32[]{:S(2)}) %all-to-all-start.1) | async-done | bytes 786464 | tf_op jit(solution)/shard_map/all_to_all | solution.py:91
  121.8 3.5 %all-to-all-start = ((bf16[8,16,3200]{2,1,0:T(8,128)(2,1)}), bf16[8,16,3200]{2,1,0:T(8,128)(2,1)S(1)}, u32[]{:S(2)}, u32[]{:S(2)}) async-start(bf16[8,16,3200]{2,1,0:T(8,128)(2,1)} %concatenate.10), calls=%async_computation | async-start | bytes 1638400 | tf_op jit(solution)/shard_map/all_to_all | solution.py:90
  125.4 24.1 %all-to-all-done = bf16[8,16,3200]{2,1,0:T(8,128)(2,1)S(1)} async-done(((bf16[8,16,3200]{2,1,0:T(8,128)(2,1)}), bf16[8,16,3200]{2,1,0:T(8,128)(2,1)S(1)}, u32[]{:S(2)}, u32[]{:S(2)}) %all-to-all-start) | async-done | bytes 819232 | tf_op jit(solution)/shard_map/all_to_all | solution.py:90
  149.6 0.2 add_reduce_fusion
  149.9 0.8 fusion.11
  (38 shorter events, 2.6 us)
Async XLA Ops:
  0.0 50.6 %copy-start = (bf16[256,512]{1,0:T(8,128)(2,1)S(1)}, bf16[256,512]{1,0:T(8,128)(2,1)}, u32[]{:S(2)}) copy-start(bf16[256,512]{1,0:T(8,128)(2,1)} %param.7) | copy-start | bytes 786436
  3.1 47.5 %copy-start.1 = (bf16[256,512]{1,0:T(8,128)(2,1)S(1)}, bf16[256,512]{1,0:T(8,128)(2,1)}, u32[]{:S(2)}) copy-start(bf16[256,512]{1,0:T(8,128)(2,1)} %param.9) | copy-start | bytes 786436
  3.1 6.3 %collective-permute-start = (bf16[4,128,128]{2,1,0:T(8,128)(2,1)S(1)}, bf16[4,128,128]{2,1,0:T(8,128)(2,1)S(1)}, u32[]{:S(2)}, u32[]{:S(2)}) collective-permute-start(bf16[4,128,128]{2,1,0:T(8,128)(2,1)S(1)} %get-tuple-element.31), channel_id=1, source_target_pairs={{0,16},{16,32},{32,48},{48,64},{64,80},{80,96},{96,112},{112,128},... | collective-permute-start | bytes 393224 | tf_op jit(solution)/shard_map/ppermute | solution.py:48
  9.5 7.4 %collective-permute-start.1 = (bf16[4,128,128]{2,1,0:T(8,128)(2,1)S(1)}, bf16[4,128,128]{2,1,0:T(8,128)(2,1)S(1)}, u32[]{:S(2)}, u32[]{:S(2)}) collective-permute-start(bf16[4,128,128]{2,1,0:T(8,128)(2,1)S(1)} %fusion.36), channel_id=1, source_target_pairs={{0,32},{16,48},{32,64},{48,80},{64,96},{80,112},{96,128},{112,144}... | collective-permute-start | bytes 393224 | tf_op jit(solution)/shard_map/ppermute | solution.py:48
  17.0 12.4 %collective-permute-start.2 = (bf16[4,128,128]{2,1,0:T(8,128)(2,1)S(1)}, bf16[4,128,128]{2,1,0:T(8,128)(2,1)S(1)}, u32[]{:S(2)}, u32[]{:S(2)}) collective-permute-start(bf16[4,128,128]{2,1,0:T(8,128)(2,1)S(1)} %get-tuple-element.9), channel_id=1, source_target_pairs={{0,64},{16,80},{32,96},{48,112},{64,128},{80,144},{96,160},{112,17... | collective-permute-start | bytes 393224 | tf_op jit(solution)/shard_map/ppermute | solution.py:48
  29.5 10.7 %collective-permute-start.3 = (bf16[4,128,128]{2,1,0:T(8,128)(2,1)S(1)}, bf16[4,128,128]{2,1,0:T(8,128)(2,1)S(1)}, u32[]{:S(2)}, u32[]{:S(2)}) collective-permute-start(bf16[4,128,128]{2,1,0:T(8,128)(2,1)S(1)} %fusion.37), channel_id=1, source_target_pairs={{0,128},{16,144},{32,160},{48,176},{64,192},{80,208},{96,224},{112... | collective-permute-start | bytes 393224 | tf_op jit(solution)/shard_map/ppermute | solution.py:48
  40.4 30.5 %copy-start.2 = (bf16[256,512]{1,0:T(8,128)(2,1)S(1)}, bf16[256,512]{1,0:T(8,128)(2,1)}, u32[]{:S(2)}) copy-start(bf16[256,512]{1,0:T(8,128)(2,1)} %param.10) | copy-start | bytes 786436
  40.4 12.1 %collective-permute-start.4 = (bf16[4,128,128]{2,1,0:T(8,128)(2,1)S(1)}, bf16[4,128,128]{2,1,0:T(8,128)(2,1)S(1)}, u32[]{:S(2)}, u32[]{:S(2)}) collective-permute-start(bf16[4,128,128]{2,1,0:T(8,128)(2,1)S(1)} %fusion.49), channel_id=1, source_target_pairs={{0,256},{16,272},{32,288},{48,304},{64,320},{80,336},{96,352},{112... | collective-permute-start | bytes 393224 | tf_op jit(solution)/shard_map/ppermute | solution.py:48
  51.1 21.6 %copy-start.3 = (f32[512]{0:T(512)S(1)}, f32[512]{0:T(512)}, u32[]{:S(2)}) copy-start(f32[512]{0:T(512)} %param.12) | copy-start | bytes 6148
  52.7 20.1 %collective-permute-start.5 = (bf16[4,128,128]{2,1,0:T(8,128)(2,1)S(1)}, bf16[4,128,128]{2,1,0:T(8,128)(2,1)S(1)}, u32[]{:S(2)}, u32[]{:S(2)}) collective-permute-start(bf16[4,128,128]{2,1,0:T(8,128)(2,1)S(1)} %add_convert_fusion), channel_id=1, source_target_pairs={{0,512},{16,528},{32,544},{48,560},{64,576},{80,592},{96,608},{112... | collective-permute-start | bytes 393224 | tf_op jit(solution)/shard_map/ppermute | solution.py:48
  80.5 8.9 %collective-permute-start.6 = (bf16[8,16,6272]{2,1,0:T(8,128)(2,1)}, bf16[8,16,6272]{2,1,0:T(8,128)(2,1)S(1)}, u32[]{:S(2)}, u32[]{:S(2)}) collective-permute-start(bf16[8,16,6272]{2,1,0:T(8,128)(2,1)} %concatenate.9), channel_id=1, source_target_pairs={{0,1},{1,0},{2,3},{3,2},{4,5},{5,4},{6,7},{7,6},{8,9},{9,8},{10,11... | collective-permute-start | bytes 4816904 | tf_op jit(solution)/shard_map/ppermute | solution.py:83
  90.8 30.9 %all-to-all-start.1 = ((bf16[8,16,3072]{2,1,0:T(8,128)(2,1)}), bf16[8,16,3072]{2,1,0:T(8,128)(2,1)S(1)}, u32[]{:S(2)}, u32[]{:S(2)}) async-start(bf16[8,16,3072]{2,1,0:T(8,128)(2,1)} %get-tuple-element.14), calls=%async_computation.1 | async-start | bytes 1572864 | tf_op jit(solution)/shard_map/all_to_all | solution.py:91
  121.8 27.8 %all-to-all-start = ((bf16[8,16,3200]{2,1,0:T(8,128)(2,1)}), bf16[8,16,3200]{2,1,0:T(8,128)(2,1)S(1)}, u32[]{:S(2)}, u32[]{:S(2)}) async-start(bf16[8,16,3200]{2,1,0:T(8,128)(2,1)} %concatenate.10), calls=%async_computation | async-start | bytes 1638400 | tf_op jit(solution)/shard_map/all_to_all | solution.py:90

commit v13 on v8

--- a/solution.py
+++ b/solution.py
@@ -88,7 +88,12 @@
     mine_sq = keep_sq + got_sq
     moved = lax.all_to_all(pack(mine, mine_sq), "fy", 0, 0, tiled=True)
     values, sums = unpack(moved, lanes)
-    return jnp.sum(values, axis=0), jnp.sum(sums, axis=0)
+    chip = lax.axis_index("fy")
+    others = (jnp.arange(values.shape[0]) != chip)[:, None]
+    own = lax.dynamic_index_in_dim(mine, chip, axis=0, keepdims=False)
+    own_sq = lax.dynamic_index_in_dim(mine_sq, chip, axis=0, keepdims=False)
+    total = jnp.sum(jnp.where(others[:, :, None], values, 0.0), axis=0) + own
+    return total, jnp.sum(jnp.where(others, sums, 0.0), axis=0) + own_sq
 
 
 def per_device(query_act, key_act, value_act, gate_act, rate_index, norm_gain, out_weight):

time: 142 us -> 147 us (1.035)
  blocking collectives: 47.9 us -> 0 us
  waiting for transfers between devices: 10.6 us -> 51.8 us
  starting transfers between devices: 62.2 us -> 69.4 us
  other arithmetic: 4.77 us -> 7.55 us
  local copies, waits for them, and re-layouts: 5.45 us -> 7.25 us
    all_to_all x1 -> x0, blocking collectives: 47.9 us -> none  [fsdp_reduce(): moved = lax.all_to_all(pack(mine, mine_sq), 'fy', 0, 0, tiled=True)]
    all_to_all x0 -> x1, waiting for transfers between devices: none -> 41.1 us  [fsdp_reduce(): moved = lax.all_to_all(pack(mine, mine_sq), 'fy', 0, 0, tiled=True)]
    all_to_all x0 -> x1, starting transfers between devices: none -> 7.28 us  [fsdp_reduce(): moved = lax.all_to_all(pack(mine, mine_sq), 'fy', 0, 0, tiled=True)]
    add x0 -> x2, other arithmetic: none -> 3.52 us  [the longest x1 3.52 us: fsdp_reduce(): mine = keep.astype(jnp.float32) + got]
    convert_element_type x1 -> x0, other arithmetic: 1.79 us -> none  [pack(): return jnp.concatenate([values.astype(jnp.bfloat16), extra], axis=-1)]
  transfers between devices with their start and end apart: 7 -> 8, of which waited for: 6 -> 7; matrix products, arithmetic and copies ran while one was open for 4% -> 3% of each run, Pallas kernels for 0% -> 0%
where the time goes in v13:
time: 147 us; the launch traced here: 146 us
  starting transfers between devices  69.4 us (47%)
  waiting for transfers between devices  51.8 us (35%)
  matrix products  9.95 us (7%)
  other arithmetic  7.55 us (5%)
  local copies, waits for them, and re-layouts  7.25 us (5%)
    ppermute x6, starting transfers between devices, decayed_scan(): lax.ppermute(total.astype(jnp.bfloat16), axis, perm=[(i, i + shift) for i...  57 us
    all_to_all x1, waiting for transfers between devices, fsdp_reduce(): moved = lax.all_to_all(pack(mine, mine_sq), 'fy', 0, 0, tiled=True)  41.1 us
    ppermute x6, waiting for transfers between devices, decayed_scan(): lax.ppermute(total.astype(jnp.bfloat16), axis, perm=[(i, i + shift) for i...  10.6 us
    dot_general x2, matrix products, project(): jnp.dot(block.reshape(-1, features), weight, preferred_element_type=jnp.f...  7.63 us
    all_to_all x1, starting transfers between devices, fsdp_reduce(): moved = lax.all_to_all(pack(mine, mine_sq), 'fy', 0, 0, tiled=True)  7.28 us
    ppermute x1, starting transfers between devices, fsdp_reduce(): sent = lax.ppermute(pack(give, give_sq), 'fc', perm=[(0, 1), (1, 0)])  5.06 us
    add x1, other arithmetic, fsdp_reduce(): mine = keep.astype(jnp.float32) + got  3.52 us
  transfers between devices with their start and end apart: 8, of which 7 were waited for; matrix products, arithmetic and copies ran while one was open for 3% of the time, Pallas kernels for 0%

profile of v13, /device:TPU:1, one launch (start us, length us, event | category | flops | bytes accessed | tf_op | source)
XLA Modules:
  0.0 146.2 jit_solution(16090824541505626201)
XLA Ops:
  0.0 1.1 copy.71
  1.2 0.7 multiply_exponential_fusion.3
  1.9 1.2 fusion.60
  3.1 4.1 %collective-permute-start = (bf16[4,128,128]{2,1,0:T(8,128)(2,1)S(1)}, bf16[4,128,128]{2,1,0:T(8,128)(2,1)S(1)}, u32[]{:S(2)}, u32[]{:S(2)}) collective-permute-start(bf16[4,128,128]{2,1,0:T(8,128)(2,1)S(1)} %get-tuple-element.33), channel_id=1, source_target_pairs={{0,16},{16,32},{32,48},{48,64},{64,80},{80,96},{96,112},{112,128},... | collective-permute-start | bytes 393224 | tf_op jit(solution)/shard_map/ppermute | solution.py:48
  7.2 2.2 %collective-permute-done = bf16[4,128,128]{2,1,0:T(8,128)(2,1)S(1)} collective-permute-done((bf16[4,128,128]{2,1,0:T(8,128)(2,1)S(1)}, bf16[4,128,128]{2,1,0:T(8,128)(2,1)S(1)}, u32[]{:S(2)}, u32[]{:S(2)}) %collective-permute-start) | collective-permute-done | bytes 131104 | tf_op jit(solution)/shard_map/ppermute | solution.py:48
  9.5 5.5 %collective-permute-start.1 = (bf16[4,128,128]{2,1,0:T(8,128)(2,1)S(1)}, bf16[4,128,128]{2,1,0:T(8,128)(2,1)S(1)}, u32[]{:S(2)}, u32[]{:S(2)}) collective-permute-start(bf16[4,128,128]{2,1,0:T(8,128)(2,1)S(1)} %fusion.36), channel_id=1, source_target_pairs={{0,32},{16,48},{32,64},{48,80},{64,96},{80,112},{96,128},{112,144}... | collective-permute-start | bytes 393224 | tf_op jit(solution)/shard_map/ppermute | solution.py:48
  15.0 1.9 %collective-permute-done.1 = bf16[4,128,128]{2,1,0:T(8,128)(2,1)S(1)} collective-permute-done((bf16[4,128,128]{2,1,0:T(8,128)(2,1)S(1)}, bf16[4,128,128]{2,1,0:T(8,128)(2,1)S(1)}, u32[]{:S(2)}, u32[]{:S(2)}) %collective-permute-start.1) | collective-permute-done | bytes 131104 | tf_op jit(solution)/shard_map/ppermute | solution.py:48
  17.0 10.4 %collective-permute-start.2 = (bf16[4,128,128]{2,1,0:T(8,128)(2,1)S(1)}, bf16[4,128,128]{2,1,0:T(8,128)(2,1)S(1)}, u32[]{:S(2)}, u32[]{:S(2)}) collective-permute-start(bf16[4,128,128]{2,1,0:T(8,128)(2,1)S(1)} %get-tuple-element.9), channel_id=1, source_target_pairs={{0,64},{16,80},{32,96},{48,112},{64,128},{80,144},{96,160},{112,17... | collective-permute-start | bytes 393224 | tf_op jit(solution)/shard_map/ppermute | solution.py:48
  27.6 1.8 %collective-permute-done.2 = bf16[4,128,128]{2,1,0:T(8,128)(2,1)S(1)} collective-permute-done((bf16[4,128,128]{2,1,0:T(8,128)(2,1)S(1)}, bf16[4,128,128]{2,1,0:T(8,128)(2,1)S(1)}, u32[]{:S(2)}, u32[]{:S(2)}) %collective-permute-start.2) | collective-permute-done | bytes 131104 | tf_op jit(solution)/shard_map/ppermute | solution.py:48
  29.5 8.8 %collective-permute-start.3 = (bf16[4,128,128]{2,1,0:T(8,128)(2,1)S(1)}, bf16[4,128,128]{2,1,0:T(8,128)(2,1)S(1)}, u32[]{:S(2)}, u32[]{:S(2)}) collective-permute-start(bf16[4,128,128]{2,1,0:T(8,128)(2,1)S(1)} %fusion.37), channel_id=1, source_target_pairs={{0,128},{16,144},{32,160},{48,176},{64,192},{80,208},{96,224},{112... | collective-permute-start | bytes 393224 | tf_op jit(solution)/shard_map/ppermute | solution.py:48
  38.4 1.8 %collective-permute-done.3 = bf16[4,128,128]{2,1,0:T(8,128)(2,1)S(1)} collective-permute-done((bf16[4,128,128]{2,1,0:T(8,128)(2,1)S(1)}, bf16[4,128,128]{2,1,0:T(8,128)(2,1)S(1)}, u32[]{:S(2)}, u32[]{:S(2)}) %collective-permute-start.3) | collective-permute-done | bytes 131104 | tf_op jit(solution)/shard_map/ppermute | solution.py:48
  40.3 10.1 %collective-permute-start.4 = (bf16[4,128,128]{2,1,0:T(8,128)(2,1)S(1)}, bf16[4,128,128]{2,1,0:T(8,128)(2,1)S(1)}, u32[]{:S(2)}, u32[]{:S(2)}) collective-permute-start(bf16[4,128,128]{2,1,0:T(8,128)(2,1)S(1)} %fusion.54), channel_id=1, source_target_pairs={{0,256},{16,272},{32,288},{48,304},{64,320},{80,336},{96,352},{112... | collective-permute-start | bytes 393224 | tf_op jit(solution)/shard_map/ppermute | solution.py:48
  50.5 0.5 convolution_bitcast_fusion.1
  51.0 1.4 collective-permute-done.4
  52.4 0.2 add_convert_fusion
  52.5 18.1 %collective-permute-start.5 = (bf16[4,128,128]{2,1,0:T(8,128)(2,1)S(1)}, bf16[4,128,128]{2,1,0:T(8,128)(2,1)S(1)}, u32[]{:S(2)}, u32[]{:S(2)}) collective-permute-start(bf16[4,128,128]{2,1,0:T(8,128)(2,1)S(1)} %add_convert_fusion), channel_id=1, source_target_pairs={{0,512},{16,528},{32,544},{48,560},{64,576},{80,592},{96,608},{112... | collective-permute-start | bytes 393224 | tf_op jit(solution)/shard_map/ppermute | solution.py:48
  70.8 0.2 copy.53
  71.1 1.6 %collective-permute-done.5 = bf16[4,128,128]{2,1,0:T(8,128)(2,1)S(1)} collective-permute-done((bf16[4,128,128]{2,1,0:T(8,128)(2,1)S(1)}, bf16[4,128,128]{2,1,0:T(8,128)(2,1)S(1)}, u32[]{:S(2)}, u32[]{:S(2)}) %collective-permute-start.5) | collective-permute-done | bytes 131104 | tf_op jit(solution)/shard_map/ppermute | solution.py:48
  72.6 0.6 multiply_reduce_fusion
  73.2 0.2 copy.54
  73.6 0.7 constant_dynamic-slice_fusion.4
  74.6 3.8 %convolution_convert_fusion = bf16[128,6144]{1,0:T(8,128)(2,1)S(1)} fusion(bf16[128,512]{1,0:T(8,128)(2,1)S(1)} %bitcast.80, bf16[512,6144]{1,0:T(8,128)(2,1)} %param.13), kind=kOutput, calls=%fused_computation | convolution fusion | flops 806092800 | bytes 7995392 | tf_op jit(solution)/shard_map/dot_general | solution.py:78
  78.4 0.5 concatenate.6
  78.9 5.1 %collective-permute-start.6 = (bf16[8,16,6272]{2,1,0:T(8,128)(2,1)S(1)}, bf16[8,16,6272]{2,1,0:T(8,128)(2,1)S(1)}, u32[]{:S(2)}, u32[]{:S(2)}) collective-permute-start(bf16[8,16,6272]{2,1,0:T(8,128)(2,1)S(1)} %concatenate.6), channel_id=1, source_target_pairs={{0,1},{1,0},{2,3},{3,2},{4,5},{5,4},{6,7},{7,6},{8,9},{9,8},{10,11... | collective-permute-start | bytes 4816904 | tf_op jit(solution)/shard_map/ppermute | solution.py:83
  84.0 3.9 %convolution_convert_fusion.1 = bf16[128,6144]{1,0:T(8,128)(2,1)S(1)} fusion(bf16[128,512]{1,0:T(8,128)(2,1)} %bitcast.79, bf16[512,6144]{1,0:T(8,128)(2,1)} %param.13), kind=kOutput, calls=%fused_computation.1 | convolution fusion | flops 806092800 | bytes 7995392 | tf_op jit(solution)/shard_map/dot_general | solution.py:78
  87.9 1.2 copy-done.1
  89.7 3.5 %convert_add_fusion = (f32[8,16,6144]{2,1,0:T(8,128)}, bf16[8,16,6144]{2,1,0:T(8,128)(2,1)S(1)}) fusion(bf16[8,16,6144]{2,1,0:T(8,128)(2,1)S(1)} %bitcast.75, bf16[8,16,6272]{2,1,0:T(8,128)(2,1)} %copy-done.1), kind=kLoop, calls=%fused_computation.2 | loop fusion | flops 3145728 | bytes 7864320 | tf_op jit(solution)/shard_map/add | solution.py:87
  93.2 1.9 %concatenate.7 = bf16[8,16,6272]{2,1,0:T(8,128)(2,1)} concatenate(bf16[8,16,6144]{2,1,0:T(8,128)(2,1)S(1)} %get-tuple-element.12, bf16[8,16,1]{2,1,0:T(8,128)(2,1)S(1)} %copy.59, bf16[8,16,1]{2,1,0:T(8,128)(2,1)S(1)} %copy.60, bf16[8,16,126]{2,1,0:T(8,128)(2,1)S(1)} %broadcast.169), dimensions={2} | concatenate | bytes 3211264 | tf_op jit(solution)/shard_map/concatenate | solution.py:64
  95.1 7.3 %all-to-all-start = ((bf16[8,16,6272]{2,1,0:T(8,128)(2,1)}), bf16[8,16,6272]{2,1,0:T(8,128)(2,1)S(1)}, u32[]{:S(2)}, u32[]{:S(2)}) async-start(bf16[8,16,6272]{2,1,0:T(8,128)(2,1)} %concatenate.7), calls=%async_computation | async-start | bytes 3211264 | tf_op jit(solution)/shard_map/all_to_all | solution.py:89
  102.4 41.1 %all-to-all-done = bf16[8,16,6272]{2,1,0:T(8,128)(2,1)S(1)} async-done(((bf16[8,16,6272]{2,1,0:T(8,128)(2,1)}), bf16[8,16,6272]{2,1,0:T(8,128)(2,1)S(1)}, u32[]{:S(2)}, u32[]{:S(2)}) %all-to-all-start) | async-done | bytes 1605664 | tf_op jit(solution)/shard_map/all_to_all | solution.py:89
  144.0 0.4 select_reduce_fusion
  144.4 1.8 %fusion.11 = bf16[16,6144]{1,0:T(8,128)(2,1)} fusion(f32[16,6144]{1,0:T(8,128)S(1)} %select_reduce_fusion, f32[8,16,6144]{2,1,0:T(8,128)} %get-tuple-element.11, s32[]{:T(128)S(6)} %select_n.32, f32[16]{0:T(128)S(1)} %add_rsqrt_fusion), kind=kLoop, calls=%fused_computation.23 | loop fusion | flops 294912 | bytes 983108 | tf_op jit(solution)/shard_map/convert_element_type | solution.py:123
  (41 shorter events, 2.5 us)
Async XLA Ops:
  0.0 50.5 %copy-start = (bf16[256,512]{1,0:T(8,128)(2,1)S(1)}, bf16[256,512]{1,0:T(8,128)(2,1)}, u32[]{:S(2)}) copy-start(bf16[256,512]{1,0:T(8,128)(2,1)} %param.7) | copy-start | bytes 786436
  0.0 50.5 %copy-start.2 = (bf16[256,512]{1,0:T(8,128)(2,1)S(1)}, bf16[256,512]{1,0:T(8,128)(2,1)}, u32[]{:S(2)}) copy-start(bf16[256,512]{1,0:T(8,128)(2,1)} %param.9) | copy-start | bytes 786436
  3.1 67.6 %copy-start.3 = (bf16[256,512]{1,0:T(8,128)(2,1)S(1)}, bf16[256,512]{1,0:T(8,128)(2,1)}, u32[]{:S(2)}) copy-start(bf16[256,512]{1,0:T(8,128)(2,1)} %param.10) | copy-start | bytes 786436
  3.1 6.3 %collective-permute-start = (bf16[4,128,128]{2,1,0:T(8,128)(2,1)S(1)}, bf16[4,128,128]{2,1,0:T(8,128)(2,1)S(1)}, u32[]{:S(2)}, u32[]{:S(2)}) collective-permute-start(bf16[4,128,128]{2,1,0:T(8,128)(2,1)S(1)} %get-tuple-element.33), channel_id=1, source_target_pairs={{0,16},{16,32},{32,48},{48,64},{64,80},{80,96},{96,112},{112,128},... | collective-permute-start | bytes 393224 | tf_op jit(solution)/shard_map/ppermute | solution.py:48
  9.5 7.4 %collective-permute-start.1 = (bf16[4,128,128]{2,1,0:T(8,128)(2,1)S(1)}, bf16[4,128,128]{2,1,0:T(8,128)(2,1)S(1)}, u32[]{:S(2)}, u32[]{:S(2)}) collective-permute-start(bf16[4,128,128]{2,1,0:T(8,128)(2,1)S(1)} %fusion.36), channel_id=1, source_target_pairs={{0,32},{16,48},{32,64},{48,80},{64,96},{80,112},{96,128},{112,144}... | collective-permute-start | bytes 393224 | tf_op jit(solution)/shard_map/ppermute | solution.py:48
  17.0 12.4 %collective-permute-start.2 = (bf16[4,128,128]{2,1,0:T(8,128)(2,1)S(1)}, bf16[4,128,128]{2,1,0:T(8,128)(2,1)S(1)}, u32[]{:S(2)}, u32[]{:S(2)}) collective-permute-start(bf16[4,128,128]{2,1,0:T(8,128)(2,1)S(1)} %get-tuple-element.9), channel_id=1, source_target_pairs={{0,64},{16,80},{32,96},{48,112},{64,128},{80,144},{96,160},{112,17... | collective-permute-start | bytes 393224 | tf_op jit(solution)/shard_map/ppermute | solution.py:48
  29.4 43.2 %copy-start.4 = (f32[512]{0:T(512)S(1)}, f32[512]{0:T(512)}, u32[]{:S(2)}) copy-start(f32[512]{0:T(512)} %param.12) | copy-start | bytes 6148
  29.5 10.7 %collective-permute-start.3 = (bf16[4,128,128]{2,1,0:T(8,128)(2,1)S(1)}, bf16[4,128,128]{2,1,0:T(8,128)(2,1)S(1)}, u32[]{:S(2)}, u32[]{:S(2)}) collective-permute-start(bf16[4,128,128]{2,1,0:T(8,128)(2,1)S(1)} %fusion.37), channel_id=1, source_target_pairs={{0,128},{16,144},{32,160},{48,176},{64,192},{80,208},{96,224},{112... | collective-permute-start | bytes 393224 | tf_op jit(solution)/shard_map/ppermute | solution.py:48
  40.3 12.0 %collective-permute-start.4 = (bf16[4,128,128]{2,1,0:T(8,128)(2,1)S(1)}, bf16[4,128,128]{2,1,0:T(8,128)(2,1)S(1)}, u32[]{:S(2)}, u32[]{:S(2)}) collective-permute-start(bf16[4,128,128]{2,1,0:T(8,128)(2,1)S(1)} %fusion.54), channel_id=1, source_target_pairs={{0,256},{16,272},{32,288},{48,304},{64,320},{80,336},{96,352},{112... | collective-permute-start | bytes 393224 | tf_op jit(solution)/shard_map/ppermute | solution.py:48
  52.5 20.1 %collective-permute-start.5 = (bf16[4,128,128]{2,1,0:T(8,128)(2,1)S(1)}, bf16[4,128,128]{2,1,0:T(8,128)(2,1)S(1)}, u32[]{:S(2)}, u32[]{:S(2)}) collective-permute-start(bf16[4,128,128]{2,1,0:T(8,128)(2,1)S(1)} %add_convert_fusion), channel_id=1, source_target_pairs={{0,512},{16,528},{32,544},{48,560},{64,576},{80,592},{96,608},{112... | collective-permute-start | bytes 393224 | tf_op jit(solution)/shard_map/ppermute | solution.py:48
  78.9 8.9 %collective-permute-start.6 = (bf16[8,16,6272]{2,1,0:T(8,128)(2,1)S(1)}, bf16[8,16,6272]{2,1,0:T(8,128)(2,1)S(1)}, u32[]{:S(2)}, u32[]{:S(2)}) collective-permute-start(bf16[8,16,6272]{2,1,0:T(8,128)(2,1)S(1)} %concatenate.6), channel_id=1, source_target_pairs={{0,1},{1,0},{2,3},{3,2},{4,5},{5,4},{6,7},{7,6},{8,9},{9,8},{10,11... | collective-permute-start | bytes 4816904 | tf_op jit(solution)/shard_map/ppermute | solution.py:83
  87.9 1.2 copy-start.1
  95.1 48.4 %all-to-all-start = ((bf16[8,16,6272]{2,1,0:T(8,128)(2,1)}), bf16[8,16,6272]{2,1,0:T(8,128)(2,1)S(1)}, u32[]{:S(2)}, u32[]{:S(2)}) async-start(bf16[8,16,6272]{2,1,0:T(8,128)(2,1)} %concatenate.7), calls=%async_computation | async-start | bytes 3211264 | tf_op jit(solution)/shard_map/all_to_all | solution.py:89

commit v14 on v8

--- a/solution.py
+++ b/solution.py
@@ -31,9 +31,12 @@
     )
     to_end = jnp.exp(-slopes[None, :] * (tok_count - 1.0 - position)[:, None])
     key_scaled = (key_rows.astype(jnp.float32) * to_end[:, :, None]).astype(jnp.bfloat16)
-    local_state = jnp.einsum(
-        "thd,the->hde", key_scaled, value_rows, preferred_element_type=jnp.float32
-    )
+    heads = key_scaled.shape[1]
+    full = lax.dot_general(
+        key_scaled.reshape(tok_count, -1), value_rows.reshape(tok_count, -1),
+        (((0,), (0,)), ((), ())), preferred_element_type=jnp.float32,
+    ).reshape(heads, HEAD_DIM, heads, HEAD_DIM)
+    local_state = jnp.stack([full[h, :, h] for h in range(heads)])
     from_start = jnp.exp(-slopes[None, :] * (position + 1.0)[:, None])
     return (intra_part, local_state, from_start)
 

time: 142 us -> 141 us (level)
  no operation moved by 1% of the time
where the time goes in v14:
time: 141 us
  starting transfers between devices  62.1 us (44%)
  blocking collectives  47.9 us (34%)
  waiting for transfers between devices  10.5 us (7%)
  matrix products  9.11 us (6%)
  other arithmetic  5.84 us (4%)
  local copies, waits for them, and re-layouts  5.26 us (4%)
    ppermute x6, starting transfers between devices, decayed_scan(): lax.ppermute(total.astype(jnp.bfloat16), axis, perm=[(i, i + shift) for i...  57.1 us
    all_to_all x1, blocking collectives, fsdp_reduce(): moved = lax.all_to_all(pack(mine, mine_sq), 'fy', 0, 0, tiled=True)  47.9 us
    ppermute x6, waiting for transfers between devices, decayed_scan(): lax.ppermute(total.astype(jnp.bfloat16), axis, perm=[(i, i + shift) for i...  10.5 us
    dot_general x2, matrix products, project(): jnp.dot(block.reshape(-1, features), weight, preferred_element_type=jnp.f...  7.63 us
    ppermute x1, starting transfers between devices, fsdp_reduce(): sent = lax.ppermute(pack(give, give_sq), 'fc', perm=[(0, 1), (1, 0)])  5.01 us
  transfers between devices with their start and end apart: 7, of which 6 were waited for; matrix products, arithmetic and copies ran while one was open for 4% of the time, Pallas kernels for 0%

profile of v14, /device:TPU:1, one launch (start us, length us, event | category | flops | bytes accessed | tf_op | source)
XLA Modules:
  0.0 141.0 jit_solution(2712163297945767089)
XLA Ops:
  0.0 0.7 multiply_exponential_fusion.3
  1.0 0.3 mul.194
  1.3 1.0 fusion.12
  2.6 0.3 fusion.53
  3.0 3.9 %collective-permute-start = (bf16[4,128,128]{2,1,0:T(8,128)(2,1)S(1)}, bf16[4,128,128]{2,1,0:T(8,128)(2,1)S(1)}, u32[]{:S(2)}, u32[]{:S(2)}) collective-permute-start(bf16[4,128,128]{2,1,0:T(8,128)(2,1)S(1)} %fusion.44), channel_id=1, source_target_pairs={{0,16},{16,32},{32,48},{48,64},{64,80},{80,96},{96,112},{112,128},... | collective-permute-start | bytes 393224 | tf_op jit(solution)/shard_map/ppermute | solution.py:51
  7.0 2.2 %collective-permute-done = bf16[4,128,128]{2,1,0:T(8,128)(2,1)S(1)} collective-permute-done((bf16[4,128,128]{2,1,0:T(8,128)(2,1)S(1)}, bf16[4,128,128]{2,1,0:T(8,128)(2,1)S(1)}, u32[]{:S(2)}, u32[]{:S(2)}) %collective-permute-start) | collective-permute-done | bytes 131104 | tf_op jit(solution)/shard_map/ppermute | solution.py:51
  9.3 5.6 %collective-permute-start.1 = (bf16[4,128,128]{2,1,0:T(8,128)(2,1)S(1)}, bf16[4,128,128]{2,1,0:T(8,128)(2,1)S(1)}, u32[]{:S(2)}, u32[]{:S(2)}) collective-permute-start(bf16[4,128,128]{2,1,0:T(8,128)(2,1)S(1)} %fusion.35), channel_id=1, source_target_pairs={{0,32},{16,48},{32,64},{48,80},{64,96},{80,112},{96,128},{112,144}... | collective-permute-start | bytes 393224 | tf_op jit(solution)/shard_map/ppermute | solution.py:51
  15.0 1.8 %collective-permute-done.1 = bf16[4,128,128]{2,1,0:T(8,128)(2,1)S(1)} collective-permute-done((bf16[4,128,128]{2,1,0:T(8,128)(2,1)S(1)}, bf16[4,128,128]{2,1,0:T(8,128)(2,1)S(1)}, u32[]{:S(2)}, u32[]{:S(2)}) %collective-permute-start.1) | collective-permute-done | bytes 131104 | tf_op jit(solution)/shard_map/ppermute | solution.py:51
  17.0 10.4 %collective-permute-start.2 = (bf16[4,128,128]{2,1,0:T(8,128)(2,1)S(1)}, bf16[4,128,128]{2,1,0:T(8,128)(2,1)S(1)}, u32[]{:S(2)}, u32[]{:S(2)}) collective-permute-start(bf16[4,128,128]{2,1,0:T(8,128)(2,1)S(1)} %get-tuple-element.9), channel_id=1, source_target_pairs={{0,64},{16,80},{32,96},{48,112},{64,128},{80,144},{96,160},{112,17... | collective-permute-start | bytes 393224 | tf_op jit(solution)/shard_map/ppermute | solution.py:51
  27.5 1.8 %collective-permute-done.2 = bf16[4,128,128]{2,1,0:T(8,128)(2,1)S(1)} collective-permute-done((bf16[4,128,128]{2,1,0:T(8,128)(2,1)S(1)}, bf16[4,128,128]{2,1,0:T(8,128)(2,1)S(1)}, u32[]{:S(2)}, u32[]{:S(2)}) %collective-permute-start.2) | collective-permute-done | bytes 131104 | tf_op jit(solution)/shard_map/ppermute | solution.py:51
  29.4 8.8 %collective-permute-start.3 = (bf16[4,128,128]{2,1,0:T(8,128)(2,1)S(1)}, bf16[4,128,128]{2,1,0:T(8,128)(2,1)S(1)}, u32[]{:S(2)}, u32[]{:S(2)}) collective-permute-start(bf16[4,128,128]{2,1,0:T(8,128)(2,1)S(1)} %fusion.36), channel_id=1, source_target_pairs={{0,128},{16,144},{32,160},{48,176},{64,192},{80,208},{96,224},{112... | collective-permute-start | bytes 393224 | tf_op jit(solution)/shard_map/ppermute | solution.py:51
  38.4 1.8 %collective-permute-done.3 = bf16[4,128,128]{2,1,0:T(8,128)(2,1)S(1)} collective-permute-done((bf16[4,128,128]{2,1,0:T(8,128)(2,1)S(1)}, bf16[4,128,128]{2,1,0:T(8,128)(2,1)S(1)}, u32[]{:S(2)}, u32[]{:S(2)}) %collective-permute-start.3) | collective-permute-done | bytes 131104 | tf_op jit(solution)/shard_map/ppermute | solution.py:51
  40.3 10.1 %collective-permute-start.4 = (bf16[4,128,128]{2,1,0:T(8,128)(2,1)S(1)}, bf16[4,128,128]{2,1,0:T(8,128)(2,1)S(1)}, u32[]{:S(2)}, u32[]{:S(2)}) collective-permute-start(bf16[4,128,128]{2,1,0:T(8,128)(2,1)S(1)} %fusion.49), channel_id=1, source_target_pairs={{0,256},{16,272},{32,288},{48,304},{64,320},{80,336},{96,352},{112... | collective-permute-start | bytes 393224 | tf_op jit(solution)/shard_map/ppermute | solution.py:51
  50.4 0.5 convolution_bitcast_fusion.1
  51.0 1.3 collective-permute-done.4
  52.5 18.2 %collective-permute-start.5 = (bf16[4,128,128]{2,1,0:T(8,128)(2,1)S(1)}, bf16[4,128,128]{2,1,0:T(8,128)(2,1)S(1)}, u32[]{:S(2)}, u32[]{:S(2)}) collective-permute-start(bf16[4,128,128]{2,1,0:T(8,128)(2,1)S(1)} %add_convert_fusion), channel_id=1, source_target_pairs={{0,512},{16,528},{32,544},{48,560},{64,576},{80,592},{96,608},{112... | collective-permute-start | bytes 393224 | tf_op jit(solution)/shard_map/ppermute | solution.py:51
  70.8 0.2 copy.53
  71.0 1.6 %collective-permute-done.5 = bf16[4,128,128]{2,1,0:T(8,128)(2,1)S(1)} collective-permute-done((bf16[4,128,128]{2,1,0:T(8,128)(2,1)S(1)}, bf16[4,128,128]{2,1,0:T(8,128)(2,1)S(1)}, u32[]{:S(2)}, u32[]{:S(2)}) %collective-permute-start.5) | collective-permute-done | bytes 131104 | tf_op jit(solution)/shard_map/ppermute | solution.py:51
  72.6 0.6 multiply_reduce_fusion
  73.2 0.2 copy.54
  73.6 0.7 constant_dynamic-slice_fusion.2
  74.6 3.8 %convolution_convert_fusion = bf16[128,6144]{1,0:T(8,128)(2,1)S(1)} fusion(bf16[128,512]{1,0:T(8,128)(2,1)S(1)} %bitcast.84, bf16[512,6144]{1,0:T(8,128)(2,1)} %param.13), kind=kOutput, calls=%fused_computation | convolution fusion | flops 806092800 | bytes 7995392 | tf_op jit(solution)/shard_map/dot_general | solution.py:81
  78.4 0.5 concatenate.6
  78.9 5.0 %collective-permute-start.6 = (bf16[8,16,6272]{2,1,0:T(8,128)(2,1)S(1)}, bf16[8,16,6272]{2,1,0:T(8,128)(2,1)S(1)}, u32[]{:S(2)}, u32[]{:S(2)}) collective-permute-start(bf16[8,16,6272]{2,1,0:T(8,128)(2,1)S(1)} %concatenate.6), channel_id=1, source_target_pairs={{0,1},{1,0},{2,3},{3,2},{4,5},{5,4},{6,7},{7,6},{8,9},{9,8},{10,11... | collective-permute-start | bytes 4816904 | tf_op jit(solution)/shard_map/ppermute | solution.py:86
  83.9 3.9 %convolution_convert_fusion.1 = bf16[128,6144]{1,0:T(8,128)(2,1)S(1)} fusion(bf16[128,512]{1,0:T(8,128)(2,1)} %bitcast.83, bf16[512,6144]{1,0:T(8,128)(2,1)} %param.13), kind=kOutput, calls=%fused_computation.1 | convolution fusion | flops 806092800 | bytes 7995392 | tf_op jit(solution)/shard_map/dot_general | solution.py:81
  87.8 1.2 copy-done.1
  89.6 1.8 %fusion = bf16[8,16,6144]{2,1,0:T(8,128)(2,1)S(1)} fusion(bf16[8,16,6144]{2,1,0:T(8,128)(2,1)S(1)} %bitcast.77, bf16[8,16,6272]{2,1,0:T(8,128)(2,1)} %copy-done.1), kind=kLoop, calls=%fused_computation.3 | loop fusion | flops 3145728 | bytes 4718592 | tf_op jit(solution)/shard_map/convert_element_type | solution.py:67
  91.4 0.5 concatenate.7
  91.9 47.9 %all_to_all.5 = bf16[8,16,6272]{2,1,0:T(8,128)(2,1)S(1)} all-to-all(bf16[8,16,6272]{2,1,0:T(8,128)(2,1)S(1)} %concatenate.7), channel_id=1, replica_groups=mesh['sz'=8,'sx'=8,'fy'=8,'fc'=2] {'fy'}, dimensions={0} | all-to-all | bytes 3211264 | tf_op jit(solution)/shard_map/all_to_all | solution.py:92
  139.8 0.2 add_reduce_fusion
  140.0 0.2 convert_reduce_fusion
  140.2 0.8 multiply_convert_fusion.1
  (44 shorter events, 2.8 us)
Async XLA Ops:
  0.0 50.4 %copy-start = (bf16[256,512]{1,0:T(8,128)(2,1)S(1)}, bf16[256,512]{1,0:T(8,128)(2,1)}, u32[]{:S(2)}) copy-start(bf16[256,512]{1,0:T(8,128)(2,1)} %param.7) | copy-start | bytes 786436
  0.0 2.5 %copy-start.2 = (bf16[256,512]{1,0:T(8,128)(2,1)S(1)}, bf16[256,512]{1,0:T(8,128)(2,1)}, u32[]{:S(2)}) copy-start(bf16[256,512]{1,0:T(8,128)(2,1)} %param.9) | copy-start | bytes 786436
  3.0 6.1 %collective-permute-start = (bf16[4,128,128]{2,1,0:T(8,128)(2,1)S(1)}, bf16[4,128,128]{2,1,0:T(8,128)(2,1)S(1)}, u32[]{:S(2)}, u32[]{:S(2)}) collective-permute-start(bf16[4,128,128]{2,1,0:T(8,128)(2,1)S(1)} %fusion.44), channel_id=1, source_target_pairs={{0,16},{16,32},{32,48},{48,64},{64,80},{80,96},{96,112},{112,128},... | collective-permute-start | bytes 393224 | tf_op jit(solution)/shard_map/ppermute | solution.py:51
  9.3 41.2 %copy-start.4 = (bf16[256,512]{1,0:T(8,128)(2,1)S(1)}, bf16[256,512]{1,0:T(8,128)(2,1)}, u32[]{:S(2)}) copy-start(bf16[256,512]{1,0:T(8,128)(2,1)} %param.8) | copy-start | bytes 786436
  9.3 7.5 %collective-permute-start.1 = (bf16[4,128,128]{2,1,0:T(8,128)(2,1)S(1)}, bf16[4,128,128]{2,1,0:T(8,128)(2,1)S(1)}, u32[]{:S(2)}, u32[]{:S(2)}) collective-permute-start(bf16[4,128,128]{2,1,0:T(8,128)(2,1)S(1)} %fusion.35), channel_id=1, source_target_pairs={{0,32},{16,48},{32,64},{48,80},{64,96},{80,112},{96,128},{112,144}... | collective-permute-start | bytes 393224 | tf_op jit(solution)/shard_map/ppermute | solution.py:51
  17.0 12.4 %collective-permute-start.2 = (bf16[4,128,128]{2,1,0:T(8,128)(2,1)S(1)}, bf16[4,128,128]{2,1,0:T(8,128)(2,1)S(1)}, u32[]{:S(2)}, u32[]{:S(2)}) collective-permute-start(bf16[4,128,128]{2,1,0:T(8,128)(2,1)S(1)} %get-tuple-element.9), channel_id=1, source_target_pairs={{0,64},{16,80},{32,96},{48,112},{64,128},{80,144},{96,160},{112,17... | collective-permute-start | bytes 393224 | tf_op jit(solution)/shard_map/ppermute | solution.py:51
  29.4 10.7 %collective-permute-start.3 = (bf16[4,128,128]{2,1,0:T(8,128)(2,1)S(1)}, bf16[4,128,128]{2,1,0:T(8,128)(2,1)S(1)}, u32[]{:S(2)}, u32[]{:S(2)}) collective-permute-start(bf16[4,128,128]{2,1,0:T(8,128)(2,1)S(1)} %fusion.36), channel_id=1, source_target_pairs={{0,128},{16,144},{32,160},{48,176},{64,192},{80,208},{96,224},{112... | collective-permute-start | bytes 393224 | tf_op jit(solution)/shard_map/ppermute | solution.py:51
  40.3 12.0 %collective-permute-start.4 = (bf16[4,128,128]{2,1,0:T(8,128)(2,1)S(1)}, bf16[4,128,128]{2,1,0:T(8,128)(2,1)S(1)}, u32[]{:S(2)}, u32[]{:S(2)}) collective-permute-start(bf16[4,128,128]{2,1,0:T(8,128)(2,1)S(1)} %fusion.49), channel_id=1, source_target_pairs={{0,256},{16,272},{32,288},{48,304},{64,320},{80,336},{96,352},{112... | collective-permute-start | bytes 393224 | tf_op jit(solution)/shard_map/ppermute | solution.py:51
  50.4 20.2 %copy-start.3 = (bf16[256,512]{1,0:T(8,128)(2,1)S(1)}, bf16[256,512]{1,0:T(8,128)(2,1)}, u32[]{:S(2)}) copy-start(bf16[256,512]{1,0:T(8,128)(2,1)} %param.10) | copy-start | bytes 786436
  51.0 21.6 %copy-start.5 = (f32[512]{0:T(512)S(1)}, f32[512]{0:T(512)}, u32[]{:S(2)}) copy-start(f32[512]{0:T(512)} %param.12) | copy-start | bytes 6148
  52.5 20.1 %collective-permute-start.5 = (bf16[4,128,128]{2,1,0:T(8,128)(2,1)S(1)}, bf16[4,128,128]{2,1,0:T(8,128)(2,1)S(1)}, u32[]{:S(2)}, u32[]{:S(2)}) collective-permute-start(bf16[4,128,128]{2,1,0:T(8,128)(2,1)S(1)} %add_convert_fusion), channel_id=1, source_target_pairs={{0,512},{16,528},{32,544},{48,560},{64,576},{80,592},{96,608},{112... | collective-permute-start | bytes 393224 | tf_op jit(solution)/shard_map/ppermute | solution.py:51
  78.9 8.9 %collective-permute-start.6 = (bf16[8,16,6272]{2,1,0:T(8,128)(2,1)S(1)}, bf16[8,16,6272]{2,1,0:T(8,128)(2,1)S(1)}, u32[]{:S(2)}, u32[]{:S(2)}) collective-permute-start(bf16[8,16,6272]{2,1,0:T(8,128)(2,1)S(1)} %concatenate.6), channel_id=1, source_target_pairs={{0,1},{1,0},{2,3},{3,2},{4,5},{5,4},{6,7},{7,6},{8,9},{9,8},{10,11... | collective-permute-start | bytes 4816904 | tf_op jit(solution)/shard_map/ppermute | solution.py:86
  87.8 1.2 copy-start.1

commit v15 on v14

--- a/solution.py
+++ b/solution.py
@@ -106,9 +106,11 @@
     gain_table = norm_gain.reshape(heads_here, HEAD_DIM)
     intra_part, local_state, from_start = span_terms(query_rows, key_rows, value_rows, slopes)
     incoming = decayed_scan(local_state, slopes, tok_count, ("sz", "sx"))
+    state_hi = incoming.astype(jnp.bfloat16)
+    state_lo = (incoming - state_hi.astype(jnp.float32)).astype(jnp.bfloat16)
     inter_part = jnp.einsum(
-        "thd,hde->the", query_rows.astype(jnp.float32), incoming, precision=lax.Precision.HIGHEST
-    )
+        "thd,hde->the", query_rows, state_hi, preferred_element_type=jnp.float32
+    ) + jnp.einsum("thd,hde->the", query_rows, state_lo, preferred_element_type=jnp.float32)
     attended = intra_part + from_start[:, :, None] * inter_part
     local_squares = jnp.sum(attended * attended, axis=(1, 2))
     gated = attended * gain_table[None] * jax.nn.sigmoid(gate_rows.astype(jnp.float32))

time: 141 us -> 142 us (level)
  transfers between devices with their start and end apart: 7 -> 7, of which waited for: 6 -> 6; matrix products, arithmetic and copies ran while one was open for 4% -> 3% of each run, Pallas kernels for 0% -> 0%
where the time goes in v15:
time: 142 us
  starting transfers between devices  62 us (44%)
  blocking collectives  47.9 us (34%)
  waiting for transfers between devices  11 us (8%)
  matrix products  9.05 us (6%)
  other arithmetic  6.1 us (4%)
  local copies, waits for them, and re-layouts  5.38 us (4%)
    ppermute x6, starting transfers between devices, decayed_scan(): lax.ppermute(total.astype(jnp.bfloat16), axis, perm=[(i, i + shift) for i...  56.9 us
    all_to_all x1, blocking collectives, fsdp_reduce(): moved = lax.all_to_all(pack(mine, mine_sq), 'fy', 0, 0, tiled=True)  47.9 us
    ppermute x6, waiting for transfers between devices, decayed_scan(): lax.ppermute(total.astype(jnp.bfloat16), axis, perm=[(i, i + shift) for i...  11 us
    dot_general x2, matrix products, project(): jnp.dot(block.reshape(-1, features), weight, preferred_element_type=jnp.f...  7.63 us
    ppermute x1, starting transfers between devices, fsdp_reduce(): sent = lax.ppermute(pack(give, give_sq), 'fc', perm=[(0, 1), (1, 0)])  5.02 us
  transfers between devices with their start and end apart: 7, of which 6 were waited for; matrix products, arithmetic and copies ran while one was open for 3% of the time, Pallas kernels for 0%

profile of v15, /device:TPU:1, one launch (start us, length us, event | category | flops | bytes accessed | tf_op | source)
XLA Modules:
  0.0 141.7 jit_solution(4398957828449836858)
XLA Ops:
  0.0 0.7 multiply_exponential_fusion.3
  1.0 0.3 mul.194
  1.3 1.0 fusion.13
  2.6 0.3 fusion.48
  3.0 3.9 %collective-permute-start = (bf16[4,128,128]{2,1,0:T(8,128)(2,1)S(1)}, bf16[4,128,128]{2,1,0:T(8,128)(2,1)S(1)}, u32[]{:S(2)}, u32[]{:S(2)}) collective-permute-start(bf16[4,128,128]{2,1,0:T(8,128)(2,1)S(1)} %fusion.35), channel_id=1, source_target_pairs={{0,16},{16,32},{32,48},{48,64},{64,80},{80,96},{96,112},{112,128},... | collective-permute-start | bytes 393224 | tf_op jit(solution)/shard_map/ppermute | solution.py:51
  7.0 2.1 %collective-permute-done = bf16[4,128,128]{2,1,0:T(8,128)(2,1)S(1)} collective-permute-done((bf16[4,128,128]{2,1,0:T(8,128)(2,1)S(1)}, bf16[4,128,128]{2,1,0:T(8,128)(2,1)S(1)}, u32[]{:S(2)}, u32[]{:S(2)}) %collective-permute-start) | collective-permute-done | bytes 131104 | tf_op jit(solution)/shard_map/ppermute | solution.py:51
  9.3 5.5 %collective-permute-start.1 = (bf16[4,128,128]{2,1,0:T(8,128)(2,1)S(1)}, bf16[4,128,128]{2,1,0:T(8,128)(2,1)S(1)}, u32[]{:S(2)}, u32[]{:S(2)}) collective-permute-start(bf16[4,128,128]{2,1,0:T(8,128)(2,1)S(1)} %fusion.31), channel_id=1, source_target_pairs={{0,32},{16,48},{32,64},{48,80},{64,96},{80,112},{96,128},{112,144}... | collective-permute-start | bytes 393224 | tf_op jit(solution)/shard_map/ppermute | solution.py:51
  14.8 1.9 %collective-permute-done.1 = bf16[4,128,128]{2,1,0:T(8,128)(2,1)S(1)} collective-permute-done((bf16[4,128,128]{2,1,0:T(8,128)(2,1)S(1)}, bf16[4,128,128]{2,1,0:T(8,128)(2,1)S(1)}, u32[]{:S(2)}, u32[]{:S(2)}) %collective-permute-start.1) | collective-permute-done | bytes 131104 | tf_op jit(solution)/shard_map/ppermute | solution.py:51
  16.8 10.4 %collective-permute-start.2 = (bf16[4,128,128]{2,1,0:T(8,128)(2,1)S(1)}, bf16[4,128,128]{2,1,0:T(8,128)(2,1)S(1)}, u32[]{:S(2)}, u32[]{:S(2)}) collective-permute-start(bf16[4,128,128]{2,1,0:T(8,128)(2,1)S(1)} %get-tuple-element.9), channel_id=1, source_target_pairs={{0,64},{16,80},{32,96},{48,112},{64,128},{80,144},{96,160},{112,17... | collective-permute-start | bytes 393224 | tf_op jit(solution)/shard_map/ppermute | solution.py:51
  27.3 1.9 %collective-permute-done.2 = bf16[4,128,128]{2,1,0:T(8,128)(2,1)S(1)} collective-permute-done((bf16[4,128,128]{2,1,0:T(8,128)(2,1)S(1)}, bf16[4,128,128]{2,1,0:T(8,128)(2,1)S(1)}, u32[]{:S(2)}, u32[]{:S(2)}) %collective-permute-start.2) | collective-permute-done | bytes 131104 | tf_op jit(solution)/shard_map/ppermute | solution.py:51
  29.3 8.8 %collective-permute-start.3 = (bf16[4,128,128]{2,1,0:T(8,128)(2,1)S(1)}, bf16[4,128,128]{2,1,0:T(8,128)(2,1)S(1)}, u32[]{:S(2)}, u32[]{:S(2)}) collective-permute-start(bf16[4,128,128]{2,1,0:T(8,128)(2,1)S(1)} %fusion.32), channel_id=1, source_target_pairs={{0,128},{16,144},{32,160},{48,176},{64,192},{80,208},{96,224},{112... | collective-permute-start | bytes 393224 | tf_op jit(solution)/shard_map/ppermute | solution.py:51
  38.4 0.2 copy.61
  38.7 1.4 collective-permute-done.3
  40.2 10.1 %collective-permute-start.4 = (bf16[4,128,128]{2,1,0:T(8,128)(2,1)S(1)}, bf16[4,128,128]{2,1,0:T(8,128)(2,1)S(1)}, u32[]{:S(2)}, u32[]{:S(2)}) collective-permute-start(bf16[4,128,128]{2,1,0:T(8,128)(2,1)S(1)} %fusion.40), channel_id=1, source_target_pairs={{0,256},{16,272},{32,288},{48,304},{64,320},{80,336},{96,352},{112... | collective-permute-start | bytes 393224 | tf_op jit(solution)/shard_map/ppermute | solution.py:51
  50.4 1.8 %collective-permute-done.4 = bf16[4,128,128]{2,1,0:T(8,128)(2,1)S(1)} collective-permute-done((bf16[4,128,128]{2,1,0:T(8,128)(2,1)S(1)}, bf16[4,128,128]{2,1,0:T(8,128)(2,1)S(1)}, u32[]{:S(2)}, u32[]{:S(2)}) %collective-permute-start.4) | collective-permute-done | bytes 131104 | tf_op jit(solution)/shard_map/ppermute | solution.py:51
  52.4 18.2 %collective-permute-start.5 = (bf16[4,128,128]{2,1,0:T(8,128)(2,1)S(1)}, bf16[4,128,128]{2,1,0:T(8,128)(2,1)S(1)}, u32[]{:S(2)}, u32[]{:S(2)}) collective-permute-start(bf16[4,128,128]{2,1,0:T(8,128)(2,1)S(1)} %add_convert_fusion), channel_id=1, source_target_pairs={{0,512},{16,528},{32,544},{48,560},{64,576},{80,592},{96,608},{112... | collective-permute-start | bytes 393224 | tf_op jit(solution)/shard_map/ppermute | solution.py:51
  70.6 1.8 %collective-permute-done.5 = bf16[4,128,128]{2,1,0:T(8,128)(2,1)S(1)} collective-permute-done((bf16[4,128,128]{2,1,0:T(8,128)(2,1)S(1)}, bf16[4,128,128]{2,1,0:T(8,128)(2,1)S(1)}, u32[]{:S(2)}, u32[]{:S(2)}) %collective-permute-start.5) | collective-permute-done | bytes 131104 | tf_op jit(solution)/shard_map/ppermute | solution.py:51
  72.5 0.3 add_multiply_fusion
  72.7 0.3 fusion.19
  73.0 0.3 fusion.4
  73.4 0.6 multiply_reduce_fusion
  74.3 0.7 constant_dynamic-slice_fusion.2
  75.3 3.8 %convolution_convert_fusion = bf16[128,6144]{1,0:T(8,128)(2,1)S(1)} fusion(bf16[128,512]{1,0:T(8,128)(2,1)S(1)} %bitcast.90, bf16[512,6144]{1,0:T(8,128)(2,1)} %param.13), kind=kOutput, calls=%fused_computation | convolution fusion | flops 806092800 | bytes 7995392 | tf_op jit(solution)/shard_map/dot_general | solution.py:81
  79.1 0.5 concatenate.6
  79.6 5.0 %collective-permute-start.6 = (bf16[8,16,6272]{2,1,0:T(8,128)(2,1)S(1)}, bf16[8,16,6272]{2,1,0:T(8,128)(2,1)S(1)}, u32[]{:S(2)}, u32[]{:S(2)}) collective-permute-start(bf16[8,16,6272]{2,1,0:T(8,128)(2,1)S(1)} %concatenate.6), channel_id=1, source_target_pairs={{0,1},{1,0},{2,3},{3,2},{4,5},{5,4},{6,7},{7,6},{8,9},{9,8},{10,11... | collective-permute-start | bytes 4816904 | tf_op jit(solution)/shard_map/ppermute | solution.py:86
  84.7 3.9 %convolution_convert_fusion.1 = bf16[128,6144]{1,0:T(8,128)(2,1)S(1)} fusion(bf16[128,512]{1,0:T(8,128)(2,1)} %bitcast.89, bf16[512,6144]{1,0:T(8,128)(2,1)} %param.13), kind=kOutput, calls=%fused_computation.1 | convolution fusion | flops 806092800 | bytes 7995392 | tf_op jit(solution)/shard_map/dot_general | solution.py:81
  88.6 1.2 copy-done.1
  90.4 1.8 %fusion = bf16[8,16,6144]{2,1,0:T(8,128)(2,1)S(1)} fusion(bf16[8,16,6144]{2,1,0:T(8,128)(2,1)S(1)} %bitcast.84, bf16[8,16,6272]{2,1,0:T(8,128)(2,1)} %copy-done.1), kind=kLoop, calls=%fused_computation.3 | loop fusion | flops 3145728 | bytes 4718592 | tf_op jit(solution)/shard_map/convert_element_type | solution.py:67
  92.2 0.5 concatenate.7
  92.7 47.9 %all_to_all.5 = bf16[8,16,6272]{2,1,0:T(8,128)(2,1)S(1)} all-to-all(bf16[8,16,6272]{2,1,0:T(8,128)(2,1)S(1)} %concatenate.7), channel_id=1, replica_groups=mesh['sz'=8,'sx'=8,'fy'=8,'fc'=2] {'fy'}, dimensions={0} | all-to-all | bytes 3211264 | tf_op jit(solution)/shard_map/all_to_all | solution.py:92
  140.7 0.2 convert_reduce_fusion
  141.0 0.8 multiply_convert_fusion.1
  (46 shorter events, 3.3 us)
Async XLA Ops:
  0.0 72.7 %copy-start = (bf16[256,512]{1,0:T(8,128)(2,1)S(1)}, bf16[256,512]{1,0:T(8,128)(2,1)}, u32[]{:S(2)}) copy-start(bf16[256,512]{1,0:T(8,128)(2,1)} %param.7) | copy-start | bytes 786436
  0.0 2.5 %copy-start.2 = (bf16[256,512]{1,0:T(8,128)(2,1)S(1)}, bf16[256,512]{1,0:T(8,128)(2,1)}, u32[]{:S(2)}) copy-start(bf16[256,512]{1,0:T(8,128)(2,1)} %param.9) | copy-start | bytes 786436
  3.0 35.2 %copy-start.3 = (bf16[256,512]{1,0:T(8,128)(2,1)S(1)}, bf16[256,512]{1,0:T(8,128)(2,1)}, u32[]{:S(2)}) copy-start(bf16[256,512]{1,0:T(8,128)(2,1)} %param.10) | copy-start | bytes 786436
  3.0 6.1 %collective-permute-start = (bf16[4,128,128]{2,1,0:T(8,128)(2,1)S(1)}, bf16[4,128,128]{2,1,0:T(8,128)(2,1)S(1)}, u32[]{:S(2)}, u32[]{:S(2)}) collective-permute-start(bf16[4,128,128]{2,1,0:T(8,128)(2,1)S(1)} %fusion.35), channel_id=1, source_target_pairs={{0,16},{16,32},{32,48},{48,64},{64,80},{80,96},{96,112},{112,128},... | collective-permute-start | bytes 393224 | tf_op jit(solution)/shard_map/ppermute | solution.py:51
  9.3 7.4 %collective-permute-start.1 = (bf16[4,128,128]{2,1,0:T(8,128)(2,1)S(1)}, bf16[4,128,128]{2,1,0:T(8,128)(2,1)S(1)}, u32[]{:S(2)}, u32[]{:S(2)}) collective-permute-start(bf16[4,128,128]{2,1,0:T(8,128)(2,1)S(1)} %fusion.31), channel_id=1, source_target_pairs={{0,32},{16,48},{32,64},{48,80},{64,96},{80,112},{96,128},{112,144}... | collective-permute-start | bytes 393224 | tf_op jit(solution)/shard_map/ppermute | solution.py:51
  16.8 12.4 %collective-permute-start.2 = (bf16[4,128,128]{2,1,0:T(8,128)(2,1)S(1)}, bf16[4,128,128]{2,1,0:T(8,128)(2,1)S(1)}, u32[]{:S(2)}, u32[]{:S(2)}) collective-permute-start(bf16[4,128,128]{2,1,0:T(8,128)(2,1)S(1)} %get-tuple-element.9), channel_id=1, source_target_pairs={{0,64},{16,80},{32,96},{48,112},{64,128},{80,144},{96,160},{112,17... | collective-permute-start | bytes 393224 | tf_op jit(solution)/shard_map/ppermute | solution.py:51
  29.3 10.8 %collective-permute-start.3 = (bf16[4,128,128]{2,1,0:T(8,128)(2,1)S(1)}, bf16[4,128,128]{2,1,0:T(8,128)(2,1)S(1)}, u32[]{:S(2)}, u32[]{:S(2)}) collective-permute-start(bf16[4,128,128]{2,1,0:T(8,128)(2,1)S(1)} %fusion.32), channel_id=1, source_target_pairs={{0,128},{16,144},{32,160},{48,176},{64,192},{80,208},{96,224},{112... | collective-permute-start | bytes 393224 | tf_op jit(solution)/shard_map/ppermute | solution.py:51
  40.2 12.0 %collective-permute-start.4 = (bf16[4,128,128]{2,1,0:T(8,128)(2,1)S(1)}, bf16[4,128,128]{2,1,0:T(8,128)(2,1)S(1)}, u32[]{:S(2)}, u32[]{:S(2)}) collective-permute-start(bf16[4,128,128]{2,1,0:T(8,128)(2,1)S(1)} %fusion.40), channel_id=1, source_target_pairs={{0,256},{16,272},{32,288},{48,304},{64,320},{80,336},{96,352},{112... | collective-permute-start | bytes 393224 | tf_op jit(solution)/shard_map/ppermute | solution.py:51
  52.4 20.1 %collective-permute-start.5 = (bf16[4,128,128]{2,1,0:T(8,128)(2,1)S(1)}, bf16[4,128,128]{2,1,0:T(8,128)(2,1)S(1)}, u32[]{:S(2)}, u32[]{:S(2)}) collective-permute-start(bf16[4,128,128]{2,1,0:T(8,128)(2,1)S(1)} %add_convert_fusion), channel_id=1, source_target_pairs={{0,512},{16,528},{32,544},{48,560},{64,576},{80,592},{96,608},{112... | collective-permute-start | bytes 393224 | tf_op jit(solution)/shard_map/ppermute | solution.py:51
  72.4 0.9 copy-start.4
  72.5 1.0 copy-start.5
  79.6 8.9 %collective-permute-start.6 = (bf16[8,16,6272]{2,1,0:T(8,128)(2,1)S(1)}, bf16[8,16,6272]{2,1,0:T(8,128)(2,1)S(1)}, u32[]{:S(2)}, u32[]{:S(2)}) collective-permute-start(bf16[8,16,6272]{2,1,0:T(8,128)(2,1)S(1)} %concatenate.6), channel_id=1, source_target_pairs={{0,1},{1,0},{2,3},{3,2},{4,5},{5,4},{6,7},{7,6},{8,9},{9,8},{10,11... | collective-permute-start | bytes 4816904 | tf_op jit(solution)/shard_map/ppermute | solution.py:86
  88.5 1.2 copy-start.1
